TPU v7x, 128 devices: a whole 4x4x4 slice. The times are simulated.
128 devices in a mesh: dp: 8 (over x_lo, y), seq: 16 (over x_hi, z, core).
Axes of the slice: x: 4 (x_hi: 2, x_lo: 2; x = x_hi * 2 + x_lo), y: 4, z: 4, core: 2. Of those that a mesh axis runs over, the one named last changes fastest.
Arguments:
- query_tok: bfloat16 [8, 2048, 2560], P('dp', 'seq'), may hold values from -6 to 6
- key_tok: bfloat16 [8, 2048, 2560], P('dp', 'seq'), may hold values from -6 to 6
- value_tok: bfloat16 [8, 2048, 2560], P('dp', 'seq'), may hold values from -6 to 6
- grad_out: bfloat16 [8, 2048, 5120], P('dp', 'seq'), may hold values from -6 to 6
- out_weight: bfloat16 [32, 128, 5120], P('seq', None, 'dp'), may hold values from -0.125 to 0.125
- block_mask: int32 [20, 16, 16], replicated, may hold values from 0 to 1, as said below
- head_owner: int32 [20], replicated, may hold values from 0 to 15, as said below
Outputs:
- attn_out: bfloat16 [8, 2048, 2560], P('dp', 'seq')
- query_grad: bfloat16 [8, 2048, 2560], P('dp', 'seq')
- key_grad: bfloat16 [8, 2048, 2560], P('dp', 'seq')
- value_grad: bfloat16 [8, 2048, 2560], P('dp', 'seq')
- weight_grad: float32 [32, 128, 5120], P('seq', None, 'dp')
Inputs may be any that keep to these rules, and one draw needn't show every extreme that they name: `block_mask`: every diagonal tile is 1; each head has its own share of other tiles. `head_owner`: each value is an index of seq; no index holds more than 2 heads, and some index holds exactly 2.
All inputs are finite; a program needn't handle non-finite values.
Results may differ from a plain program's by a relative error of at most 0.017.
Values may be sent and summed in bfloat16 or wider, within the bound.
No kernel may reach another device: no remote copies, remote signals or barrier semaphores. Data moves between devices by JAX's collectives and lax.ppermute only.
A program may use at most 128 MiB of HBM per device.

v0:
```python
import jax
import jax.numpy as jnp
from jax import lax
from jax.sharding import PartitionSpec as P


def slot_table(head_owner, most_slots, seq_count):
    head_count = head_owner.shape[0]
    same_owner = head_owner[:, None] == head_owner[None, :]
    earlier = jnp.arange(head_count)[None, :] < jnp.arange(head_count)[:, None]
    owner_rank = jnp.sum(jnp.logical_and(same_owner, earlier), axis=1)
    slot_index = head_owner * most_slots + owner_rank
    return slot_index[:, None] == jnp.arange(seq_count * most_slots, dtype=jnp.int32)[None, :]


def allowed_rows(blocks, row_first, rows_count, block_len):
    band = lax.dynamic_slice_in_dim(blocks, row_first // block_len, rows_count // block_len, 0)
    spread = jnp.repeat(jnp.repeat(band, block_len, axis=0), block_len, axis=1)
    return spread > 0.5


def block_probs(q_rows, keys_all, allowed, score_scale):
    scores = jnp.dot(q_rows, keys_all.T, preferred_element_type=jnp.float32) * score_scale
    scores = jnp.where(allowed, scores, -jnp.inf)
    row_max = jnp.max(scores, axis=1, keepdims=True)
    expd = jnp.exp(scores - row_max)
    return expd / jnp.sum(expd, axis=1, keepdims=True)


def forward_slot(queries, keys_all, values_all, blocks, rows_count, block_len, score_scale):

    def forward_one_block(number):
        row_first = number * rows_count
        q_rows = lax.dynamic_slice_in_dim(queries, row_first, rows_count, 0)
        attn_prob = block_probs(
            q_rows, keys_all, allowed_rows(blocks, row_first, rows_count, block_len), score_scale
        )
        return jnp.dot(
            attn_prob.astype(jnp.bfloat16), values_all, preferred_element_type=jnp.float32
        ).astype(jnp.bfloat16)

    numbers = jnp.arange(queries.shape[0] // rows_count, dtype=jnp.int32)
    return lax.map(forward_one_block, numbers).reshape(queries.shape)


def backward_slot(
    queries, keys_all, values_all, outputs, grad_attn, blocks, rows_count, block_len, score_scale
):

    def backward_one_block(totals, number):
        key_total, value_total = totals
        row_first = number * rows_count
        q_rows = lax.dynamic_slice_in_dim(queries, row_first, rows_count, 0)
        attn_prob = block_probs(
            q_rows, keys_all, allowed_rows(blocks, row_first, rows_count, block_len), score_scale
        )
        prob_low = attn_prob.astype(jnp.bfloat16)
        grad_rows = lax.dynamic_slice_in_dim(grad_attn, row_first, rows_count, 0)
        out_rows = lax.dynamic_slice_in_dim(outputs, row_first, rows_count, 0)
        value_total = value_total + jnp.dot(
            prob_low.T, grad_rows, preferred_element_type=jnp.float32
        )
        prob_grad = jnp.dot(grad_rows, values_all.T, preferred_element_type=jnp.float32)
        row_delta = jnp.sum(
            grad_rows.astype(jnp.float32) * out_rows.astype(jnp.float32), axis=1, keepdims=True
        )
        score_grad = (attn_prob * (prob_grad - row_delta) * score_scale).astype(jnp.bfloat16)
        query_rows = jnp.dot(score_grad, keys_all, preferred_element_type=jnp.float32).astype(
            jnp.bfloat16
        )
        key_total = key_total + jnp.dot(score_grad.T, q_rows, preferred_element_type=jnp.float32)
        return ((key_total, value_total), query_rows)

    empty = jnp.zeros(queries.shape, jnp.float32)
    numbers = jnp.arange(queries.shape[0] // rows_count, dtype=jnp.int32)
    totals, query_parts = lax.scan(backward_one_block, (empty, empty), numbers)
    query_grad = query_parts.reshape(queries.shape)
    return (query_grad, totals[0].astype(jnp.bfloat16), totals[1].astype(jnp.bfloat16))


def heads_to_tokens(received, select, token_count, head_count, head_dim):
    merged = jnp.einsum("jtd,hj->thd", received[:, 0], select, preferred_element_type=jnp.float32)
    return merged.astype(jnp.bfloat16).reshape(1, token_count, head_count * head_dim)


def on_device(query_tok, key_tok, value_tok, grad_out, out_weight, block_mask, head_owner):
    seq_count = lax.axis_size("seq")
    most_slots = out_weight.shape[0]
    head_dim = out_weight.shape[1]
    token_count = query_tok.shape[1]
    head_count = block_mask.shape[0]
    length = seq_count * token_count
    block_len = length // block_mask.shape[1]
    rows_count = min(512, length)
    score_scale = head_dim ** (-0.5)
    grad_scale = (lax.axis_size("dp") * length) ** (-0.5)
    table = slot_table(head_owner, most_slots, seq_count)
    select = table.astype(jnp.bfloat16)
    my_first = lax.axis_index("seq") * most_slots
    local_select = lax.dynamic_slice_in_dim(table.astype(jnp.float32), my_first, most_slots, 1)
    slot_blocks = jnp.einsum("hs,hab->sab", local_select, block_mask.astype(jnp.float32))
    slot_used = jnp.sum(local_select, axis=0)
    slot_blocks = slot_blocks + (1.0 - slot_used)[:, None, None]

    def to_slots(tensor):
        split_heads = tensor[0].reshape(token_count, head_count, head_dim)
        spread = jnp.einsum("thd,hj->jtd", split_heads, select, preferred_element_type=jnp.float32)
        return spread.astype(jnp.bfloat16).reshape(seq_count, most_slots, token_count, head_dim)

    arrived = (
        lax.all_to_all(to_slots(query_tok), "seq", split_axis=0, concat_axis=2, tiled=True),
        lax.all_to_all(to_slots(key_tok), "seq", split_axis=0, concat_axis=2, tiled=True),
        lax.all_to_all(to_slots(value_tok), "seq", split_axis=0, concat_axis=2, tiled=True),
    )
    slot_query = arrived[0][0]
    slot_key = arrived[1][0]
    slot_value = arrived[2][0]
    weight_full = lax.all_gather(out_weight, "dp", axis=2, tiled=True)
    forward_list = []
    for slot_number in range(most_slots):
        forward_list.append(
            forward_slot(
                slot_query[slot_number],
                slot_key[slot_number],
                slot_value[slot_number],
                slot_blocks[slot_number],
                rows_count,
                block_len,
                score_scale,
            )
        )
    slot_out = jnp.stack(forward_list)

    def back_layout(stacked):
        return stacked.reshape(most_slots, seq_count, token_count, head_dim)

    dy_rows = lax.all_gather(grad_out, "seq", axis=1, tiled=True)[0]
    part = jnp.einsum(
        "td,shd->sth", dy_rows, weight_full, preferred_element_type=jnp.float32
    ).astype(jnp.bfloat16)
    grad_attn = part
    weight_total = jnp.einsum("sth,td->shd", slot_out, dy_rows, preferred_element_type=jnp.float32)
    grad_attn, weight_total = (grad_attn, weight_total)
    weight_grad = lax.psum_scatter(
        (weight_total * grad_scale).astype(jnp.bfloat16), "dp", scatter_dimension=2, tiled=True
    ).astype(jnp.float32)
    query_list = []
    key_list = []
    value_list = []
    for slot_number in range(most_slots):
        grads = backward_slot(
            slot_query[slot_number],
            slot_key[slot_number],
            slot_value[slot_number],
            slot_out[slot_number],
            grad_attn[slot_number],
            slot_blocks[slot_number],
            rows_count,
            block_len,
            score_scale,
        )
        query_list.append(grads[0])
        key_list.append(grads[1])
        value_list.append(grads[2])
    slot_qgrad = jnp.stack(query_list)
    slot_kgrad = jnp.stack(key_list)
    slot_vgrad = jnp.stack(value_list)
    all_back = (
        lax.all_to_all(back_layout(slot_out), "seq", split_axis=1, concat_axis=0, tiled=True),
        lax.all_to_all(back_layout(slot_qgrad), "seq", split_axis=1, concat_axis=0, tiled=True),
        lax.all_to_all(back_layout(slot_kgrad), "seq", split_axis=1, concat_axis=0, tiled=True),
        lax.all_to_all(back_layout(slot_vgrad), "seq", split_axis=1, concat_axis=0, tiled=True),
    )
    attn_out = heads_to_tokens(all_back[0], select, token_count, head_count, head_dim)
    query_grad = heads_to_tokens(all_back[1], select, token_count, head_count, head_dim)
    key_grad = heads_to_tokens(all_back[2], select, token_count, head_count, head_dim)
    value_grad = heads_to_tokens(all_back[3], select, token_count, head_count, head_dim)
    return (attn_out, query_grad, key_grad, value_grad, weight_grad)


def solution(mesh):
    placed = (
        P("dp", "seq", None),
        P("dp", "seq", None),
        P("dp", "seq", None),
        P("dp", "seq", None),
        P("seq", None, "dp"),
        P(),
        P(),
    )
    return jax.shard_map(
        on_device,
        mesh=mesh,
        in_specs=placed,
        out_specs=(
            P("dp", "seq", None),
            P("dp", "seq", None),
            P("dp", "seq", None),
            P("dp", "seq", None),
            P("seq", None, "dp"),
        ),
        check_vma=False,
    )
```

profile of v0, /device:TPU:1, one launch (start us, length us, event | category | flops | bytes accessed | tf_op | source)
XLA Modules:
  0.0 463.8 jit_solution(18401418277999480480)
XLA Ops:
  13.4 9.3 %all-to-all-start = ((bf16[16,2,128,128]{3,1,2,0:T(2,128)(2,1)}), bf16[16,2,128,128]{3,1,2,0:T(2,128)(2,1)S(1)}, u32[]{:S(2)}, u32[]{:S(2)}) async-start(bf16[16,2,128,128]{3,1,2,0:T(2,128)(2,1)} %copy.189), calls=%async_computation | async-start | bytes 2097152 | tf_op jit(solution)/shard_map/all_to_all | solution.py:111
  26.0 24.8 %all-to-all-done = bf16[16,2,128,128]{3,1,2,0:T(2,128)(2,1)S(1)} async-done(((bf16[16,2,128,128]{3,1,2,0:T(2,128)(2,1)}), bf16[16,2,128,128]{3,1,2,0:T(2,128)(2,1)S(1)}, u32[]{:S(2)}, u32[]{:S(2)}) %all-to-all-start) | async-done | bytes 1048608 | tf_op jit(solution)/shard_map/all_to_all | solution.py:111
  50.8 4.4 all-to-all-start.1
  61.7 15.1 %all-to-all-done.1 = bf16[16,2,128,128]{3,1,2,0:T(2,128)(2,1)S(1)} async-done(((bf16[16,2,128,128]{3,1,2,0:T(2,128)(2,1)}), bf16[16,2,128,128]{3,1,2,0:T(2,128)(2,1)S(1)}, u32[]{:S(2)}, u32[]{:S(2)}) %all-to-all-start.1) | async-done | bytes 1048608 | tf_op jit(solution)/shard_map/all_to_all | solution.py:112
  76.8 5.3 %all-to-all-start.2 = ((bf16[16,2,128,128]{3,1,2,0:T(2,128)(2,1)}), bf16[16,2,128,128]{3,1,2,0:T(2,128)(2,1)}, u32[]{:S(2)}, u32[]{:S(2)}) async-start(bf16[16,2,128,128]{3,1,2,0:T(2,128)(2,1)} %copy.197), calls=%async_computation.2 | async-start | bytes 2097152 | tf_op jit(solution)/shard_map/all_to_all | solution.py:113
  84.2 26.7 %all-to-all-done.2 = bf16[16,2,128,128]{3,1,2,0:T(2,128)(2,1)} async-done(((bf16[16,2,128,128]{3,1,2,0:T(2,128)(2,1)}), bf16[16,2,128,128]{3,1,2,0:T(2,128)(2,1)}, u32[]{:S(2)}, u32[]{:S(2)}) %all-to-all-start.2) | async-done | bytes 1048608 | tf_op jit(solution)/shard_map/all_to_all | solution.py:113
  116.5 34.0 %while.58 = (s32[]{:T(128)}, bf16[4,512,128]{2,1,0:T(8,128)(2,1)S(1)}, s32[4]{0:T(128)S(1)}, f32[16,16]{1,0:T(8,128)S(1)}, bf16[2048,128]{1,0:T(8,128)(2,1)S(1)}...) while((s32[]{:T(128)}, ...), condition=%wide.region_5.6_spmd, body=%wide.region_2.5_spmd.sunk | while | flops 545324160 | bytes 16018186 | solution.py:43
  117.8 3.5 broadcast_in_dim.136
  134.8 3.5 broadcast_in_dim.136
  143.3 3.5 broadcast_in_dim.136
  151.7 33.7 %while.59 = (s32[]{:T(128)}, bf16[4,512,128]{2,1,0:T(8,128)(2,1)S(1)}, s32[4]{0:T(128)S(1)}, f32[16,16]{1,0:T(8,128)S(1)}, bf16[2048,128]{1,0:T(8,128)(2,1)}, /*...) while((s32[]{:T(128)}, ...), condition=%wide.region_9.10_spmd, body=%wide.region_6.9_spmd.sunk | while | flops 545324160 | bytes 18115364 | solution.py:43
  152.9 3.5 broadcast_in_dim.138
  169.8 3.5 broadcast_in_dim.138
  187.8 4.8 %all-to-all-start.3 = ((bf16[2,16,128,128]{3,0,2,1:T(2,128)(2,1)}), bf16[2,16,128,128]{3,0,2,1:T(2,128)(2,1)}, u32[]{:S(2)}, u32[]{:S(2)}) async-start(bf16[2,16,128,128]{3,0,2,1:T(2,128)(2,1)} %copy.199), calls=%async_computation.3 | async-start | bytes 2097152 | tf_op jit(solution)/shard_map/all_to_all | solution.py:169
  192.9 26.6 %all-gather.5.cloned.1.call-done = bf16[1,2048,5120]{2,1,0:T(8,128)(2,1)} async-done(((bf16[1,128,5120]{2,1,0:T(8,128)(2,1)}), bf16[1,2048,5120]{2,1,0:T(8,128)(2,1)}) %all-gather.5.cloned.1.call-update) | async-done | bytes 20971536 | tf_op jit(solution)/shard_map/all_gather | solution.py:137
  219.5 10.6 %fusion.47 = bf16[2,2048,128]{1,2,0:T(8,128)(2,1)S(1)} fusion(bf16[2,128,5120]{2,1,0:T(8,128)(2,1)} %all-gather.3.cloned.1.call-done, bf16[1,2048,5120]{2,1,0:T(8,128)(2,1)} %all-gather.5.cloned.1.call-done), kind=kOutput, calls=%fused_computation.66 | convolution fusion | flops 5369233408 | bytes 24641536 | tf_op jit(solution)/shard_map/td,shd->sth/dot_general | solution.py:138
  231.2 13.9 %fusion.41 = bf16[2,128,5120]{2,1,0:T(8,128)(2,1)} fusion(bf16[1,2048,5120]{2,1,0:T(8,128)(2,1)} %all-gather.5.cloned.1.call-done, bf16[1,2048,128]{1,2,0:T(8,128)(2,1)S(1)} %copy.222, bf16[1,2048,128]{1,2,0:T(8,128)(2,1)S(1)} %copy.221), kind=kOutput, calls=%fused_computation.63 | convolution fusion | flops 5371854848 | bytes 24641536 | tf_op jit(solution)/shard_map/sth,td->shd/dot_general | solution.py:142
  245.0 7.4 %copy.223 = bf16[2,128,5120]{1,0,2:T(2,128)(2,1)} copy(bf16[2,128,5120]{2,1,0:T(8,128)(2,1)} %fusion.41) | data formatting | bytes 5242880
  252.5 3.6 copy.240
  257.0 63.1 %while.61 = (s32[]{:T(128)}, f32[2048,128]{1,0:T(8,128)S(1)}, f32[2048,128]{1,0:T(8,128)}, bf16[4,512,128]{2,1,0:T(8,128)(2,1)}, s32[4]{0:T(128)S(1)}, /*index=5...) while((s32[]{:T(128)}, f32[2048,128]{1,0:T(8,128)S(1)}, ...), condition=%wide.region_19.20_spmd.clone, body=%wide.region_15.19_spmd.clone.sunk | while | flops 1358232192 | bytes 44993452 | solution.py:76
  306.9 3.5 broadcast_in_dim.142
  320.2 63.5 %while.60 = (s32[]{:T(128)}, f32[2048,128]{1,0:T(8,128)S(1)}, f32[2048,128]{1,0:T(8,128)}, bf16[4,512,128]{2,1,0:T(8,128)(2,1)S(1)}, s32[4]{0:T(128)S(1)}, /*ind...) while((s32[]{:T(128)}, f32[2048,128]{1,0:T(8,128)S(1)}, ...), condition=%wide.region_14.15_spmd.clone, body=%wide.region_10.14_spmd.clone.sunk | while | flops 1358232192 | bytes 44993452 | solution.py:76
  323.6 3.5 broadcast_in_dim.140
  339.4 3.5 broadcast_in_dim.140
  355.2 3.5 broadcast_in_dim.140
  371.1 3.5 broadcast_in_dim.140
  386.9 3.7 all-to-all-start.4
  392.9 14.9 %all-to-all-done.4 = bf16[2,16,128,128]{3,0,2,1:T(2,128)(2,1)S(1)} async-done(((bf16[2,16,128,128]{3,0,2,1:T(2,128)(2,1)}), bf16[2,16,128,128]{3,0,2,1:T(2,128)(2,1)S(1)}, u32[]{:S(2)}, u32[]{:S(2)}) %all-to-all-start.4) | async-done | bytes 1048608 | tf_op jit(solution)/shard_map/all_to_all | solution.py:170
  407.7 4.4 all-to-all-start.5
  415.7 13.7 %all-to-all-done.5 = bf16[2,16,128,128]{3,0,2,1:T(2,128)(2,1)S(1)} async-done(((bf16[2,16,128,128]{3,0,2,1:T(2,128)(2,1)}), bf16[2,16,128,128]{3,0,2,1:T(2,128)(2,1)S(1)}, u32[]{:S(2)}, u32[]{:S(2)}) %all-to-all-start.5) | async-done | bytes 1048608 | tf_op jit(solution)/shard_map/all_to_all | solution.py:171
  429.4 4.8 %all-to-all-start.6 = ((bf16[2,16,128,128]{3,0,2,1:T(2,128)(2,1)}), bf16[2,16,128,128]{3,0,2,1:T(2,128)(2,1)S(1)}, u32[]{:S(2)}, u32[]{:S(2)}) async-start(bf16[2,16,128,128]{3,0,2,1:T(2,128)(2,1)} %copy.210), calls=%async_computation.6 | async-start | bytes 2097152 | tf_op jit(solution)/shard_map/all_to_all | solution.py:172
  447.4 3.9 all-to-all-done.6
  (324 shorter events, 204.8 us)
Async XLA Ops:
  7.2 3.4 copy-start.19
  7.2 185.7 %all-gather.3.cloned.1.call-start = ((), (), s32[]{:S(2)}) async-start(), calls=%async_computation.8 | async-start | bytes 2949120 | tf_op jit(solution)/shard_map/all_gather | solution.py:118
  7.9 211.6 %all-gather.5.cloned.1.call-start = ((), (), s32[]{:S(2)}) async-start(), calls=%async_computation.9 | async-start | bytes 22282240 | tf_op jit(solution)/shard_map/all_gather | solution.py:137
  8.7 14.0 %copy-start.7 = (bf16[1,128,2560]{2,1,0:T(8,128)(2,1)S(1)}, bf16[1,128,2560]{2,1,0:T(8,128)(2,1)}, u32[]{:S(2)}) copy-start(bf16[1,128,2560]{2,1,0:T(8,128)(2,1)} %param.16) | copy-start | bytes 1966084
  10.8 71.4 %copy-start.17 = (s32[20]{0:T(128)}, s32[20]{0:T(128)S(1)}, u32[]{:S(2)}) copy-start(s32[20]{0:T(128)S(1)} %multiply_add_fusion) | copy-start | bytes 244
  13.4 37.4 %all-to-all-start = ((bf16[16,2,128,128]{3,1,2,0:T(2,128)(2,1)}), bf16[16,2,128,128]{3,1,2,0:T(2,128)(2,1)S(1)}, u32[]{:S(2)}, u32[]{:S(2)}) async-start(bf16[16,2,128,128]{3,1,2,0:T(2,128)(2,1)} %copy.189), calls=%async_computation | async-start | bytes 2097152 | tf_op jit(solution)/shard_map/all_to_all | solution.py:111
  50.8 26.0 %all-to-all-start.1 = ((bf16[16,2,128,128]{3,1,2,0:T(2,128)(2,1)}), bf16[16,2,128,128]{3,1,2,0:T(2,128)(2,1)S(1)}, u32[]{:S(2)}, u32[]{:S(2)}) async-start(bf16[16,2,128,128]{3,1,2,0:T(2,128)(2,1)} %copy.193), calls=%async_computation.1 | async-start | bytes 2097152 | tf_op jit(solution)/shard_map/all_to_all | solution.py:112
  55.2 27.1 %copy-start.15 = (s32[20,16,16]{0,2,1:T(8,128)S(1)}, s32[20,16,16]{0,2,1:T(8,128)}, u32[]{:S(2)}) copy-start(s32[20,16,16]{0,2,1:T(8,128)} %param.20) | copy-start | bytes 61444
  76.8 34.2 %all-to-all-start.2 = ((bf16[16,2,128,128]{3,1,2,0:T(2,128)(2,1)}), bf16[16,2,128,128]{3,1,2,0:T(2,128)(2,1)}, u32[]{:S(2)}, u32[]{:S(2)}) async-start(bf16[16,2,128,128]{3,1,2,0:T(2,128)(2,1)} %copy.197), calls=%async_computation.2 | async-start | bytes 2097152 | tf_op jit(solution)/shard_map/all_to_all | solution.py:113
  116.5 35.2 %copy-start.11 = (bf16[1,1,16,128,128]{4,3,2,1,0:T(8,128)(2,1)S(1)}, bf16[1,1,16,128,128]{4,3,2,1,0:T(8,128)(2,1)}, u32[]{:S(2)}) copy-start(bf16[1,1,16,128,128]{4,3,2,1,0:T(8,128)(2,1)} %get-tuple-element.787) | copy-start | bytes 1572868
  156.4 2.8 copy-start.13
  164.8 2.8 copy-start.13
  173.2 2.8 copy-start.13
  181.7 2.8 copy-start.13
  187.8 199.1 %all-to-all-start.3 = ((bf16[2,16,128,128]{3,0,2,1:T(2,128)(2,1)}), bf16[2,16,128,128]{3,0,2,1:T(2,128)(2,1)}, u32[]{:S(2)}, u32[]{:S(2)}) async-start(bf16[2,16,128,128]{3,0,2,1:T(2,128)(2,1)} %copy.199), calls=%async_computation.3 | async-start | bytes 2097152 | tf_op jit(solution)/shard_map/all_to_all | solution.py:169
  192.6 261.3 %reduce-scatter.4.cloned.1.call-start = ((), (), s32[]{:S(2)}) async-start(), calls=%async_computation.10 | async-start | bytes 2949120
  257.0 63.2 %copy-start = (f32[2048,128]{1,0:T(8,128)S(1)}, f32[2048,128]{1,0:T(8,128)}, u32[]{:S(2)}) copy-start(f32[2048,128]{1,0:T(8,128)} %custom-call) | copy-start | bytes 3145732
  263.0 3.0 copy-start.5
  278.8 3.0 copy-start.5
  294.6 3.0 copy-start.5
  310.3 3.0 copy-start.5
  314.9 1.8 copy-start.6
  314.9 1.8 copy-start.12
  327.1 3.0 copy-start.2
  342.9 3.0 copy-start.2
  358.7 3.0 copy-start.2
  374.5 3.0 copy-start.2
  386.9 20.9 %all-to-all-start.4 = ((bf16[2,16,128,128]{3,0,2,1:T(2,128)(2,1)}), bf16[2,16,128,128]{3,0,2,1:T(2,128)(2,1)S(1)}, u32[]{:S(2)}, u32[]{:S(2)}) async-start(bf16[2,16,128,128]{3,0,2,1:T(2,128)(2,1)} %copy.204), calls=%async_computation.4 | async-start | bytes 2097152 | tf_op jit(solution)/shard_map/all_to_all | solution.py:170
  390.7 22.8 %copy-start.4 = (f32[2048,128]{1,0:T(8,128)S(1)}, f32[2048,128]{1,0:T(8,128)}, u32[]{:S(2)}) copy-start(f32[2048,128]{1,0:T(8,128)} %get-tuple-element.471) | copy-start | bytes 3145732
  407.7 21.6 %all-to-all-start.5 = ((bf16[2,16,128,128]{3,0,2,1:T(2,128)(2,1)}), bf16[2,16,128,128]{3,0,2,1:T(2,128)(2,1)S(1)}, u32[]{:S(2)}, u32[]{:S(2)}) async-start(bf16[2,16,128,128]{3,0,2,1:T(2,128)(2,1)} %copy.207), calls=%async_computation.5 | async-start | bytes 2097152 | tf_op jit(solution)/shard_map/all_to_all | solution.py:171
  413.5 22.6 %copy-start.18 = (s32[20]{0:T(128)S(1)}, s32[20]{0:T(128)}, u32[]{:S(2)}) copy-start(s32[20]{0:T(128)} %copy-done.17) | copy-start | bytes 244
  429.4 21.9 %all-to-all-start.6 = ((bf16[2,16,128,128]{3,0,2,1:T(2,128)(2,1)}), bf16[2,16,128,128]{3,0,2,1:T(2,128)(2,1)S(1)}, u32[]{:S(2)}, u32[]{:S(2)}) async-start(bf16[2,16,128,128]{3,0,2,1:T(2,128)(2,1)} %copy.210), calls=%async_computation.6 | async-start | bytes 2097152 | tf_op jit(solution)/shard_map/all_to_all | solution.py:172
  (25 other events, 40.8 us)
Sparse Core Ops, SparseCore 0:
  9.6 53.9 all-gather.2
  66.1 153.2 all-gather.4
  256.2 37.0 reduce-scatter.3
where the time goes:
time: 471 us; the launch traced here: 464 us
  local copies, waits for them, and re-layouts  130 us (28%)
  waiting for transfers between devices  127 us (27%)
  matrix products  123 us (26%)
  starting transfers between devices  37 us (8%)
  other arithmetic  19.7 us (4%)
  between operations  14.7 us (3%)
  loops' own time  11.7 us (2%)
    broadcast_in_dim x32, local copies, waits for them, and re-layouts, allowed_rows(): spread = jnp.repeat(jnp.repeat(band, block_len, axis=0), block_len, axis=1)  55.8 us
    dot_general x16, matrix products, block_probs(): jnp.dot(q_rows, keys_all.T, preferred_element_type=jnp.float32)  35 us
    all_to_all x1, waiting for transfers between devices, on_device(): lax.all_to_all(to_slots(value_tok), 'seq', split_axis=0, concat_axis=2, t...  26.7 us
    all_gather x1, waiting for transfers between devices, on_device(): dy_rows = lax.all_gather(grad_out, 'seq', axis=1, tiled=True)[0]  26.6 us
    all_to_all x1, waiting for transfers between devices, on_device(): lax.all_to_all(to_slots(query_tok), 'seq', split_axis=0, concat_axis=2, t...  24.8 us
    unnamed x33, local copies, waits for them, and re-layouts  22.5 us
    dot_general x8, matrix products, backward_one_block(): jnp.dot(score_grad.T, q_rows, preferred_element_type=jnp.float32)  15.6 us
    all_to_all x1, waiting for transfers between devices, on_device(): lax.all_to_all(to_slots(key_tok), 'seq', split_axis=0, concat_axis=2, til...  15.1 us
  transfers between devices with their start and end apart: 10, of which 7 were waited for; matrix products, arithmetic and copies ran while one was open for 58% of the time, Pallas kernels for 0%

commit v1 on v0

--- a/solution.py
+++ b/solution.py
@@ -83,8 +83,11 @@
     return merged.astype(jnp.bfloat16).reshape(1, token_count, head_count * head_dim)
 
 
+SEQ = ("chip", "core")
+
+
 def on_device(query_tok, key_tok, value_tok, grad_out, out_weight, block_mask, head_owner):
-    seq_count = lax.axis_size("seq")
+    seq_count = lax.axis_size(SEQ)
     most_slots = out_weight.shape[0]
     head_dim = out_weight.shape[1]
     token_count = query_tok.shape[1]
@@ -96,7 +99,7 @@
     grad_scale = (lax.axis_size("dp") * length) ** (-0.5)
     table = slot_table(head_owner, most_slots, seq_count)
     select = table.astype(jnp.bfloat16)
-    my_first = lax.axis_index("seq") * most_slots
+    my_first = lax.axis_index(SEQ) * most_slots
     local_select = lax.dynamic_slice_in_dim(table.astype(jnp.float32), my_first, most_slots, 1)
     slot_blocks = jnp.einsum("hs,hab->sab", local_select, block_mask.astype(jnp.float32))
     slot_used = jnp.sum(local_select, axis=0)
@@ -107,14 +110,11 @@
         spread = jnp.einsum("thd,hj->jtd", split_heads, select, preferred_element_type=jnp.float32)
         return spread.astype(jnp.bfloat16).reshape(seq_count, most_slots, token_count, head_dim)
 
-    arrived = (
-        lax.all_to_all(to_slots(query_tok), "seq", split_axis=0, concat_axis=2, tiled=True),
-        lax.all_to_all(to_slots(key_tok), "seq", split_axis=0, concat_axis=2, tiled=True),
-        lax.all_to_all(to_slots(value_tok), "seq", split_axis=0, concat_axis=2, tiled=True),
-    )
-    slot_query = arrived[0][0]
-    slot_key = arrived[1][0]
-    slot_value = arrived[2][0]
+    stacked = jnp.stack([to_slots(query_tok), to_slots(key_tok), to_slots(value_tok)], axis=1)
+    arrived = lax.all_to_all(stacked, SEQ, split_axis=0, concat_axis=3, tiled=True)[0]
+    slot_query = arrived[0]
+    slot_key = arrived[1]
+    slot_value = arrived[2]
     weight_full = lax.all_gather(out_weight, "dp", axis=2, tiled=True)
     forward_list = []
     for slot_number in range(most_slots):
@@ -134,7 +134,8 @@
     def back_layout(stacked):
         return stacked.reshape(most_slots, seq_count, token_count, head_dim)
 
-    dy_rows = lax.all_gather(grad_out, "seq", axis=1, tiled=True)[0]
+    by_chip = lax.all_gather(grad_out[0], "chip", axis=0, tiled=False)
+    dy_rows = lax.all_gather(by_chip, "core", axis=1, tiled=False).reshape(length, grad_out.shape[2])
     part = jnp.einsum(
         "td,shd->sth", dy_rows, weight_full, preferred_element_type=jnp.float32
     ).astype(jnp.bfloat16)
@@ -165,12 +166,10 @@
     slot_qgrad = jnp.stack(query_list)
     slot_kgrad = jnp.stack(key_list)
     slot_vgrad = jnp.stack(value_list)
-    all_back = (
-        lax.all_to_all(back_layout(slot_out), "seq", split_axis=1, concat_axis=0, tiled=True),
-        lax.all_to_all(back_layout(slot_qgrad), "seq", split_axis=1, concat_axis=0, tiled=True),
-        lax.all_to_all(back_layout(slot_kgrad), "seq", split_axis=1, concat_axis=0, tiled=True),
-        lax.all_to_all(back_layout(slot_vgrad), "seq", split_axis=1, concat_axis=0, tiled=True),
-    )
+    back_stack = jnp.stack(
+        [back_layout(slot_out), back_layout(slot_qgrad), back_layout(slot_kgrad), back_layout(slot_vgrad)]
+    )
+    all_back = lax.all_to_all(back_stack, SEQ, split_axis=2, concat_axis=1, tiled=True)
     attn_out = heads_to_tokens(all_back[0], select, token_count, head_count, head_dim)
     query_grad = heads_to_tokens(all_back[1], select, token_count, head_count, head_dim)
     key_grad = heads_to_tokens(all_back[2], select, token_count, head_count, head_dim)
@@ -179,12 +178,15 @@
 
 
 def solution(mesh):
+    mesh = jax.sharding.Mesh(
+        mesh.devices.reshape(mesh.devices.shape[0], -1, 2), ("dp", "chip", "core")
+    )
     placed = (
-        P("dp", "seq", None),
-        P("dp", "seq", None),
-        P("dp", "seq", None),
-        P("dp", "seq", None),
-        P("seq", None, "dp"),
+        P("dp", SEQ, None),
+        P("dp", SEQ, None),
+        P("dp", SEQ, None),
+        P("dp", SEQ, None),
+        P(SEQ, None, "dp"),
         P(),
         P(),
     )
@@ -193,11 +195,11 @@
         mesh=mesh,
         in_specs=placed,
         out_specs=(
-            P("dp", "seq", None),
-            P("dp", "seq", None),
-            P("dp", "seq", None),
-            P("dp", "seq", None),
-            P("seq", None, "dp"),
+            P("dp", SEQ, None),
+            P("dp", SEQ, None),
+            P("dp", SEQ, None),
+            P("dp", SEQ, None),
+            P(SEQ, None, "dp"),
         ),
         check_vma=False,
     )

time: 471 us -> 563 us (1.20)
  waiting for transfers between devices: 127 us -> 235 us
  starting transfers between devices: 37 us -> 16.5 us
  other arithmetic: 19.7 us -> 26.5 us
    all_gather x1 -> x2, waiting for transfers between devices: 26.6 us -> 130 us  [the longest x1 130 us: on_device(): by_chip = lax.all_gather(grad_out[0], 'chip', axis=0, tiled=False)]
    all_to_all x7 -> x2, starting transfers between devices: 36.8 us -> 16.4 us  [the longest x1 10.3 us: on_device(): lax.all_to_all(back_stack, SEQ, split_axis=2, concat_axis=1, tiled=True)]
    another operation x4 -> x2, other arithmetic: 1.44 us -> 8.04 us  [the longest x1 5.41 us: on_device(): jnp.stack([to_slots(query_tok), to_slots(key_tok), to_slots(value_tok)],...]
    reshape x3 -> x0, local copies, waits for them, and re-layouts: 6.08 us -> none  [to_slots(): spread.astype(jnp.bfloat16)]
    another operation x7 -> x6, local copies, waits for them, and re-layouts: 7.23 us -> 12.6 us  [the longest x1 6.33 us: on_device(): jnp.stack([back_layout(slot_out), back_layout(slot_qgrad), back_layout(sl...]
    all_to_all x7 -> x2, waiting for transfers between devices: 99 us -> 104 us  [the longest x1 52.6 us: on_device(): lax.all_to_all(back_stack, SEQ, split_axis=2, concat_axis=1, tiled=True)]
    unnamed x33 -> x37, local copies, waits for them, and re-layouts: 22.5 us -> 18.3 us
  transfers between devices with their start and end apart: 10 -> 6, of which waited for: 7 -> 3; matrix products, arithmetic and copies ran while one was open for 58% -> 23% of each run, Pallas kernels for 0% -> 0%
where the time goes in v1:
time: 563 us; the launch traced here: 554 us
  waiting for transfers between devices  235 us (42%)
  local copies, waits for them, and re-layouts  125 us (22%)
  matrix products  123 us (22%)
  other arithmetic  26.5 us (5%)
  starting transfers between devices  16.5 us (3%)
  between operations  14.4 us (3%)
  loops' own time  12.9 us (2%)
    all_gather x1, waiting for transfers between devices, on_device(): by_chip = lax.all_gather(grad_out[0], 'chip', axis=0, tiled=False)  130 us
    broadcast_in_dim x32, local copies, waits for them, and re-layouts, allowed_rows(): spread = jnp.repeat(jnp.repeat(band, block_len, axis=0), block_len, axis=1)  55.8 us
    all_to_all x1, waiting for transfers between devices, on_device(): lax.all_to_all(back_stack, SEQ, split_axis=2, concat_axis=1, tiled=True)  52.6 us
    all_to_all x1, waiting for transfers between devices, on_device(): lax.all_to_all(stacked, SEQ, split_axis=0, concat_axis=3, tiled=True)[0]  51.8 us
    dot_general x16, matrix products, block_probs(): jnp.dot(q_rows, keys_all.T, preferred_element_type=jnp.float32)  35.4 us
    unnamed x37, local copies, waits for them, and re-layouts  18.3 us
    dot_general x8, matrix products, backward_one_block(): jnp.dot(score_grad.T, q_rows, preferred_element_type=jnp.float32)  15.6 us
    dot_general x8, matrix products, backward_one_block(): jnp.dot(grad_rows, values_all.T, preferred_element_type=jnp.float32)  14.2 us
  transfers between devices with their start and end apart: 6, of which 3 were waited for; matrix products, arithmetic and copies ran while one was open for 23% of the time, Pallas kernels for 0%

profile of v1, /device:TPU:1, one launch (start us, length us, event | category | flops | bytes accessed | tf_op | source)
XLA Modules:
  0.0 553.8 jit_solution(7509974547992065933)
XLA Ops:
  8.7 129.7 %all-gather.7.cloned.1.call-done = bf16[8,128,5120]{2,1,0:T(8,128)(2,1)} async-done(((bf16[1,128,5120]{2,1,0:T(8,128)(2,1)}), bf16[8,128,5120]{2,1,0:T(8,128)(2,1)}) %all-gather.7.cloned.1.call-update) | async-done | bytes 10485776 | tf_op jit(solution)/shard_map/all_gather | solution.py:137
  144.7 5.4 pad_maximum_fusion
  150.2 5.2 copy.206
  155.3 6.1 %all-to-all-start = ((bf16[16,3,2,128,128]{4,2,3,1,0:T(2,128)(2,1)}), bf16[16,3,2,128,128]{4,2,3,1,0:T(2,128)(2,1)}, u32[]{:S(2)}, u32[]{:S(2)}) async-start(bf16[16,3,2,128,128]{4,2,3,1,0:T(2,128)(2,1)} %copy.206), calls=%async_computation | async-start | bytes 6291456 | tf_op jit(solution)/shard_map/all_to_all | solution.py:114
  162.1 51.8 %all-to-all-done = bf16[16,3,2,128,128]{4,2,3,1,0:T(2,128)(2,1)} async-done(((bf16[16,3,2,128,128]{4,2,3,1,0:T(2,128)(2,1)}), bf16[16,3,2,128,128]{4,2,3,1,0:T(2,128)(2,1)}, u32[]{:S(2)}, u32[]{:S(2)}) %all-to-all-start) | async-done | bytes 3145760 | tf_op jit(solution)/shard_map/all_to_all | solution.py:114
  218.5 34.8 %while.58 = (s32[]{:T(128)}, bf16[4,512,128]{2,1,0:T(8,128)(2,1)S(1)}, s32[4]{0:T(128)S(1)}, f32[16,16]{1,0:T(8,128)S(1)}, bf16[2048,128]{1,0:T(8,128)(2,1)S(1)}...) while((s32[]{:T(128)}, ...), condition=%wide.region_5.6_spmd, body=%wide.region_2.5_spmd.sunk | while | flops 545324160 | bytes 16018186 | solution.py:43
  219.9 3.5 broadcast_in_dim.136
  228.6 3.5 broadcast_in_dim.136
  237.3 3.5 broadcast_in_dim.136
  246.0 3.5 broadcast_in_dim.136
  254.5 34.6 %while.59 = (s32[]{:T(128)}, bf16[4,512,128]{2,1,0:T(8,128)(2,1)S(1)}, s32[4]{0:T(128)S(1)}, f32[16,16]{1,0:T(8,128)S(1)}, bf16[2048,128]{1,0:T(8,128)(2,1)S(1)}...) while((s32[]{:T(128)}, ...), condition=%wide.region_9.10_spmd, body=%wide.region_6.9_spmd.sunk | while | flops 545324160 | bytes 18115364 | solution.py:43
  255.9 3.5 broadcast_in_dim.138
  264.5 3.5 broadcast_in_dim.138
  273.1 3.5 broadcast_in_dim.138
  281.8 3.5 broadcast_in_dim.138
  290.1 10.6 %fusion.35 = bf16[2,2048,128]{1,2,0:T(8,128)(2,1)S(1)} fusion(bf16[2,128,5120]{2,1,0:T(8,128)(2,1)} %all-gather.5.cloned.1.call-done, bf16[2048,5120,1]{1,0,2:T(8,128)(2,1)} %bitcast.261), kind=kOutput, calls=%fused_computation.65 | convolution fusion | flops 5369233408 | bytes 24641536 | tf_op jit(solution)/shard_map/td,shd->sth/dot_general | solution.py:139
  302.7 62.9 %while.61 = (s32[]{:T(128)}, f32[2048,128]{1,0:T(8,128)S(1)}, f32[2048,128]{1,0:T(8,128)}, bf16[4,512,128]{2,1,0:T(8,128)(2,1)}, s32[4]{0:T(128)S(1)}, /*index=5...) while((s32[]{:T(128)}, f32[2048,128]{1,0:T(8,128)S(1)}, ...), condition=%wide.region_19.20_spmd.clone, body=%wide.region_15.19_spmd.clone.sunk | while | flops 1358232192 | bytes 44993452 | solution.py:76
  305.4 3.5 broadcast_in_dim.142
  321.1 3.5 broadcast_in_dim.142
  336.8 3.5 broadcast_in_dim.142
  352.4 3.5 broadcast_in_dim.142
  368.6 61.1 %while.60 = (s32[]{:T(128)}, f32[2048,128]{1,0:T(8,128)S(1)}, f32[2048,128]{1,0:T(8,128)}, bf16[4,512,128]{2,1,0:T(8,128)(2,1)S(1)}, s32[4]{0:T(128)S(1)}, /*ind...) while((s32[]{:T(128)}, f32[2048,128]{1,0:T(8,128)S(1)}, ...), condition=%wide.region_14.15_spmd.clone, body=%wide.region_10.14_spmd.clone.sunk | while | flops 1358232192 | bytes 44993452 | solution.py:76
  371.6 3.5 broadcast_in_dim.140
  386.8 3.5 broadcast_in_dim.140
  401.9 3.5 broadcast_in_dim.140
  417.1 3.5 broadcast_in_dim.140
  433.8 6.3 %copy.189 = bf16[4,2,16,128,128]{4,1,3,0,2:T(2,128)(2,1)} copy(bf16[4,2,16,128,128]{4,3,2,1,0:T(8,128)(2,1)S(1)} %maximum_maximum_fusion) | data formatting | bytes 8388608 | tf_op jit(solution)/shard_map/stack | solution.py:169
  440.2 10.3 %all-to-all-start.1 = ((bf16[4,2,16,128,128]{4,1,3,0,2:T(2,128)(2,1)}), bf16[4,2,16,128,128]{4,1,3,0,2:T(2,128)(2,1)}, u32[]{:S(2)}, u32[]{:S(2)}) async-start(bf16[4,2,16,128,128]{4,1,3,0,2:T(2,128)(2,1)} %copy.189), calls=%async_computation.1 | async-start | bytes 8388608 | tf_op jit(solution)/shard_map/all_to_all | solution.py:172
  450.5 14.0 %fusion.34 = bf16[2,128,5120]{2,1,0:T(8,128)(2,1)} fusion(bf16[2048,5120,1]{1,0,2:T(8,128)(2,1)} %bitcast.262, bf16[1,2048,128]{1,2,0:T(8,128)(2,1)S(1)} %copy-done.17, bf16[1,2048,128]{1,2,0:T(8,128)(2,1)S(1)} %copy-done.16), kind=kOutput, calls=%fused_computation.59 | convolution fusion | flops 5371854848 | bytes 24641536 | tf_op jit(solution)/shard_map/sth,td->shd/dot_general | solution.py:143
  464.5 5.9 %copy.209 = bf16[2,128,5120]{1,0,2:T(2,128)(2,1)S(1)} copy(bf16[2,128,5120]{2,1,0:T(8,128)(2,1)} %fusion.34) | data formatting | bytes 5242880
  472.3 52.6 %all-to-all-done.1 = bf16[4,2,16,128,128]{4,1,3,0,2:T(2,128)(2,1)} async-done(((bf16[4,2,16,128,128]{4,1,3,0,2:T(2,128)(2,1)}), bf16[4,2,16,128,128]{4,1,3,0,2:T(2,128)(2,1)}, u32[]{:S(2)}, u32[]{:S(2)}) %all-to-all-start.1) | async-done | bytes 4194336 | tf_op jit(solution)/shard_map/all_to_all | solution.py:172
  524.8 4.7 fusion.65
  (311 shorter events, 168.5 us)
Async XLA Ops:
  7.2 131.3 %all-gather.7.cloned.1.call-start = ((), (), s32[]{:S(2)}) async-start(), calls=%async_computation.4 | async-start | bytes 11796480 | tf_op jit(solution)/shard_map/all_gather | solution.py:137
  7.9 282.2 %all-gather.5.cloned.1.call-start = ((), (), s32[]{:S(2)}) async-start(), calls=%async_computation.3 | async-start | bytes 2949120 | tf_op jit(solution)/shard_map/all_gather | solution.py:118
  8.6 281.5 %all-gather.9.cloned.1.call-start = ((), (), s32[]{:S(2)}) async-start(), calls=%async_computation.5 | async-start | bytes 31457280 | tf_op jit(solution)/shard_map/all_gather | solution.py:138
  138.4 1.8 copy-start.9
  139.5 3.4 copy-start.21
  143.1 18.5 %copy-start.19 = (s32[20]{0:T(128)}, s32[20]{0:T(128)S(1)}, u32[]{:S(2)}) copy-start(s32[20]{0:T(128)S(1)} %multiply_add_fusion) | copy-start | bytes 244
  155.3 6.4 %copy-start.18 = (s32[20,16,16]{0,2,1:T(8,128)S(1)}, s32[20,16,16]{0,2,1:T(8,128)}, u32[]{:S(2)}) copy-start(s32[20,16,16]{0,2,1:T(8,128)} %param.20) | copy-start | bytes 61444
  155.3 58.5 %all-to-all-start = ((bf16[16,3,2,128,128]{4,2,3,1,0:T(2,128)(2,1)}), bf16[16,3,2,128,128]{4,2,3,1,0:T(2,128)(2,1)}, u32[]{:S(2)}, u32[]{:S(2)}) async-start(bf16[16,3,2,128,128]{4,2,3,1,0:T(2,128)(2,1)} %copy.206), calls=%async_computation | async-start | bytes 6291456 | tf_op jit(solution)/shard_map/all_to_all | solution.py:114
  259.3 2.9 copy-start.13
  268.0 2.9 copy-start.13
  276.6 2.9 copy-start.13
  285.3 2.9 copy-start.13
  289.1 11.7 %copy-start.2 = (bf16[2048,128]{1,0:T(8,128)(2,1)}, bf16[2048,128]{1,0:T(8,128)(2,1)S(1)}, u32[]{:S(2)}) copy-start(bf16[2048,128]{1,0:T(8,128)(2,1)S(1)} %get-tuple-element.1250) | copy-start | bytes 1572868
  302.7 65.9 %copy-start = (f32[2048,128]{1,0:T(8,128)S(1)}, f32[2048,128]{1,0:T(8,128)}, u32[]{:S(2)}) copy-start(f32[2048,128]{1,0:T(8,128)} %custom-call) | copy-start | bytes 3145732
  308.9 3.0 copy-start.6
  313.5 1.8 copy-start.7
  313.5 1.8 copy-start.15
  324.6 3.0 copy-start.6
  340.2 3.0 copy-start.6
  355.9 3.0 copy-start.6
  375.1 3.0 copy-start.4
  390.3 3.0 copy-start.4
  394.8 1.8 copy-start.5
  394.8 1.8 copy-start.12
  405.4 3.0 copy-start.4
  420.6 3.0 copy-start.4
  425.1 1.8 copy-start.5
  440.2 10.3 %copy-start.16 = (bf16[1,2048,128]{1,2,0:T(8,128)(2,1)S(1)}, bf16[1,2048,128]{1,2,0:T(8,128)(2,1)}, u32[]{:S(2)}) copy-start(bf16[1,2048,128]{1,2,0:T(8,128)(2,1)} %copy.207) | copy-start | bytes 1572868
  440.2 10.3 %copy-start.17 = (bf16[1,2048,128]{1,2,0:T(8,128)(2,1)S(1)}, bf16[1,2048,128]{1,2,0:T(8,128)(2,1)}, u32[]{:S(2)}) copy-start(bf16[1,2048,128]{1,2,0:T(8,128)(2,1)} %copy.208) | copy-start | bytes 1572868
  440.2 84.7 %all-to-all-start.1 = ((bf16[4,2,16,128,128]{4,1,3,0,2:T(2,128)(2,1)}), bf16[4,2,16,128,128]{4,1,3,0,2:T(2,128)(2,1)}, u32[]{:S(2)}, u32[]{:S(2)}) async-start(bf16[4,2,16,128,128]{4,1,3,0,2:T(2,128)(2,1)} %copy.189), calls=%async_computation.1 | async-start | bytes 8388608 | tf_op jit(solution)/shard_map/all_to_all | solution.py:172
  450.4 93.8 %reduce-scatter.4.cloned.1.call-start = ((), (), s32[]{:S(2)}) async-start(), calls=%async_computation.6 | async-start | bytes 2949120
  524.8 5.4 copy-start.20
  (23 other events, 37.3 us)
Sparse Core Ops, SparseCore 0:
  10.3 128.1 all-gather.6
  140.1 46.8 all-gather.4
  188.6 42.3 all-gather.8
  472.4 56.3 reduce-scatter.3

commit v2 on v0

v2 whole, which is shorter than its diff:
```python
import jax
import jax.numpy as jnp
from jax import lax
from jax.sharding import PartitionSpec as P
import functools
from jax.experimental import pallas as pl
from jax.experimental.pallas import tpu as pltpu


TILE = 128


def _scores_pass(mask_ref, s, qi, q, k_ref, s_scr, m_scr, l_scr, nb, scale):
    m_scr[...] = jnp.full(m_scr.shape, -jnp.inf, jnp.float32)
    l_scr[...] = jnp.zeros(l_scr.shape, jnp.float32)

    def first(j, carry):
        @pl.when(mask_ref[s, qi, j] != 0)
        def _():
            col = pl.multiple_of(j * TILE, TILE)
            kj = k_ref[0, pl.ds(col, TILE), :]
            sc = lax.dot_general(q, kj, ((( 1,), (1,)), ((), ())), preferred_element_type=jnp.float32) * scale
            s_scr[:, pl.ds(col, TILE)] = sc
            m_scr[...] = jnp.maximum(m_scr[...], jnp.max(sc, axis=1, keepdims=True))
        return carry

    lax.fori_loop(0, nb, first, 0)

    def second(j, carry):
        @pl.when(mask_ref[s, qi, j] != 0)
        def _():
            col = pl.multiple_of(j * TILE, TILE)
            e = jnp.exp(s_scr[:, pl.ds(col, TILE)] - m_scr[...])
            s_scr[:, pl.ds(col, TILE)] = e
            l_scr[...] = l_scr[...] + jnp.sum(e, axis=1, keepdims=True)
        return carry

    lax.fori_loop(0, nb, second, 0)


def _fwd_kernel(mask_ref, q_ref, k_ref, v_ref, o_ref, s_scr, m_scr, l_scr, acc_scr, *, nb, scale):
    s = pl.program_id(0)
    qi = pl.program_id(1)
    q = q_ref[0]
    _scores_pass(mask_ref, s, qi, q, k_ref, s_scr, m_scr, l_scr, nb, scale)
    acc_scr[...] = jnp.zeros(acc_scr.shape, jnp.float32)

    def third(j, carry):
        @pl.when(mask_ref[s, qi, j] != 0)
        def _():
            col = pl.multiple_of(j * TILE, TILE)
            prob = (s_scr[:, pl.ds(col, TILE)] / l_scr[...]).astype(jnp.bfloat16)
            vj = v_ref[0, pl.ds(col, TILE), :]
            acc_scr[...] += jnp.dot(prob, vj, preferred_element_type=jnp.float32)
        return carry

    lax.fori_loop(0, nb, third, 0)
    o_ref[0] = acc_scr[...].astype(o_ref.dtype)


def _bwd_kernel(mask_ref, q_ref, k_ref, v_ref, o_ref, do_ref, dq_ref, dk_ref, dv_ref,
                s_scr, m_scr, l_scr, dq_scr, dk_scr, dv_scr, *, nb, scale):
    s = pl.program_id(0)
    qi = pl.program_id(1)

    @pl.when(qi == 0)
    def _():
        dk_scr[...] = jnp.zeros(dk_scr.shape, jnp.float32)
        dv_scr[...] = jnp.zeros(dv_scr.shape, jnp.float32)

    q = q_ref[0]
    _scores_pass(mask_ref, s, qi, q, k_ref, s_scr, m_scr, l_scr, nb, scale)
    do = do_ref[0]
    delta = jnp.sum(do.astype(jnp.float32) * o_ref[0].astype(jnp.float32), axis=1, keepdims=True)
    m_scr[...] = delta
    dq_scr[...] = jnp.zeros(dq_scr.shape, jnp.float32)

    def third(j, carry):
        @pl.when(mask_ref[s, qi, j] != 0)
        def _():
            col = pl.multiple_of(j * TILE, TILE)
            prob = s_scr[:, pl.ds(col, TILE)] / l_scr[...]
            low = prob.astype(jnp.bfloat16)
            vj = v_ref[0, pl.ds(col, TILE), :]
            kj = k_ref[0, pl.ds(col, TILE), :]
            dv_scr[pl.ds(col, TILE), :] += lax.dot_general(
                low, do, (((0,), (0,)), ((), ())), preferred_element_type=jnp.float32)
            dp = lax.dot_general(do, vj, (((1,), (1,)), ((), ())), preferred_element_type=jnp.float32)
            ds = (prob * (dp - m_scr[...]) * scale).astype(jnp.bfloat16)
            dq_scr[...] += jnp.dot(ds, kj, preferred_element_type=jnp.float32)
            dk_scr[pl.ds(col, TILE), :] += lax.dot_general(
                ds, q, (((0,), (0,)), ((), ())), preferred_element_type=jnp.float32)
        return carry

    lax.fori_loop(0, nb, third, 0)
    dq_ref[0] = dq_scr[...].astype(dq_ref.dtype)

    @pl.when(qi == nb - 1)
    def _():
        dk_ref[0] = dk_scr[...].astype(dk_ref.dtype)
        dv_ref[0] = dv_scr[...].astype(dv_ref.dtype)


def attn_forward(mask, q, k, v, scale, interpret=False):
    slots, length, hd = q.shape
    nb = length // TILE
    row = pl.BlockSpec((1, TILE, hd), lambda s, i, m: (s, i, 0))
    full = pl.BlockSpec((1, length, hd), lambda s, i, m: (s, 0, 0))
    return pl.pallas_call(
        functools.partial(_fwd_kernel, nb=nb, scale=scale),
        grid_spec=pltpu.PrefetchScalarGridSpec(
            num_scalar_prefetch=1,
            grid=(slots, nb),
            in_specs=[row, full, full],
            out_specs=row,
            scratch_shapes=[
                pltpu.VMEM((TILE, length), jnp.float32),
                pltpu.VMEM((TILE, 1), jnp.float32),
                pltpu.VMEM((TILE, 1), jnp.float32),
                pltpu.VMEM((TILE, hd), jnp.float32),
            ],
        ),
        out_shape=jax.ShapeDtypeStruct(q.shape, jnp.bfloat16),
        compiler_params=pltpu.CompilerParams(dimension_semantics=("arbitrary", "arbitrary")),
        interpret=interpret,
    )(mask, q, k, v)


def attn_backward(mask, q, k, v, o, do, scale, interpret=False):
    slots, length, hd = q.shape
    nb = length // TILE
    row = pl.BlockSpec((1, TILE, hd), lambda s, i, m: (s, i, 0))
    full = pl.BlockSpec((1, length, hd), lambda s, i, m: (s, 0, 0))
    shape = jax.ShapeDtypeStruct(q.shape, jnp.bfloat16)
    return pl.pallas_call(
        functools.partial(_bwd_kernel, nb=nb, scale=scale),
        grid_spec=pltpu.PrefetchScalarGridSpec(
            num_scalar_prefetch=1,
            grid=(slots, nb),
            in_specs=[row, full, full, row, row],
            out_specs=[row, full, full],
            scratch_shapes=[
                pltpu.VMEM((TILE, length), jnp.float32),
                pltpu.VMEM((TILE, 1), jnp.float32),
                pltpu.VMEM((TILE, 1), jnp.float32),
                pltpu.VMEM((TILE, hd), jnp.float32),
                pltpu.VMEM((length, hd), jnp.float32),
                pltpu.VMEM((length, hd), jnp.float32),
            ],
        ),
        out_shape=(shape, shape, shape),
        compiler_params=pltpu.CompilerParams(dimension_semantics=("arbitrary", "arbitrary")),
        interpret=interpret,
    )(mask, q, k, v, o, do)


def slot_table(head_owner, most_slots, seq_count):
    head_count = head_owner.shape[0]
    same_owner = head_owner[:, None] == head_owner[None, :]
    earlier = jnp.arange(head_count)[None, :] < jnp.arange(head_count)[:, None]
    owner_rank = jnp.sum(jnp.logical_and(same_owner, earlier), axis=1)
    slot_index = head_owner * most_slots + owner_rank
    return slot_index[:, None] == jnp.arange(seq_count * most_slots, dtype=jnp.int32)[None, :]


def heads_to_tokens(received, select, token_count, head_count, head_dim):
    merged = jnp.einsum("jtd,hj->thd", received[:, 0], select, preferred_element_type=jnp.float32)
    return merged.astype(jnp.bfloat16).reshape(1, token_count, head_count * head_dim)


def on_device(query_tok, key_tok, value_tok, grad_out, out_weight, block_mask, head_owner):
    seq_count = lax.axis_size("seq")
    most_slots = out_weight.shape[0]
    head_dim = out_weight.shape[1]
    token_count = query_tok.shape[1]
    head_count = block_mask.shape[0]
    length = seq_count * token_count
    score_scale = head_dim ** (-0.5)
    grad_scale = (lax.axis_size("dp") * length) ** (-0.5)
    table = slot_table(head_owner, most_slots, seq_count)
    select = table.astype(jnp.bfloat16)
    my_first = lax.axis_index("seq") * most_slots
    local_select = lax.dynamic_slice_in_dim(table.astype(jnp.float32), my_first, most_slots, 1)
    slot_blocks = jnp.einsum("hs,hab->sab", local_select, block_mask.astype(jnp.float32))
    slot_used = jnp.sum(local_select, axis=0)
    diagonal = jnp.eye(block_mask.shape[1], dtype=jnp.float32)
    slot_blocks = slot_blocks + (1.0 - slot_used)[:, None, None] * diagonal[None]
    slot_mask = (slot_blocks > 0.5).astype(jnp.int32)

    def to_slots(tensor):
        split_heads = tensor[0].reshape(token_count, head_count, head_dim)
        spread = jnp.einsum("thd,hj->jtd", split_heads, select, preferred_element_type=jnp.float32)
        return spread.astype(jnp.bfloat16).reshape(seq_count, most_slots, token_count, head_dim)

    stacked = jnp.stack([to_slots(query_tok), to_slots(key_tok), to_slots(value_tok)], axis=1)
    arrived = lax.all_to_all(stacked, "seq", split_axis=0, concat_axis=3, tiled=True)[0]
    slot_query = arrived[0]
    slot_key = arrived[1]
    slot_value = arrived[2]
    weight_full = lax.all_gather(out_weight, "dp", axis=2, tiled=True)
    slot_out = attn_forward(slot_mask, slot_query, slot_key, slot_value, score_scale)

    def back_layout(stacked):
        return stacked.reshape(most_slots, seq_count, token_count, head_dim)

    out_back = lax.all_to_all(back_layout(slot_out), "seq", split_axis=1, concat_axis=0, tiled=True)

    dy_rows = lax.all_gather(grad_out, "seq", axis=1, tiled=True)[0]
    part = jnp.einsum(
        "td,shd->sth", dy_rows, weight_full, preferred_element_type=jnp.float32
    ).astype(jnp.bfloat16)
    grad_attn = part
    weight_total = jnp.einsum("sth,td->shd", slot_out, dy_rows, preferred_element_type=jnp.float32)
    grad_attn, weight_total = (grad_attn, weight_total)
    weight_grad = lax.psum_scatter(
        (weight_total * grad_scale).astype(jnp.bfloat16), "dp", scatter_dimension=2, tiled=True
    ).astype(jnp.float32)
    slot_qgrad, slot_kgrad, slot_vgrad = attn_backward(
        slot_mask, slot_query, slot_key, slot_value, slot_out, grad_attn, score_scale
    )
    back_stack = jnp.stack([back_layout(slot_qgrad), back_layout(slot_kgrad), back_layout(slot_vgrad)])
    grads_back = lax.all_to_all(back_stack, "seq", split_axis=2, concat_axis=1, tiled=True)
    all_back = (out_back, grads_back[0], grads_back[1], grads_back[2])
    attn_out = heads_to_tokens(all_back[0], select, token_count, head_count, head_dim)
    query_grad = heads_to_tokens(all_back[1], select, token_count, head_count, head_dim)
    key_grad = heads_to_tokens(all_back[2], select, token_count, head_count, head_dim)
    value_grad = heads_to_tokens(all_back[3], select, token_count, head_count, head_dim)
    return (attn_out, query_grad, key_grad, value_grad, weight_grad)


def solution(mesh):
    placed = (
        P("dp", "seq", None),
        P("dp", "seq", None),
        P("dp", "seq", None),
        P("dp", "seq", None),
        P("seq", None, "dp"),
        P(),
        P(),
    )
    return jax.shard_map(
        on_device,
        mesh=mesh,
        in_specs=placed,
        out_specs=(
            P("dp", "seq", None),
            P("dp", "seq", None),
            P("dp", "seq", None),
            P("dp", "seq", None),
            P("seq", None, "dp"),
        ),
        check_vma=False,
    )
```

time: 471 us -> 451 us (0.958)
  Pallas kernels: 0 us -> 251 us
  matrix products: 123 us -> 30.2 us
  local copies, waits for them, and re-layouts: 130 us -> 39.7 us
  waiting for transfers between devices: 127 us -> 86 us
  starting transfers between devices: 37 us -> 17.8 us
  other arithmetic: 19.7 us -> 6.12 us
  loops' own time: 11.7 us -> 0 us
    pallas_call x0 -> x2, Pallas kernels: none -> 251 us  [the longest x1 136 us: attn_backward(): pl.pallas_call(functools.partial(_bwd_kernel, nb=nb, scale=scale), grid_s...]
    dot_general x56 -> x0, matrix products: 93.1 us -> none  [the longest x16 35 us: block_probs(): jnp.dot(q_rows, keys_all.T, preferred_element_type=jnp.float32)]
    broadcast_in_dim x32 -> x0, local copies, waits for them, and re-layouts: 55.8 us -> none  [allowed_rows(): spread = jnp.repeat(jnp.repeat(band, block_len, axis=0), block_len, axis=1)]
    all_gather x1, waiting for transfers between devices: 26.6 us -> 0.02 us  [on_device(): dy_rows = lax.all_gather(grad_out, 'seq', axis=1, tiled=True)[0]]
    all_to_all x6 -> x2, starting transfers between devices: 31.9 us -> 13.3 us  [the longest x1 9.41 us: on_device(): lax.all_to_all(stacked, 'seq', split_axis=0, concat_axis=3, tiled=True)[0]]
    dynamic_slice x32 -> x0, local copies, waits for them, and re-layouts: 17.9 us -> none  [the longest x16 9.54 us: forward_slot(): return lax.map(forward_one_block, numbers).reshape(queries.shape)]
    all_to_all x6 -> x2, waiting for transfers between devices: 99 us -> 84.6 us  [the longest x1 54.3 us: on_device(): lax.all_to_all(stacked, 'seq', split_axis=0, concat_axis=3, tiled=True)[0]]
    reduce_sum x24 -> x0, other arithmetic: 12.6 us -> none  [the longest x16 11.4 us: block_probs(): return expd / jnp.sum(expd, axis=1, keepdims=True)]
  transfers between devices with their start and end apart: 10 -> 6, of which waited for: 7 -> 2; matrix products, arithmetic and copies ran while one was open for 58% -> 16% of each run, Pallas kernels for 0% -> 56%
where the time goes in v2:
time: 451 us; the launch traced here: 445 us
  Pallas kernels  251 us (56%)
  waiting for transfers between devices  86 us (19%)
  local copies, waits for them, and re-layouts  39.7 us (9%)
  matrix products  30.2 us (7%)
  starting transfers between devices  17.8 us (4%)
  between operations  14 us (3%)
  other arithmetic  6.12 us (1%)
    pallas_call x1, Pallas kernels, attn_backward(): pl.pallas_call(functools.partial(_bwd_kernel, nb=nb, scale=scale), grid_s...  136 us
    pallas_call x1, Pallas kernels, attn_forward(): pl.pallas_call(functools.partial(_fwd_kernel, nb=nb, scale=scale), grid_s...  114 us
    all_to_all x1, waiting for transfers between devices, on_device(): lax.all_to_all(stacked, 'seq', split_axis=0, concat_axis=3, tiled=True)[0]  54.3 us
    all_to_all x1, waiting for transfers between devices, on_device(): lax.all_to_all(back_stack, 'seq', split_axis=2, concat_axis=1, tiled=True)  30.3 us
    unnamed x23, local copies, waits for them, and re-layouts  18.3 us
    dot_general x1, matrix products, on_device(): jnp.einsum('sth,td->shd', slot_out, dy_rows, preferred_element_type=jnp.f...  14.1 us
    dot_general x1, matrix products, on_device(): jnp.einsum('td,shd->sth', dy_rows, weight_full, preferred_element_type=jn...  11.4 us
    all_to_all x1, starting transfers between devices, on_device(): lax.all_to_all(stacked, 'seq', split_axis=0, concat_axis=3, tiled=True)[0]  9.41 us
  transfers between devices with their start and end apart: 6, of which 2 were waited for; matrix products, arithmetic and copies ran while one was open for 16% of the time, Pallas kernels for 56%

profile of v2, /device:TPU:1, one launch (start us, length us, event | category | flops | bytes accessed | tf_op | source)
XLA Modules:
  0.0 444.6 jit_solution(483871104251166099)
XLA Ops:
  7.9 1.5 copy.138
  12.7 1.4 copy.142
  15.5 2.0 pad_maximum_fusion
  17.5 9.4 %all-to-all-start = ((bf16[16,3,2,128,128]{4,3,2,1,0:T(8,128)(2,1)}), bf16[16,3,2,128,128]{4,3,2,1,0:T(8,128)(2,1)S(1)}, u32[]{:S(2)}, u32[]{:S(2)}) async-start(bf16[16,3,2,128,128]{4,3,2,1,0:T(8,128)(2,1)} %pad_maximum_fusion), calls=%async_computation | async-start | bytes 6291456 | tf_op jit(solution)/shard_map/all_to_all | solution.py:196
  28.9 54.3 %all-to-all-done = bf16[16,3,2,128,128]{4,3,2,1,0:T(8,128)(2,1)S(1)} async-done(((bf16[16,3,2,128,128]{4,3,2,1,0:T(8,128)(2,1)}), bf16[16,3,2,128,128]{4,3,2,1,0:T(8,128)(2,1)S(1)}, u32[]{:S(2)}, u32[]{:S(2)}) %all-to-all-start) | async-done | bytes 3145760 | tf_op jit(solution)/shard_map/all_to_all | solution.py:196
  83.4 1.1 copy.149
  84.6 1.1 copy.148
  85.7 1.1 copy.147
  86.8 114.4 %shard_map.110.o_ref = bf16[2,2048,128]{2,1,0:T(8,128)(2,1)} custom-call(s32[2,16,16]{2,1,0:T(8,128)} %fusion.23.mask_ref, bf16[2,2048,128]{2,1,0:T(8,128)(2,1)} %bitcast.96, bf16[2,2048,128]{2,1,0:T(8,128)(2,1)} %bitcast.94, bf16[2,2048,128]{2,1,0:T(8,128)(2,1)} %bitcast.92), custom_call_target="tpu_custom_call" | custom-call | tf_op jit(solution)/shard_map/pallas_call | solution.py:109
  201.2 2.4 copy.150
  203.6 4.2 all-to-all-start.1
  208.1 14.1 %fusion.7 = bf16[2,128,5120]{2,1,0:T(8,128)(2,1)} fusion(bf16[2,2048,128]{2,1,0:T(8,128)(2,1)S(1)} %copy-done, bf16[1,2048,5120]{2,1,0:T(8,128)(2,1)} %all-gather.5.cloned.1.call-done), kind=kOutput, calls=%fused_computation.5 | convolution fusion | flops 5371330560 | bytes 24641536 | tf_op jit(solution)/shard_map/sth,td->shd/dot_general | solution.py:213
  222.2 5.9 %copy.173 = bf16[2,128,5120]{1,0,2:T(2,128)(2,1)S(1)} copy(bf16[2,128,5120]{2,1,0:T(8,128)(2,1)} %fusion.7) | data formatting | bytes 5242880
  228.1 1.8 copy.182
  230.0 11.4 %fusion.13.do_ref = bf16[2,2048,128]{2,1,0:T(8,128)(2,1)} fusion(bf16[2,128,5120]{2,1,0:T(8,128)(2,1)} %all-gather.3.cloned.1.call-done, bf16[1,2048,5120]{2,1,0:T(8,128)(2,1)} %all-gather.5.cloned.1.call-done), kind=kOutput, calls=%fused_computation.10 | convolution fusion | flops 5369233408 | bytes 24641536 | tf_op jit(solution)/shard_map/td,shd->sth/dot_general | solution.py:209
  241.4 136.4 %shard_map.111 = (bf16[2,2048,128]{2,1,0:T(8,128)(2,1)}, bf16[2,2048,128]{2,1,0:T(8,128)(2,1)}, bf16[2,2048,128]{2,1,0:T(8,128)(2,1)}) custom-call(s32[2,16,16]{2,1,0:T(8,128)} %fusion.23.mask_ref, bf16[2,2048,128]{2,1,0:T(8,128)(2,1)} %bitcast.97, bf16[2,2048,128]{2,1,0:T(8,128)(2,1)} %bitcast.95, bf16[2,2048,128]{2,1,0:T(8,128)(2,1)} %bitcast.93, ...), custom_call_target="tpu_custom_call" | custom-call | tf_op jit(solution)/shard_map/pallas_call | solution.py:135
  377.8 2.2 pad_maximum_fusion.1
  380.0 2.1 copy.172
  382.1 3.9 all-to-all-start.2
  386.0 2.3 copy.151
  388.3 1.3 fusion.16
  389.6 2.3 copy.152
  391.9 2.2 copy.164
  394.1 30.3 %all-to-all-done.2 = bf16[3,2,16,128,128]{4,3,1,0,2:T(8,128)(2,1)S(1)} async-done(((bf16[3,2,16,128,128]{4,3,1,0,2:T(8,128)(2,1)}), bf16[3,2,16,128,128]{4,3,1,0,2:T(8,128)(2,1)S(1)}, u32[]{:S(2)}, u32[]{:S(2)}) %all-to-all-start.2) | async-done | bytes 3145760 | tf_op jit(solution)/shard_map/all_to_all | solution.py:222
  424.4 1.6 fusion.41
  426.0 1.1 copy.161
  428.0 1.1 copy.167
  429.1 1.1 copy.159
  431.1 1.1 copy.166
  432.1 1.1 copy.157
  434.1 1.1 copy.165
  435.2 1.1 reshape.62
  (49 shorter events, 12.3 us)
Async XLA Ops:
  7.2 2.7 copy-start.5
  7.2 200.9 %all-gather.5.cloned.1.call-start = ((), (), s32[]{:S(2)}) async-start(), calls=%async_computation.5 | async-start | bytes 22282240 | tf_op jit(solution)/shard_map/all_gather | solution.py:208
  7.9 3.1 copy-start.3
  17.5 10.3 %copy-start.4 = (s32[20,16,16]{0,2,1:T(8,128)S(1)}, s32[20,16,16]{0,2,1:T(8,128)}, u32[]{:S(2)}) copy-start(s32[20,16,16]{0,2,1:T(8,128)} %param.12) | copy-start | bytes 61444
  17.5 65.7 %all-to-all-start = ((bf16[16,3,2,128,128]{4,3,2,1,0:T(8,128)(2,1)}), bf16[16,3,2,128,128]{4,3,2,1,0:T(8,128)(2,1)S(1)}, u32[]{:S(2)}, u32[]{:S(2)}) async-start(bf16[16,3,2,128,128]{4,3,2,1,0:T(8,128)(2,1)} %pad_maximum_fusion), calls=%async_computation | async-start | bytes 6291456 | tf_op jit(solution)/shard_map/all_to_all | solution.py:196
  26.9 203.0 %all-gather.3.cloned.1.call-start = ((), (), s32[]{:S(2)}) async-start(), calls=%async_computation.4 | async-start | bytes 2949120 | tf_op jit(solution)/shard_map/all_gather | solution.py:200
  201.2 6.9 %copy-start = (bf16[2,2048,128]{2,1,0:T(8,128)(2,1)S(1)}, bf16[2,2048,128]{2,1,0:T(8,128)(2,1)}, u32[]{:S(2)}) copy-start(bf16[2,2048,128]{2,1,0:T(8,128)(2,1)} %shard_map.110.o_ref) | copy-start | bytes 3145732
  203.6 178.5 %all-to-all-start.1 = ((bf16[2,16,128,128]{3,2,0,1:T(8,128)(2,1)}), bf16[2,16,128,128]{3,2,0,1:T(8,128)(2,1)}, u32[]{:S(2)}, u32[]{:S(2)}) async-start(bf16[2,16,128,128]{3,2,0,1:T(8,128)(2,1)} %copy.150), calls=%async_computation.1 | async-start | bytes 2097152 | tf_op jit(solution)/shard_map/all_to_all | solution.py:206
  207.8 227.4 %reduce-scatter.4.cloned.1.call-start = ((), (), s32[]{:S(2)}) async-start(), calls=%async_computation.6 | async-start | bytes 2949120
  382.1 42.3 %all-to-all-start.2 = ((bf16[3,2,16,128,128]{4,3,1,0,2:T(8,128)(2,1)}), bf16[3,2,16,128,128]{4,3,1,0,2:T(8,128)(2,1)S(1)}, u32[]{:S(2)}, u32[]{:S(2)}) async-start(bf16[3,2,16,128,128]{4,3,1,0,2:T(8,128)(2,1)} %copy.172), calls=%async_computation.2 | async-start | bytes 6291456 | tf_op jit(solution)/shard_map/all_to_all | solution.py:222
  426.0 3.1 copy-start.2
  429.1 3.1 copy-start.1
Sparse Core Ops, SparseCore 0:
  10.5 164.2 all-gather.4
  176.4 41.6 all-gather.2
  230.1 38.8 reduce-scatter.3

commit v3 on v2

v3 whole, which is shorter than its diff:
```python
import jax
import jax.numpy as jnp
from jax import lax
from jax.sharding import PartitionSpec as P
import functools
from jax.experimental import pallas as pl
from jax.experimental.pallas import tpu as pltpu


TILE = 128
NT = (((1,), (1,)), ((), ()))
TN = (((0,), (0,)), ((), ()))


def _probs(q, k, bias, scale):
    sc = lax.dot_general(q, k, NT, preferred_element_type=jnp.float32) * scale + bias
    e = jnp.exp(sc - jnp.max(sc, axis=1, keepdims=True))
    return e / jnp.sum(e, axis=1, keepdims=True)


def _fwd_kernel(q_ref, k_ref, v_ref, b_ref, o_ref, *, scale):
    prob = _probs(q_ref[0], k_ref[0], b_ref[0, 0], scale)
    out = jnp.dot(prob.astype(jnp.bfloat16), v_ref[0], preferred_element_type=jnp.float32)
    o_ref[0] = out.astype(o_ref.dtype)


def _bwd_kernel(q_ref, k_ref, v_ref, b_ref, o_ref, do_ref, dq_ref, dk_ref, dv_ref,
                dk_scr, dv_scr, *, nb, scale):
    qi = pl.program_id(1)

    @pl.when(qi == 0)
    def _():
        dk_scr[...] = jnp.zeros(dk_scr.shape, jnp.float32)
        dv_scr[...] = jnp.zeros(dv_scr.shape, jnp.float32)

    q = q_ref[0]
    k = k_ref[0]
    v = v_ref[0]
    do = do_ref[0]
    prob = _probs(q, k, b_ref[0, 0], scale)
    low = prob.astype(jnp.bfloat16)
    delta = jnp.sum(do.astype(jnp.float32) * o_ref[0].astype(jnp.float32), axis=1, keepdims=True)
    dv_scr[...] += lax.dot_general(low, do, TN, preferred_element_type=jnp.float32)
    dp = lax.dot_general(do, v, NT, preferred_element_type=jnp.float32)
    ds = (prob * (dp - delta) * scale).astype(jnp.bfloat16)
    dq_ref[0] = jnp.dot(ds, k, preferred_element_type=jnp.float32).astype(dq_ref.dtype)
    dk_scr[...] += lax.dot_general(ds, q, TN, preferred_element_type=jnp.float32)

    @pl.when(qi == nb - 1)
    def _():
        dk_ref[0] = dk_scr[...].astype(dk_ref.dtype)
        dv_ref[0] = dv_scr[...].astype(dv_ref.dtype)


def mask_bias(slot_mask, length):
    spread = jnp.repeat(slot_mask, length // slot_mask.shape[2], axis=2)
    return jnp.where(spread > 0, 0.0, -jnp.inf).astype(jnp.float32)[:, :, None, :]


def attn_forward(bias, q, k, v, scale, interpret=False):
    slots, length, hd = q.shape
    nb = length // TILE
    row = pl.BlockSpec((1, TILE, hd), lambda s, i: (s, i, 0))
    full = pl.BlockSpec((1, length, hd), lambda s, i: (s, 0, 0))
    brow = pl.BlockSpec((1, 1, 1, length), lambda s, i: (s, i, 0, 0))
    return pl.pallas_call(
        functools.partial(_fwd_kernel, scale=scale),
        grid=(slots, nb),
        in_specs=[row, full, full, brow],
        out_specs=row,
        out_shape=jax.ShapeDtypeStruct(q.shape, jnp.bfloat16),
        compiler_params=pltpu.CompilerParams(dimension_semantics=("arbitrary", "arbitrary")),
        interpret=interpret,
    )(q, k, v, bias)


def attn_backward(bias, q, k, v, o, do, scale, interpret=False):
    slots, length, hd = q.shape
    nb = length // TILE
    row = pl.BlockSpec((1, TILE, hd), lambda s, i: (s, i, 0))
    full = pl.BlockSpec((1, length, hd), lambda s, i: (s, 0, 0))
    brow = pl.BlockSpec((1, 1, 1, length), lambda s, i: (s, i, 0, 0))
    shape = jax.ShapeDtypeStruct(q.shape, jnp.bfloat16)
    return pl.pallas_call(
        functools.partial(_bwd_kernel, nb=nb, scale=scale),
        grid=(slots, nb),
        in_specs=[row, full, full, brow, row, row],
        out_specs=[row, full, full],
        out_shape=(shape, shape, shape),
        scratch_shapes=[pltpu.VMEM((length, hd), jnp.float32), pltpu.VMEM((length, hd), jnp.float32)],
        compiler_params=pltpu.CompilerParams(dimension_semantics=("arbitrary", "arbitrary")),
        interpret=interpret,
    )(q, k, v, bias, o, do)


def slot_table(head_owner, most_slots, seq_count):
    head_count = head_owner.shape[0]
    same_owner = head_owner[:, None] == head_owner[None, :]
    earlier = jnp.arange(head_count)[None, :] < jnp.arange(head_count)[:, None]
    owner_rank = jnp.sum(jnp.logical_and(same_owner, earlier), axis=1)
    slot_index = head_owner * most_slots + owner_rank
    return slot_index[:, None] == jnp.arange(seq_count * most_slots, dtype=jnp.int32)[None, :]


def heads_to_tokens(received, select, token_count, head_count, head_dim):
    merged = jnp.einsum("jtd,hj->thd", received[:, 0], select, preferred_element_type=jnp.float32)
    return merged.astype(jnp.bfloat16).reshape(1, token_count, head_count * head_dim)


def on_device(query_tok, key_tok, value_tok, grad_out, out_weight, block_mask, head_owner):
    seq_count = lax.axis_size("seq")
    most_slots = out_weight.shape[0]
    head_dim = out_weight.shape[1]
    token_count = query_tok.shape[1]
    head_count = block_mask.shape[0]
    length = seq_count * token_count
    score_scale = head_dim ** (-0.5)
    grad_scale = (lax.axis_size("dp") * length) ** (-0.5)
    table = slot_table(head_owner, most_slots, seq_count)
    select = table.astype(jnp.bfloat16)
    my_first = lax.axis_index("seq") * most_slots
    local_select = lax.dynamic_slice_in_dim(table.astype(jnp.float32), my_first, most_slots, 1)
    slot_blocks = jnp.einsum("hs,hab->sab", local_select, block_mask.astype(jnp.float32))
    slot_used = jnp.sum(local_select, axis=0)
    diagonal = jnp.eye(block_mask.shape[1], dtype=jnp.float32)
    slot_blocks = slot_blocks + (1.0 - slot_used)[:, None, None] * diagonal[None]
    slot_mask = (slot_blocks > 0.5).astype(jnp.int32)
    bias = mask_bias(slot_mask, length)

    def to_slots(tensor):
        split_heads = tensor[0].reshape(token_count, head_count, head_dim)
        spread = jnp.einsum("thd,hj->jtd", split_heads, select, preferred_element_type=jnp.float32)
        return spread.astype(jnp.bfloat16).reshape(seq_count, most_slots, token_count, head_dim)

    stacked = jnp.stack([to_slots(query_tok), to_slots(key_tok), to_slots(value_tok)], axis=1)
    arrived = lax.all_to_all(stacked, "seq", split_axis=0, concat_axis=3, tiled=True)[0]
    slot_query = arrived[0]
    slot_key = arrived[1]
    slot_value = arrived[2]
    weight_full = lax.all_gather(out_weight, "dp", axis=2, tiled=True)
    slot_out = attn_forward(bias, slot_query, slot_key, slot_value, score_scale)

    def back_layout(stacked):
        return stacked.reshape(most_slots, seq_count, token_count, head_dim)

    out_back = lax.all_to_all(back_layout(slot_out), "seq", split_axis=1, concat_axis=0, tiled=True)

    dy_rows = lax.all_gather(grad_out, "seq", axis=1, tiled=True)[0]
    part = jnp.einsum(
        "td,shd->sth", dy_rows, weight_full, preferred_element_type=jnp.float32
    ).astype(jnp.bfloat16)
    grad_attn = part
    weight_total = jnp.einsum("sth,td->shd", slot_out, dy_rows, preferred_element_type=jnp.float32)
    grad_attn, weight_total = (grad_attn, weight_total)
    weight_grad = lax.psum_scatter(
        (weight_total * grad_scale).astype(jnp.bfloat16), "dp", scatter_dimension=2, tiled=True
    ).astype(jnp.float32)
    slot_qgrad, slot_kgrad, slot_vgrad = attn_backward(
        bias, slot_query, slot_key, slot_value, slot_out, grad_attn, score_scale
    )
    back_stack = jnp.stack([back_layout(slot_qgrad), back_layout(slot_kgrad), back_layout(slot_vgrad)])
    grads_back = lax.all_to_all(back_stack, "seq", split_axis=2, concat_axis=1, tiled=True)
    all_back = (out_back, grads_back[0], grads_back[1], grads_back[2])
    attn_out = heads_to_tokens(all_back[0], select, token_count, head_count, head_dim)
    query_grad = heads_to_tokens(all_back[1], select, token_count, head_count, head_dim)
    key_grad = heads_to_tokens(all_back[2], select, token_count, head_count, head_dim)
    value_grad = heads_to_tokens(all_back[3], select, token_count, head_count, head_dim)
    return (attn_out, query_grad, key_grad, value_grad, weight_grad)


def solution(mesh):
    placed = (
        P("dp", "seq", None),
        P("dp", "seq", None),
        P("dp", "seq", None),
        P("dp", "seq", None),
        P("seq", None, "dp"),
        P(),
        P(),
    )
    return jax.shard_map(
        on_device,
        mesh=mesh,
        in_specs=placed,
        out_specs=(
            P("dp", "seq", None),
            P("dp", "seq", None),
            P("dp", "seq", None),
            P("dp", "seq", None),
            P("seq", None, "dp"),
        ),
        check_vma=False,
    )
```

time: 451 us -> 367 us (0.81)
  Pallas kernels: 251 us -> 83.6 us
  waiting for transfers between devices: 86 us -> 164 us
  starting transfers between devices: 17.8 us -> 26.3 us
    pallas_call x2, Pallas kernels: 251 us -> 83.6 us  [the longest x1 53.3 us: attn_backward(): pl.pallas_call(functools.partial(_bwd_kernel, nb=nb, scale=scale), grid=(...]
    all_gather x1, waiting for transfers between devices: 0.02 us -> 59.5 us  [on_device(): dy_rows = lax.all_gather(grad_out, 'seq', axis=1, tiled=True)[0]]
    all_gather x1, waiting for transfers between devices: 0.02 us -> 15.8 us  [on_device(): weight_full = lax.all_gather(out_weight, 'dp', axis=2, tiled=True)]
    all_to_all x1, starting transfers between devices: 3.86 us -> 10.7 us  [on_device(): lax.all_to_all(back_stack, 'seq', split_axis=2, concat_axis=1, tiled=True)]
  transfers between devices with their start and end apart: 6 -> 6, of which waited for: 2 -> 4; matrix products, arithmetic and copies ran while one was open for 16% -> 20% of each run, Pallas kernels for 56% -> 23%
where the time goes in v3:
time: 367 us; the launch traced here: 364 us
  waiting for transfers between devices  164 us (45%)
  Pallas kernels  83.6 us (23%)
  local copies, waits for them, and re-layouts  40.5 us (11%)
  matrix products  30 us (8%)
  starting transfers between devices  26.3 us (7%)
  between operations  14 us (4%)
  other arithmetic  5.42 us (1%)
    all_gather x1, waiting for transfers between devices, on_device(): dy_rows = lax.all_gather(grad_out, 'seq', axis=1, tiled=True)[0]  59.5 us
    all_to_all x1, waiting for transfers between devices, on_device(): lax.all_to_all(stacked, 'seq', split_axis=0, concat_axis=3, tiled=True)[0]  55 us
    pallas_call x1, Pallas kernels, attn_backward(): pl.pallas_call(functools.partial(_bwd_kernel, nb=nb, scale=scale), grid=(...  53.3 us
    all_to_all x1, waiting for transfers between devices, on_device(): lax.all_to_all(back_stack, 'seq', split_axis=2, concat_axis=1, tiled=True)  32.4 us
    pallas_call x1, Pallas kernels, attn_forward(): pl.pallas_call(functools.partial(_fwd_kernel, scale=scale), grid=(slots,...  30.2 us
    unnamed x23, local copies, waits for them, and re-layouts  18.3 us
    all_gather x1, waiting for transfers between devices, on_device(): weight_full = lax.all_gather(out_weight, 'dp', axis=2, tiled=True)  15.8 us
    dot_general x1, matrix products, on_device(): jnp.einsum('sth,td->shd', slot_out, dy_rows, preferred_element_type=jnp.f...  14 us
  transfers between devices with their start and end apart: 6, of which 4 were waited for; matrix products, arithmetic and copies ran while one was open for 20% of the time, Pallas kernels for 23%

profile of v3, /device:TPU:1, one launch (start us, length us, event | category | flops | bytes accessed | tf_op | source)
XLA Modules:
  0.0 363.9 jit_solution(7518728576798006821)
XLA Ops:
  7.9 1.5 copy.136
  12.7 1.4 copy.140
  15.5 2.0 pad_maximum_fusion
  17.5 9.4 %all-to-all-start = ((bf16[16,3,2,128,128]{4,3,2,1,0:T(8,128)(2,1)}), bf16[16,3,2,128,128]{4,3,2,1,0:T(8,128)(2,1)S(1)}, u32[]{:S(2)}, u32[]{:S(2)}) async-start(bf16[16,3,2,128,128]{4,3,2,1,0:T(8,128)(2,1)} %pad_maximum_fusion), calls=%async_computation | async-start | bytes 6291456 | tf_op jit(solution)/shard_map/all_to_all | solution.py:136
  28.2 55.0 %all-to-all-done = bf16[16,3,2,128,128]{4,3,2,1,0:T(8,128)(2,1)S(1)} async-done(((bf16[16,3,2,128,128]{4,3,2,1,0:T(8,128)(2,1)}), bf16[16,3,2,128,128]{4,3,2,1,0:T(8,128)(2,1)S(1)}, u32[]{:S(2)}, u32[]{:S(2)}) %all-to-all-start) | async-done | bytes 3145760 | tf_op jit(solution)/shard_map/all_to_all | solution.py:136
  83.4 1.1 copy.147
  84.6 1.1 copy.146
  85.7 1.1 copy.145
  87.6 30.2 %shard_map.110.o_ref = bf16[2,2048,128]{2,1,0:T(8,128)(2,1)} custom-call(bf16[2,2048,128]{2,1,0:T(8,128)(2,1)} %bitcast.97, bf16[2,2048,128]{2,1,0:T(8,128)(2,1)} %bitcast.95, bf16[2,2048,128]{2,1,0:T(8,128)(2,1)} %bitcast.93, f32[2,16,1,2048]{3,2,1,0:T(1,128)} %bitcast.113), custom_call_target="tpu_custom_call" | custom-call | tf_op jit(solution)/shard_map/pallas_call | solution.py:66
  117.9 2.4 copy.150
  120.3 5.9 %all-to-all-start.1 = ((bf16[2,16,128,128]{3,2,0,1:T(8,128)(2,1)}), bf16[2,16,128,128]{3,2,0,1:T(8,128)(2,1)}, u32[]{:S(2)}, u32[]{:S(2)}) async-start(bf16[2,16,128,128]{3,2,0,1:T(8,128)(2,1)} %copy.150), calls=%async_computation.1 | async-start | bytes 2097152 | tf_op jit(solution)/shard_map/all_to_all | solution.py:146
  126.4 59.5 %all-gather.5.cloned.1.call-done = bf16[1,2048,5120]{2,1,0:T(8,128)(2,1)} async-done(((bf16[1,128,5120]{2,1,0:T(8,128)(2,1)}), bf16[1,2048,5120]{2,1,0:T(8,128)(2,1)}) %all-gather.5.cloned.1.call-update) | async-done | bytes 20971536 | tf_op jit(solution)/shard_map/all_gather | solution.py:148
  185.9 14.0 %fusion.7 = bf16[2,128,5120]{2,1,0:T(8,128)(2,1)} fusion(bf16[2,2048,128]{2,1,0:T(8,128)(2,1)S(1)} %copy-done, bf16[1,2048,5120]{2,1,0:T(8,128)(2,1)} %all-gather.5.cloned.1.call-done), kind=kOutput, calls=%fused_computation.5 | convolution fusion | flops 5371330560 | bytes 24641536 | tf_op jit(solution)/shard_map/sth,td->shd/dot_general | solution.py:153
  199.9 5.9 %copy.173 = bf16[2,128,5120]{1,0,2:T(2,128)(2,1)S(1)} copy(bf16[2,128,5120]{2,1,0:T(8,128)(2,1)} %fusion.7) | data formatting | bytes 5242880
  205.8 1.8 copy.177
  207.7 15.8 %all-gather.3.cloned.1.call-done = bf16[2,128,5120]{2,1,0:T(8,128)(2,1)} async-done(((bf16[2,128,640]{2,1,0:T(8,128)(2,1)}), bf16[2,128,5120]{2,1,0:T(8,128)(2,1)}) %all-gather.3.cloned.1.call-update) | async-done | bytes 2621456 | tf_op jit(solution)/shard_map/all_gather | solution.py:140
  223.5 11.4 %fusion.13.do_ref = bf16[2,2048,128]{2,1,0:T(8,128)(2,1)} fusion(bf16[2,128,5120]{2,1,0:T(8,128)(2,1)} %all-gather.3.cloned.1.call-done, bf16[1,2048,5120]{2,1,0:T(8,128)(2,1)} %all-gather.5.cloned.1.call-done), kind=kOutput, calls=%fused_computation.10 | convolution fusion | flops 5369233408 | bytes 24641536 | tf_op jit(solution)/shard_map/td,shd->sth/dot_general | solution.py:149
  234.9 53.3 %shard_map.111 = (bf16[2,2048,128]{2,1,0:T(8,128)(2,1)}, bf16[2,2048,128]{2,1,0:T(8,128)(2,1)}, bf16[2,2048,128]{2,1,0:T(8,128)(2,1)}) custom-call(bf16[2,2048,128]{2,1,0:T(8,128)(2,1)} %bitcast.98, bf16[2,2048,128]{2,1,0:T(8,128)(2,1)} %bitcast.96, bf16[2,2048,128]{2,1,0:T(8,128)(2,1)} %bitcast.94, f32[2,16,1,2048]{3,2,1,0:T(1,128)} %bitcast.114, ...), custom_call_target="tpu_custom_call" | custom-call | tf_op jit(solution)/shard_map/pallas_call | solution.py:84
  288.2 2.2 pad_maximum_fusion.1
  290.4 2.1 copy.172
  292.5 10.7 %all-to-all-start.2 = ((bf16[3,2,16,128,128]{4,3,1,0,2:T(8,128)(2,1)}), bf16[3,2,16,128,128]{4,3,1,0,2:T(8,128)(2,1)S(1)}, u32[]{:S(2)}, u32[]{:S(2)}) async-start(bf16[3,2,16,128,128]{4,3,1,0,2:T(8,128)(2,1)} %copy.172), calls=%async_computation.2 | async-start | bytes 6291456 | tf_op jit(solution)/shard_map/all_to_all | solution.py:162
  303.2 2.3 copy.151
  305.5 1.3 fusion.16
  306.8 2.3 copy.152
  309.1 2.2 copy.164
  311.3 32.4 %all-to-all-done.2 = bf16[3,2,16,128,128]{4,3,1,0,2:T(8,128)(2,1)S(1)} async-done(((bf16[3,2,16,128,128]{4,3,1,0,2:T(8,128)(2,1)}), bf16[3,2,16,128,128]{4,3,1,0,2:T(8,128)(2,1)S(1)}, u32[]{:S(2)}, u32[]{:S(2)}) %all-to-all-start.2) | async-done | bytes 3145760 | tf_op jit(solution)/shard_map/all_to_all | solution.py:162
  343.7 1.6 fusion.42
  345.2 1.1 copy.161
  347.2 1.1 copy.167
  348.3 1.1 copy.159
  350.3 1.1 copy.166
  353.4 1.1 copy.165
  (50 shorter events, 14.6 us)
Async XLA Ops:
  7.2 2.7 copy-start.5
  7.2 178.7 %all-gather.5.cloned.1.call-start = ((), (), s32[]{:S(2)}) async-start(), calls=%async_computation.5 | async-start | bytes 22282240 | tf_op jit(solution)/shard_map/all_gather | solution.py:148
  7.9 3.1 copy-start.3
  17.5 10.3 %copy-start.4 = (s32[20,16,16]{0,2,1:T(8,128)S(1)}, s32[20,16,16]{0,2,1:T(8,128)}, u32[]{:S(2)}) copy-start(s32[20,16,16]{0,2,1:T(8,128)} %param.12) | copy-start | bytes 61444
  17.5 65.7 %all-to-all-start = ((bf16[16,3,2,128,128]{4,3,2,1,0:T(8,128)(2,1)}), bf16[16,3,2,128,128]{4,3,2,1,0:T(8,128)(2,1)S(1)}, u32[]{:S(2)}, u32[]{:S(2)}) async-start(bf16[16,3,2,128,128]{4,3,2,1,0:T(8,128)(2,1)} %pad_maximum_fusion), calls=%async_computation | async-start | bytes 6291456 | tf_op jit(solution)/shard_map/all_to_all | solution.py:136
  26.9 196.5 %all-gather.3.cloned.1.call-start = ((), (), s32[]{:S(2)}) async-start(), calls=%async_computation.4 | async-start | bytes 2949120 | tf_op jit(solution)/shard_map/all_gather | solution.py:140
  117.9 68.0 %copy-start = (bf16[2,2048,128]{2,1,0:T(8,128)(2,1)S(1)}, bf16[2,2048,128]{2,1,0:T(8,128)(2,1)}, u32[]{:S(2)}) copy-start(bf16[2,2048,128]{2,1,0:T(8,128)(2,1)} %shard_map.110.o_ref) | copy-start | bytes 3145732
  120.3 172.2 %all-to-all-start.1 = ((bf16[2,16,128,128]{3,2,0,1:T(8,128)(2,1)}), bf16[2,16,128,128]{3,2,0,1:T(8,128)(2,1)}, u32[]{:S(2)}, u32[]{:S(2)}) async-start(bf16[2,16,128,128]{3,2,0,1:T(8,128)(2,1)} %copy.150), calls=%async_computation.1 | async-start | bytes 2097152 | tf_op jit(solution)/shard_map/all_to_all | solution.py:146
  126.2 228.3 %reduce-scatter.4.cloned.1.call-start = ((), (), s32[]{:S(2)}) async-start(), calls=%async_computation.6 | async-start | bytes 2949120
  292.5 51.2 %all-to-all-start.2 = ((bf16[3,2,16,128,128]{4,3,1,0,2:T(8,128)(2,1)}), bf16[3,2,16,128,128]{4,3,1,0,2:T(8,128)(2,1)S(1)}, u32[]{:S(2)}, u32[]{:S(2)}) async-start(bf16[3,2,16,128,128]{4,3,1,0,2:T(8,128)(2,1)} %copy.172), calls=%async_computation.2 | async-start | bytes 6291456 | tf_op jit(solution)/shard_map/all_to_all | solution.py:162
  345.2 3.1 copy-start.2
  348.3 3.1 copy-start.1
Sparse Core Ops, SparseCore 0:
  10.5 175.3 all-gather.4
  187.5 35.8 all-gather.2
  225.9 42.9 reduce-scatter.3

commit v4 on v3

--- a/solution.py
+++ b/solution.py
@@ -137,7 +137,9 @@
     slot_query = arrived[0]
     slot_key = arrived[1]
     slot_value = arrived[2]
-    weight_full = lax.all_gather(out_weight, "dp", axis=2, tiled=True)
+    dp_count = lax.axis_size("dp")
+    weight_copies = jnp.broadcast_to(out_weight[None], (dp_count,) + out_weight.shape)
+    weight_parts = lax.all_to_all(weight_copies, "dp", split_axis=0, concat_axis=0, tiled=True)
     slot_out = attn_forward(bias, slot_query, slot_key, slot_value, score_scale)
 
     def back_layout(stacked):
@@ -147,7 +149,10 @@
 
     dy_rows = lax.all_gather(grad_out, "seq", axis=1, tiled=True)[0]
     part = jnp.einsum(
-        "td,shd->sth", dy_rows, weight_full, preferred_element_type=jnp.float32
+        "tjd,jshd->sth",
+        dy_rows.reshape(length, dp_count, out_weight.shape[2]),
+        weight_parts,
+        preferred_element_type=jnp.float32,
     ).astype(jnp.bfloat16)
     grad_attn = part
     weight_total = jnp.einsum("sth,td->shd", slot_out, dy_rows, preferred_element_type=jnp.float32)
@@ -155,11 +160,21 @@
     weight_grad = lax.psum_scatter(
         (weight_total * grad_scale).astype(jnp.bfloat16), "dp", scatter_dimension=2, tiled=True
     ).astype(jnp.float32)
-    slot_qgrad, slot_kgrad, slot_vgrad = attn_backward(
-        bias, slot_query, slot_key, slot_value, slot_out, grad_attn, score_scale
-    )
-    back_stack = jnp.stack([back_layout(slot_qgrad), back_layout(slot_kgrad), back_layout(slot_vgrad)])
-    grads_back = lax.all_to_all(back_stack, "seq", split_axis=2, concat_axis=1, tiled=True)
+    grads_parts = []
+    for slot_number in range(most_slots):
+        one = slice(slot_number, slot_number + 1)
+        slot_grads = attn_backward(
+            bias[one],
+            slot_query[one],
+            slot_key[one],
+            slot_value[one],
+            slot_out[one],
+            grad_attn[one],
+            score_scale,
+        )
+        one_stack = jnp.stack([g.reshape(1, seq_count, token_count, head_dim) for g in slot_grads])
+        grads_parts.append(lax.all_to_all(one_stack, "seq", split_axis=2, concat_axis=1, tiled=True))
+    grads_back = jnp.stack(grads_parts, axis=2).reshape(3, seq_count * most_slots, 1, token_count, head_dim)
     all_back = (out_back, grads_back[0], grads_back[1], grads_back[2])
     attn_out = heads_to_tokens(all_back[0], select, token_count, head_count, head_dim)
     query_grad = heads_to_tokens(all_back[1], select, token_count, head_count, head_dim)

time: 367 us -> 390 us (1.063)
  local copies, waits for them, and re-layouts: 40.5 us -> 72.5 us
  waiting for transfers between devices: 164 us -> 140 us
  starting transfers between devices: 26.3 us -> 32.1 us
  other arithmetic: 5.42 us -> 10.2 us
    all_gather x0 -> x1, local copies, waits for them, and re-layouts: none -> 28.5 us  [on_device(): dy_rows = lax.all_gather(grad_out, 'seq', axis=1, tiled=True)[0]]
    all_to_all x1 -> x3, waiting for transfers between devices: 32.4 us -> 14.6 us  [the longest x2 14.6 us: on_device(): lax.all_to_all(one_stack, 'seq', split_axis=2, concat_axis=1, tiled=True)]
    all_gather x1 -> x0, waiting for transfers between devices: 15.8 us -> none  [on_device(): weight_full = lax.all_gather(out_weight, 'dp', axis=2, tiled=True)]
    all_gather x1, waiting for transfers between devices: 59.5 us -> 73.4 us  [on_device(): dy_rows = lax.all_gather(grad_out, 'seq', axis=1, tiled=True)[0]]
    all_to_all x1 -> x3, starting transfers between devices: 10.7 us -> 18.9 us  [the longest x2 14.5 us: on_device(): lax.all_to_all(one_stack, 'seq', split_axis=2, concat_axis=1, tiled=True)]
    another operation x1 -> x3, other arithmetic: 2.2 us -> 6.96 us  [the longest x2 5.35 us: on_device(): jnp.stack([g.reshape(1, seq_count, token_count, head_dim) for g in slot_g...]
    pallas_call x1 -> x2, Pallas kernels: 53.3 us -> 55.2 us  [attn_backward(): pl.pallas_call(functools.partial(_bwd_kernel, nb=nb, scale=scale), grid=(...]
    unnamed x23 -> x29, local copies, waits for them, and re-layouts: 18.3 us -> 18.4 us
  transfers between devices with their start and end apart: 6 -> 7, of which waited for: 4 -> 3; matrix products, arithmetic and copies ran while one was open for 20% -> 29% of each run, Pallas kernels for 23% -> 22%
where the time goes in v4:
time: 390 us; the launch traced here: 387 us
  waiting for transfers between devices  140 us (36%)
  Pallas kernels  85.4 us (22%)
  local copies, waits for them, and re-layouts  72.5 us (19%)
  matrix products  32.8 us (8%)
  starting transfers between devices  32.1 us (8%)
  between operations  14.3 us (4%)
  other arithmetic  10.2 us (3%)
    all_gather x1, waiting for transfers between devices, on_device(): dy_rows = lax.all_gather(grad_out, 'seq', axis=1, tiled=True)[0]  73.4 us
    pallas_call x2, Pallas kernels, attn_backward(): pl.pallas_call(functools.partial(_bwd_kernel, nb=nb, scale=scale), grid=(...  55.2 us
    all_to_all x1, waiting for transfers between devices, on_device(): lax.all_to_all(stacked, 'seq', split_axis=0, concat_axis=3, tiled=True)[0]  51.4 us
    pallas_call x1, Pallas kernels, attn_forward(): pl.pallas_call(functools.partial(_fwd_kernel, scale=scale), grid=(slots,...  30.3 us
    all_gather x1, local copies, waits for them, and re-layouts, on_device(): dy_rows = lax.all_gather(grad_out, 'seq', axis=1, tiled=True)[0]  28.5 us
    unnamed x29, local copies, waits for them, and re-layouts  18.4 us
    all_to_all x2, waiting for transfers between devices, on_device(): lax.all_to_all(one_stack, 'seq', split_axis=2, concat_axis=1, tiled=True)  14.6 us
    all_to_all x2, starting transfers between devices, on_device(): lax.all_to_all(one_stack, 'seq', split_axis=2, concat_axis=1, tiled=True)  14.5 us
  transfers between devices with their start and end apart: 7, of which 3 were waited for; matrix products, arithmetic and copies ran while one was open for 29% of the time, Pallas kernels for 22%

profile of v4, /device:TPU:1, one launch (start us, length us, event | category | flops | bytes accessed | tf_op | source)
XLA Modules:
  0.0 387.4 jit_solution(14780649945072487729)
XLA Ops:
  7.9 1.4 copy.159
  14.5 2.0 pad_maximum_fusion
  16.5 9.4 %all-to-all-start = ((bf16[16,3,2,128,128]{4,3,2,1,0:T(8,128)(2,1)}), bf16[16,3,2,128,128]{4,3,2,1,0:T(8,128)(2,1)S(1)}, u32[]{:S(2)}, u32[]{:S(2)}) async-start(bf16[16,3,2,128,128]{4,3,2,1,0:T(8,128)(2,1)} %pad_maximum_fusion), calls=%async_computation | async-start | bytes 6291456 | tf_op jit(solution)/shard_map/all_to_all | solution.py:136
  26.1 1.3 fusion.17
  27.5 51.4 %all-to-all-done = bf16[16,3,2,128,128]{4,3,2,1,0:T(8,128)(2,1)S(1)} async-done(((bf16[16,3,2,128,128]{4,3,2,1,0:T(8,128)(2,1)}), bf16[16,3,2,128,128]{4,3,2,1,0:T(8,128)(2,1)S(1)}, u32[]{:S(2)}, u32[]{:S(2)}) %all-to-all-start) | async-done | bytes 3145760 | tf_op jit(solution)/shard_map/all_to_all | solution.py:136
  78.8 1.8 broadcast_in_dim.34
  80.6 4.4 %all-to-all-start.2 = ((bf16[8,2,128,640]{3,2,1,0:T(8,128)(2,1)}), bf16[8,2,128,640]{3,2,1,0:T(8,128)(2,1)}, u32[]{:S(2)}, u32[]{:S(2)}) async-start(bf16[8,2,128,640]{3,2,1,0:T(8,128)(2,1)} %broadcast_in_dim.34), calls=%async_computation.2 | async-start | bytes 5242880 | tf_op jit(solution)/shard_map/all_to_all | solution.py:142
  85.3 1.1 copy.164
  87.5 1.2 copy.166
  89.5 30.3 %shard_map.110 = bf16[2,2048,128]{2,1,0:T(8,128)(2,1)} custom-call(bf16[2,2048,128]{2,1,0:T(8,128)(2,1)} %bitcast.126, bf16[2,2048,128]{2,1,0:T(8,128)(2,1)} %bitcast.127, bf16[2,2048,128]{2,1,0:T(8,128)(2,1)} %bitcast.128, f32[2,16,1,2048]{3,2,1,0:T(1,128)} %bitcast.151), custom_call_target="tpu_custom_call" | custom-call | tf_op jit(solution)/shard_map/pallas_call | solution.py:66
  119.7 2.3 copy.169
  122.0 1.7 fusion.38
  124.9 73.4 %all-gather.2.cloned.1.call-done = bf16[1,2048,5120]{2,1,0:T(8,128)(2,1)} async-done(((bf16[1,128,5120]{2,1,0:T(8,128)(2,1)}), bf16[1,2048,5120]{2,1,0:T(8,128)(2,1)}) %all-gather.2.cloned.1.call-update) | async-done | bytes 20971536 | tf_op jit(solution)/shard_map/all_gather | solution.py:150
  198.3 14.0 %fusion.5 = bf16[2,128,5120]{2,1,0:T(8,128)(2,1)} fusion(bf16[2,2048,128]{2,1,0:T(8,128)(2,1)S(1)} %copy-done.1, bf16[1,2048,5120]{2,1,0:T(8,128)(2,1)} %all-gather.2.cloned.1.call-done), kind=kOutput, calls=%fused_computation.3 | convolution fusion | flops 5371330560 | bytes 24641536 | tf_op jit(solution)/shard_map/sth,td->shd/dot_general | solution.py:158
  212.4 5.9 %copy.200 = bf16[2,128,5120]{1,0,2:T(2,128)(2,1)S(1)} copy(bf16[2,128,5120]{2,1,0:T(8,128)(2,1)} %fusion.5) | data formatting | bytes 5242880
  218.2 1.9 copy.204
  220.1 28.5 %copy.172 = bf16[1,2048,5120]{1,2,0:T(8,128)(2,1)} copy(bf16[1,2048,5120]{2,1,0:T(8,128)(2,1)} %all-gather.2.cloned.1.call-done) | data formatting | bytes 41943040 | tf_op jit(solution)/shard_map/all_gather | solution.py:150
  248.6 3.7 all-to-all-start.1
  252.3 13.2 %fusion.9 = bf16[2,2048,128]{2,1,0:T(8,128)(2,1)S(1)} fusion(bf16[8,2,128,640]{3,2,1,0:T(8,128)(2,1)} %all-to-all-done.2, bf16[2048,8,640,1]{0,2,3,1:T(8,128)(2,1)} %bitcast.120), kind=kOutput, calls=%fused_computation.12 | convolution fusion | flops 5369233408 | bytes 24641536 | tf_op jit(solution)/shard_map/tjd,jshd->sth/dot_general | solution.py:151
  267.3 27.6 %shard_map.112 = (bf16[1,2048,128]{2,1,0:T(8,128)(2,1)}, bf16[1,2048,128]{2,1,0:T(8,128)(2,1)}, bf16[1,2048,128]{2,1,0:T(8,128)(2,1)}) custom-call(bf16[1,2048,128]{2,1,0:T(8,128)(2,1)} %bitcast.149, bf16[1,2048,128]{2,1,0:T(8,128)(2,1)} %bitcast.148, bf16[1,2048,128]{2,1,0:T(8,128)(2,1)} %bitcast.147, f32[1,16,1,2048]{3,2,1,0:T(1,128)} %bitcast.159, ...), custom_call_target="tpu_custom_call" | custom-call | tf_op jit(solution)/shard_map/pallas_call | solution.py:84
  294.9 2.7 pad_maximum_fusion.2
  298.6 7.3 %all-to-all-start.4 = ((bf16[3,1,16,128,128]{4,3,1,0,2:T(8,128)(2,1)}), bf16[3,1,16,128,128]{4,3,1,0,2:T(8,128)(2,1)S(1)}, u32[]{:S(2)}, u32[]{:S(2)}) async-start(bf16[3,1,16,128,128]{4,3,1,0,2:T(8,128)(2,1)} %pad_maximum_fusion.2), calls=%async_computation.4 | async-start | bytes 3145728 | tf_op jit(solution)/shard_map/all_to_all | solution.py:176
  306.6 27.6 %shard_map.111 = (bf16[1,2048,128]{2,1,0:T(8,128)(2,1)}, bf16[1,2048,128]{2,1,0:T(8,128)(2,1)}, bf16[1,2048,128]{2,1,0:T(8,128)(2,1)}) custom-call(bf16[1,2048,128]{2,1,0:T(8,128)(2,1)} %bitcast.146, bf16[1,2048,128]{2,1,0:T(8,128)(2,1)} %bitcast.145, bf16[1,2048,128]{2,1,0:T(8,128)(2,1)} %bitcast.144, f32[1,16,1,2048]{3,2,1,0:T(1,128)} %bitcast.158, ...), custom_call_target="tpu_custom_call" | custom-call | tf_op jit(solution)/shard_map/pallas_call | solution.py:84
  334.2 2.7 pad_maximum_fusion.1
  336.8 7.2 %all-to-all-start.3 = ((bf16[3,1,16,128,128]{4,3,0,1,2:T(8,128)(2,1)}), bf16[3,1,16,128,128]{4,3,0,1,2:T(8,128)(2,1)S(1)}, u32[]{:S(2)}, u32[]{:S(2)}) async-start(bf16[3,1,16,128,128]{4,3,0,1,2:T(8,128)(2,1)} %pad_maximum_fusion.1), calls=%async_computation.3 | async-start | bytes 3145728 | tf_op jit(solution)/shard_map/all_to_all | solution.py:176
  344.1 2.3 copy.170
  346.4 1.3 fusion.10
  347.7 2.3 copy.171
  350.0 2.2 copy.188
  352.2 14.6 %all-to-all-done.3 = bf16[3,1,16,128,128]{4,3,0,1,2:T(8,128)(2,1)S(1)} async-done(((bf16[3,1,16,128,128]{4,3,0,1,2:T(8,128)(2,1)}), bf16[3,1,16,128,128]{4,3,0,1,2:T(8,128)(2,1)S(1)}, u32[]{:S(2)}, u32[]{:S(2)}) %all-to-all-start.3) | async-done | bytes 1572896 | tf_op jit(solution)/shard_map/all_to_all | solution.py:176
  366.8 1.6 pad_maximum_fusion.3
  376.6 1.1 copy.191
  (66 shorter events, 23.9 us)
Async XLA Ops:
  7.2 2.6 copy-start.8
  7.2 191.1 %all-gather.2.cloned.1.call-start = ((), (), s32[]{:S(2)}) async-start(), calls=%async_computation.6 | async-start | bytes 22282240 | tf_op jit(solution)/shard_map/all_gather | solution.py:150
  9.3 1.6 copy-start.5
  11.7 1.1 copy-start.6
  16.5 62.3 %copy-start.7 = (bf16[2,128,640]{2,1,0:T(8,128)(2,1)S(1)}, bf16[2,128,640]{2,1,0:T(8,128)(2,1)}, u32[]{:S(2)}) copy-start(bf16[2,128,640]{2,1,0:T(8,128)(2,1)} %param.11) | copy-start | bytes 983044
  16.5 62.3 %all-to-all-start = ((bf16[16,3,2,128,128]{4,3,2,1,0:T(8,128)(2,1)}), bf16[16,3,2,128,128]{4,3,2,1,0:T(8,128)(2,1)S(1)}, u32[]{:S(2)}, u32[]{:S(2)}) async-start(bf16[16,3,2,128,128]{4,3,2,1,0:T(8,128)(2,1)} %pad_maximum_fusion), calls=%async_computation | async-start | bytes 6291456 | tf_op jit(solution)/shard_map/all_to_all | solution.py:136
  80.6 168.0 %all-to-all-start.2 = ((bf16[8,2,128,640]{3,2,1,0:T(8,128)(2,1)}), bf16[8,2,128,640]{3,2,1,0:T(8,128)(2,1)}, u32[]{:S(2)}, u32[]{:S(2)}) async-start(bf16[8,2,128,640]{3,2,1,0:T(8,128)(2,1)} %broadcast_in_dim.34), calls=%async_computation.2 | async-start | bytes 5242880 | tf_op jit(solution)/shard_map/all_to_all | solution.py:142
  85.0 292.7 %reduce-scatter.4.cloned.1.call-start = ((), (), s32[]{:S(2)}) async-start(), calls=%async_computation.7 | async-start | bytes 2949120
  122.0 1.9 copy-start
  123.9 74.4 %copy-start.1 = (bf16[2,2048,128]{2,1,0:T(8,128)(2,1)S(1)}, bf16[2,2048,128]{2,1,0:T(8,128)(2,1)}, u32[]{:S(2)}) copy-start(bf16[2,2048,128]{2,1,0:T(8,128)(2,1)} %shard_map.110) | copy-start | bytes 3145732
  248.6 49.0 %all-to-all-start.1 = ((bf16[2,16,128,128]{3,2,0,1:T(8,128)(2,1)}), bf16[2,16,128,128]{3,2,0,1:T(8,128)(2,1)S(1)}, u32[]{:S(2)}, u32[]{:S(2)}) async-start(bf16[2,16,128,128]{3,2,0,1:T(8,128)(2,1)} %copy.169), calls=%async_computation.1 | async-start | bytes 2097152 | tf_op jit(solution)/shard_map/all_to_all | solution.py:148
  297.6 1.0 copy-start.2
  298.6 38.3 %all-to-all-start.4 = ((bf16[3,1,16,128,128]{4,3,1,0,2:T(8,128)(2,1)}), bf16[3,1,16,128,128]{4,3,1,0,2:T(8,128)(2,1)S(1)}, u32[]{:S(2)}, u32[]{:S(2)}) async-start(bf16[3,1,16,128,128]{4,3,1,0,2:T(8,128)(2,1)} %pad_maximum_fusion.2), calls=%async_computation.4 | async-start | bytes 3145728 | tf_op jit(solution)/shard_map/all_to_all | solution.py:176
  336.8 30.0 %all-to-all-start.3 = ((bf16[3,1,16,128,128]{4,3,0,1,2:T(8,128)(2,1)}), bf16[3,1,16,128,128]{4,3,0,1,2:T(8,128)(2,1)S(1)}, u32[]{:S(2)}, u32[]{:S(2)}) async-start(bf16[3,1,16,128,128]{4,3,0,1,2:T(8,128)(2,1)} %pad_maximum_fusion.1), calls=%async_computation.3 | async-start | bytes 3145728 | tf_op jit(solution)/shard_map/all_to_all | solution.py:176
  369.5 2.0 copy-start.4
  372.6 2.0 copy-start.3
Sparse Core Ops, SparseCore 0:
  10.5 187.7 all-gather.1
  220.2 39.1 reduce-scatter.3

commit v5 on v4

--- a/solution.py
+++ b/solution.py
@@ -147,15 +147,34 @@
 
     out_back = lax.all_to_all(back_layout(slot_out), "seq", split_axis=1, concat_axis=0, tiled=True)
 
-    dy_rows = lax.all_gather(grad_out, "seq", axis=1, tiled=True)[0]
-    part = jnp.einsum(
-        "tjd,jshd->sth",
-        dy_rows.reshape(length, dp_count, out_weight.shape[2]),
-        weight_parts,
-        preferred_element_type=jnp.float32,
+    weight_full = jnp.transpose(weight_parts, (1, 2, 0, 3)).reshape(
+        most_slots, head_dim, dp_count * out_weight.shape[2]
+    )
+    feature_count = grad_out.shape[2]
+    sc_features = feature_count - feature_count // 5 // 128 * 128
+    dy_first = lax.all_gather(grad_out[0, :, :sc_features], "seq", axis=0, tiled=True)
+    dy_copies = jnp.broadcast_to(
+        grad_out[:, :, sc_features:], (seq_count, token_count, feature_count - sc_features)
+    )
+    dy_second = lax.all_to_all(dy_copies, "seq", split_axis=0, concat_axis=0, tiled=True).reshape(
+        length, feature_count - sc_features
+    )
+    part = (
+        jnp.einsum(
+            "td,shd->sth", dy_first, weight_full[:, :, :sc_features], preferred_element_type=jnp.float32
+        )
+        + jnp.einsum(
+            "td,shd->sth", dy_second, weight_full[:, :, sc_features:], preferred_element_type=jnp.float32
+        )
     ).astype(jnp.bfloat16)
     grad_attn = part
-    weight_total = jnp.einsum("sth,td->shd", slot_out, dy_rows, preferred_element_type=jnp.float32)
+    weight_total = jnp.concatenate(
+        [
+            jnp.einsum("sth,td->shd", slot_out, dy_first, preferred_element_type=jnp.float32),
+            jnp.einsum("sth,td->shd", slot_out, dy_second, preferred_element_type=jnp.float32),
+        ],
+        axis=2,
+    )
     grad_attn, weight_total = (grad_attn, weight_total)
     weight_grad = lax.psum_scatter(
         (weight_total * grad_scale).astype(jnp.bfloat16), "dp", scatter_dimension=2, tiled=True

time: 390 us -> 377 us (0.967)
  waiting for transfers between devices: 140 us -> 129 us
  starting transfers between devices: 32.1 us -> 40.7 us
  local copies, waits for them, and re-layouts: 72.5 us -> 65.3 us
  matrix products: 32.8 us -> 28.4 us
    all_gather x1, waiting for transfers between devices: 73.4 us -> 0.02 us  [on_device(): lax.all_gather(grad_out[0, :, :sc_features], 'seq', axis=0, tiled=True)]
    all_gather x1 -> x0, local copies, waits for them, and re-layouts: 28.5 us -> none  [on_device(): dy_rows = lax.all_gather(grad_out, 'seq', axis=1, tiled=True)[0]]
    all_to_all x1, waiting for transfers between devices: 0.01 us -> 23.4 us  [on_device(): lax.all_to_all(weight_copies, 'dp', split_axis=0, concat_axis=0, tiled=True)]
    all_to_all x1, waiting for transfers between devices: 51.4 us -> 72.6 us  [on_device(): lax.all_to_all(stacked, 'seq', split_axis=0, concat_axis=3, tiled=True)[0]]
    all_to_all x0 -> x1, waiting for transfers between devices: none -> 18.7 us  [on_device(): lax.all_to_all(dy_copies, 'seq', split_axis=0, concat_axis=0, tiled=True)]
    unnamed x29 -> x35, local copies, waits for them, and re-layouts: 18.4 us -> 24.7 us
    all_to_all x0 -> x1, starting transfers between devices: none -> 5.34 us  [on_device(): lax.all_to_all(dy_copies, 'seq', split_axis=0, concat_axis=0, tiled=True)]
    dot_general x2 -> x4, matrix products: 27.2 us -> 23.8 us  [the longest x1 8.59 us: on_device(): jnp.einsum('td,shd->sth', dy_first, weight_full[:, :, :sc_features], pref...]
  transfers between devices with their start and end apart: 7 -> 8, of which waited for: 3 -> 4; matrix products, arithmetic and copies ran while one was open for 29% -> 26% of each run, Pallas kernels for 22% -> 23%
where the time goes in v5:
time: 377 us; the launch traced here: 376 us
  waiting for transfers between devices  129 us (34%)
  Pallas kernels  85.5 us (23%)
  local copies, waits for them, and re-layouts  65.3 us (17%)
  starting transfers between devices  40.7 us (11%)
  matrix products  28.4 us (8%)
  between operations  14.3 us (4%)
  other arithmetic  12.1 us (3%)
    all_to_all x1, waiting for transfers between devices, on_device(): lax.all_to_all(stacked, 'seq', split_axis=0, concat_axis=3, tiled=True)[0]  72.6 us
    pallas_call x2, Pallas kernels, attn_backward(): pl.pallas_call(functools.partial(_bwd_kernel, nb=nb, scale=scale), grid=(...  55.3 us
    pallas_call x1, Pallas kernels, attn_forward(): pl.pallas_call(functools.partial(_fwd_kernel, scale=scale), grid=(slots,...  30.2 us
    unnamed x35, local copies, waits for them, and re-layouts  24.7 us
    all_to_all x1, waiting for transfers between devices, on_device(): lax.all_to_all(weight_copies, 'dp', split_axis=0, concat_axis=0, tiled=True)  23.4 us
    all_to_all x1, waiting for transfers between devices, on_device(): lax.all_to_all(dy_copies, 'seq', split_axis=0, concat_axis=0, tiled=True)  18.7 us
    all_to_all x2, waiting for transfers between devices, on_device(): lax.all_to_all(one_stack, 'seq', split_axis=2, concat_axis=1, tiled=True)  14.6 us
    all_to_all x2, starting transfers between devices, on_device(): lax.all_to_all(one_stack, 'seq', split_axis=2, concat_axis=1, tiled=True)  14.5 us
  transfers between devices with their start and end apart: 8, of which 4 were waited for; matrix products, arithmetic and copies ran while one was open for 26% of the time, Pallas kernels for 23%

profile of v5, /device:TPU:1, one launch (start us, length us, event | category | flops | bytes accessed | tf_op | source)
XLA Modules:
  0.0 375.7 jit_solution(8227084874153969957)
XLA Ops:
  7.2 2.3 slice.124
  11.4 6.1 %all-to-all-start.2 = ((bf16[8,2,128,640]{3,2,1,0:T(8,128)(2,1)}), bf16[8,2,128,640]{3,2,1,0:T(8,128)(2,1)S(1)}, u32[]{:S(2)}, u32[]{:S(2)}) async-start(bf16[8,2,128,640]{3,2,1,0:T(8,128)(2,1)} %broadcast_in_dim.41), calls=%async_computation.2 | async-start | bytes 5242880 | tf_op jit(solution)/shard_map/all_to_all | solution.py:142
  22.2 2.2 copy.160
  27.9 2.2 copy.162
  33.1 2.0 pad_maximum_fusion
  35.1 23.4 %all-to-all-done.2 = bf16[8,2,128,640]{3,2,1,0:T(8,128)(2,1)S(1)} async-done(((bf16[8,2,128,640]{3,2,1,0:T(8,128)(2,1)}), bf16[8,2,128,640]{3,2,1,0:T(8,128)(2,1)S(1)}, u32[]{:S(2)}, u32[]{:S(2)}) %all-to-all-start.2) | async-done | bytes 2621472 | tf_op jit(solution)/shard_map/all_to_all | solution.py:142
  60.1 9.2 %all-to-all-start = ((bf16[16,3,2,128,128]{4,3,2,1,0:T(8,128)(2,1)}), bf16[16,3,2,128,128]{4,3,2,1,0:T(8,128)(2,1)S(1)}, u32[]{:S(2)}, u32[]{:S(2)}) async-start(bf16[16,3,2,128,128]{4,3,2,1,0:T(8,128)(2,1)} %pad_maximum_fusion), calls=%async_computation | async-start | bytes 6291456 | tf_op jit(solution)/shard_map/all_to_all | solution.py:136
  70.3 72.6 %all-to-all-done = bf16[16,3,2,128,128]{4,3,2,1,0:T(8,128)(2,1)S(1)} async-done(((bf16[16,3,2,128,128]{4,3,2,1,0:T(8,128)(2,1)}), bf16[16,3,2,128,128]{4,3,2,1,0:T(8,128)(2,1)S(1)}, u32[]{:S(2)}, u32[]{:S(2)}) %all-to-all-start) | async-done | bytes 3145760 | tf_op jit(solution)/shard_map/all_to_all | solution.py:136
  142.9 2.6 broadcast_in_dim.43
  145.5 5.3 %all-to-all-start.3 = ((bf16[16,128,1024]{2,1,0:T(8,128)(2,1)}), bf16[16,128,1024]{2,1,0:T(8,128)(2,1)}, u32[]{:S(2)}, u32[]{:S(2)}) async-start(bf16[16,128,1024]{2,1,0:T(8,128)(2,1)} %broadcast_in_dim.43), calls=%async_computation.3 | async-start | bytes 8388608 | tf_op jit(solution)/shard_map/all_to_all | solution.py:159
  151.4 3.8 %copy.204 = bf16[8,2,16,8,640]{4,3,0,2,1:T(8,128)(2,1)} copy(bf16[8,2,16,8,640]{4,3,2,1,0:T(8,128)(2,1)} %bitcast.118) | data formatting | bytes 5242880 | tf_op jit(solution)/shard_map/reshape | solution.py:150
  159.6 30.2 %shard_map.110 = bf16[2,2048,128]{2,1,0:T(8,128)(2,1)} custom-call(bf16[2,2048,128]{2,1,0:T(8,128)(2,1)} %bitcast.124, bf16[2,2048,128]{2,1,0:T(8,128)(2,1)} %bitcast.123, bf16[2,2048,128]{2,1,0:T(8,128)(2,1)} %bitcast.122, f32[2,16,1,2048]{3,2,1,0:T(1,128)} %bitcast.148), custom_call_target="tpu_custom_call" | custom-call | tf_op jit(solution)/shard_map/pallas_call | solution.py:66
  189.8 2.3 copy.172
  195.1 18.7 %all-to-all-done.3 = bf16[16,128,1024]{2,1,0:T(8,128)(2,1)} async-done(((bf16[16,128,1024]{2,1,0:T(8,128)(2,1)}), bf16[16,128,1024]{2,1,0:T(8,128)(2,1)}, u32[]{:S(2)}, u32[]{:S(2)}) %all-to-all-start.3) | async-done | bytes 4194336 | tf_op jit(solution)/shard_map/all_to_all | solution.py:159
  213.8 5.4 %all-to-all-start.1 = ((bf16[2,16,128,128]{3,2,0,1:T(8,128)(2,1)}), bf16[2,16,128,128]{3,2,0,1:T(8,128)(2,1)}, u32[]{:S(2)}, u32[]{:S(2)}) async-start(bf16[2,16,128,128]{3,2,0,1:T(8,128)(2,1)} %copy.172), calls=%async_computation.1 | async-start | bytes 2097152 | tf_op jit(solution)/shard_map/all_to_all | solution.py:148
  219.4 3.5 fusion.42
  222.9 8.1 %fusion = f32[2,128,4096]{2,1,0:T(8,128)S(1)} fusion(bf16[2,2048,128]{2,1,0:T(8,128)(2,1)S(1)} %copy-done.1, bf16[1,2048,4096]{2,1,0:T(8,128)(2,1)} %all-gather.3.cloned.1.call-done), kind=kOutput, calls=%fused_computation | convolution fusion | flops 4294967296 | bytes 22020096 | tf_op jit(solution)/shard_map/sth,td->shd/dot_general | solution.py:173
  231.1 1.9 fusion.4
  233.0 5.9 %copy.202 = bf16[2,128,5120]{1,0,2:T(2,128)(2,1)S(1)} copy(bf16[2,128,5120]{2,1,0:T(8,128)(2,1)} %fusion.4) | data formatting | bytes 5242880
  238.9 1.9 copy.207
  242.5 8.6 %fusion.2 = f32[2,128,2048]{1,2,0:T(8,128)S(1)} fusion(bf16[1,2048,4096]{2,1,0:T(8,128)(2,1)} %all-gather.3.cloned.1.call-done, bf16[2,128,5120]{2,1,0:T(8,128)(2,1)S(1)} %bitcast.132), kind=kOutput, calls=%fused_computation.2 | convolution fusion | flops 4294967296 | bytes 20971520 | tf_op jit(solution)/shard_map/td,shd->sth/dot_general | solution.py:163
  251.1 3.6 fusion.6
  256.5 27.6 %shard_map.111 = (bf16[1,2048,128]{2,1,0:T(8,128)(2,1)}, bf16[1,2048,128]{2,1,0:T(8,128)(2,1)}, bf16[1,2048,128]{2,1,0:T(8,128)(2,1)}) custom-call(bf16[1,2048,128]{2,1,0:T(8,128)(2,1)} %bitcast.146, bf16[1,2048,128]{2,1,0:T(8,128)(2,1)} %bitcast.145, bf16[1,2048,128]{2,1,0:T(8,128)(2,1)} %bitcast.144, f32[1,16,1,2048]{3,2,1,0:T(1,128)} %bitcast.156, ...), custom_call_target="tpu_custom_call" | custom-call | tf_op jit(solution)/shard_map/pallas_call | solution.py:84
  284.1 2.7 pad_maximum_fusion.1
  286.9 7.3 %all-to-all-start.4 = ((bf16[3,1,16,128,128]{4,3,0,1,2:T(8,128)(2,1)}), bf16[3,1,16,128,128]{4,3,0,1,2:T(8,128)(2,1)S(1)}, u32[]{:S(2)}, u32[]{:S(2)}) async-start(bf16[3,1,16,128,128]{4,3,0,1,2:T(8,128)(2,1)} %pad_maximum_fusion.1), calls=%async_computation.4 | async-start | bytes 3145728 | tf_op jit(solution)/shard_map/all_to_all | solution.py:195
  294.9 27.6 %shard_map.112 = (bf16[1,2048,128]{2,1,0:T(8,128)(2,1)}, bf16[1,2048,128]{2,1,0:T(8,128)(2,1)}, bf16[1,2048,128]{2,1,0:T(8,128)(2,1)}) custom-call(bf16[1,2048,128]{2,1,0:T(8,128)(2,1)} %bitcast.143, bf16[1,2048,128]{2,1,0:T(8,128)(2,1)} %bitcast.142, bf16[1,2048,128]{2,1,0:T(8,128)(2,1)} %bitcast.141, f32[1,16,1,2048]{3,2,1,0:T(1,128)} %bitcast.155, ...), custom_call_target="tpu_custom_call" | custom-call | tf_op jit(solution)/shard_map/pallas_call | solution.py:84
  322.5 2.7 pad_maximum_fusion.2
  325.2 7.2 %all-to-all-start.5 = ((bf16[3,1,16,128,128]{4,3,1,0,2:T(8,128)(2,1)}), bf16[3,1,16,128,128]{4,3,1,0,2:T(8,128)(2,1)S(1)}, u32[]{:S(2)}, u32[]{:S(2)}) async-start(bf16[3,1,16,128,128]{4,3,1,0,2:T(8,128)(2,1)} %pad_maximum_fusion.2), calls=%async_computation.5 | async-start | bytes 3145728 | tf_op jit(solution)/shard_map/all_to_all | solution.py:195
  332.4 2.3 copy.173
  336.0 2.3 copy.174
  338.3 2.2 copy.192
  340.5 14.6 %all-to-all-done.5 = bf16[3,1,16,128,128]{4,3,1,0,2:T(8,128)(2,1)S(1)} async-done(((bf16[3,1,16,128,128]{4,3,1,0,2:T(8,128)(2,1)}), bf16[3,1,16,128,128]{4,3,1,0,2:T(8,128)(2,1)S(1)}, u32[]{:S(2)}, u32[]{:S(2)}) %all-to-all-start.5) | async-done | bytes 1572896 | tf_op jit(solution)/shard_map/all_to_all | solution.py:195
  (80 shorter events, 43.2 us)
Async XLA Ops:
  7.2 2.4 copy-start.9
  7.2 215.8 %all-gather.3.cloned.1.call-start = ((), (), s32[]{:S(2)}) async-start(), calls=%async_computation.7 | async-start | bytes 17825792 | tf_op jit(solution)/shard_map/all_gather | solution.py:155
  11.4 6.1 %copy-start.8 = (bf16[1,128,2560]{2,1,0:T(8,128)(2,1)S(1)}, bf16[1,128,2560]{2,1,0:T(8,128)(2,1)}, u32[]{:S(2)}) copy-start(bf16[1,128,2560]{2,1,0:T(8,128)(2,1)} %param.7) | copy-start | bytes 1966084
  11.4 47.1 %all-to-all-start.2 = ((bf16[8,2,128,640]{3,2,1,0:T(8,128)(2,1)}), bf16[8,2,128,640]{3,2,1,0:T(8,128)(2,1)S(1)}, u32[]{:S(2)}, u32[]{:S(2)}) async-start(bf16[8,2,128,640]{3,2,1,0:T(8,128)(2,1)} %broadcast_in_dim.41), calls=%async_computation.2 | async-start | bytes 5242880 | tf_op jit(solution)/shard_map/all_to_all | solution.py:142
  17.5 2.6 copy-start.11
  31.6 1.2 copy-start.4
  31.6 1.5 copy-start.6
  58.5 1.6 copy-start.2
  60.1 82.8 %all-to-all-start = ((bf16[16,3,2,128,128]{4,3,2,1,0:T(8,128)(2,1)}), bf16[16,3,2,128,128]{4,3,2,1,0:T(8,128)(2,1)S(1)}, u32[]{:S(2)}, u32[]{:S(2)}) async-start(bf16[16,3,2,128,128]{4,3,2,1,0:T(8,128)(2,1)} %pad_maximum_fusion), calls=%async_computation | async-start | bytes 6291456 | tf_op jit(solution)/shard_map/all_to_all | solution.py:136
  145.5 5.5 %copy-start.10 = (s32[20,16,16]{0,2,1:T(8,128)S(1)}, s32[20,16,16]{0,2,1:T(8,128)}, u32[]{:S(2)}) copy-start(s32[20,16,16]{0,2,1:T(8,128)} %param.12) | copy-start | bytes 61444
  145.5 68.3 %all-to-all-start.3 = ((bf16[16,128,1024]{2,1,0:T(8,128)(2,1)}), bf16[16,128,1024]{2,1,0:T(8,128)(2,1)}, u32[]{:S(2)}, u32[]{:S(2)}) async-start(bf16[16,128,1024]{2,1,0:T(8,128)(2,1)} %broadcast_in_dim.43), calls=%async_computation.3 | async-start | bytes 8388608 | tf_op jit(solution)/shard_map/all_to_all | solution.py:159
  192.1 1.9 copy-start
  194.1 25.4 %copy-start.1 = (bf16[2,2048,128]{2,1,0:T(8,128)(2,1)S(1)}, bf16[2,2048,128]{2,1,0:T(8,128)(2,1)}, u32[]{:S(2)}) copy-start(bf16[2,2048,128]{2,1,0:T(8,128)(2,1)} %shard_map.110) | copy-start | bytes 3145732
  213.8 73.1 %all-to-all-start.1 = ((bf16[2,16,128,128]{3,2,0,1:T(8,128)(2,1)}), bf16[2,16,128,128]{3,2,0,1:T(8,128)(2,1)}, u32[]{:S(2)}, u32[]{:S(2)}) async-start(bf16[2,16,128,128]{3,2,0,1:T(8,128)(2,1)} %copy.172), calls=%async_computation.1 | async-start | bytes 2097152 | tf_op jit(solution)/shard_map/all_to_all | solution.py:148
  219.2 146.8 %reduce-scatter.4.cloned.1.call-start = ((), (), s32[]{:S(2)}) async-start(), calls=%async_computation.8 | async-start | bytes 2949120
  240.7 1.7 copy-start.7
  286.9 38.3 %all-to-all-start.4 = ((bf16[3,1,16,128,128]{4,3,0,1,2:T(8,128)(2,1)}), bf16[3,1,16,128,128]{4,3,0,1,2:T(8,128)(2,1)S(1)}, u32[]{:S(2)}, u32[]{:S(2)}) async-start(bf16[3,1,16,128,128]{4,3,0,1,2:T(8,128)(2,1)} %pad_maximum_fusion.1), calls=%async_computation.4 | async-start | bytes 3145728 | tf_op jit(solution)/shard_map/all_to_all | solution.py:195
  325.2 30.0 %all-to-all-start.5 = ((bf16[3,1,16,128,128]{4,3,1,0,2:T(8,128)(2,1)}), bf16[3,1,16,128,128]{4,3,1,0,2:T(8,128)(2,1)S(1)}, u32[]{:S(2)}, u32[]{:S(2)}) async-start(bf16[3,1,16,128,128]{4,3,1,0,2:T(8,128)(2,1)} %pad_maximum_fusion.2), calls=%async_computation.5 | async-start | bytes 3145728 | tf_op jit(solution)/shard_map/all_to_all | solution.py:195
  357.8 2.0 copy-start.5
  360.9 2.0 copy-start.3
Sparse Core Ops, SparseCore 0:
  10.4 202.5 all-gather.2
  240.9 40.9 reduce-scatter.3

commit v6 on v4

--- a/solution.py
+++ b/solution.py
@@ -145,14 +145,12 @@
     def back_layout(stacked):
         return stacked.reshape(most_slots, seq_count, token_count, head_dim)
 
-    out_back = lax.all_to_all(back_layout(slot_out), "seq", split_axis=1, concat_axis=0, tiled=True)
-
+    weight_full = jnp.transpose(weight_parts, (1, 2, 0, 3)).reshape(
+        most_slots, head_dim, dp_count * out_weight.shape[2]
+    )
     dy_rows = lax.all_gather(grad_out, "seq", axis=1, tiled=True)[0]
     part = jnp.einsum(
-        "tjd,jshd->sth",
-        dy_rows.reshape(length, dp_count, out_weight.shape[2]),
-        weight_parts,
-        preferred_element_type=jnp.float32,
+        "td,shd->sth", dy_rows, weight_full, preferred_element_type=jnp.float32
     ).astype(jnp.bfloat16)
     grad_attn = part
     weight_total = jnp.einsum("sth,td->shd", slot_out, dy_rows, preferred_element_type=jnp.float32)
@@ -172,10 +170,12 @@
             grad_attn[one],
             score_scale,
         )
-        one_stack = jnp.stack([g.reshape(1, seq_count, token_count, head_dim) for g in slot_grads])
+        one_stack = jnp.stack(
+            [g.reshape(1, seq_count, token_count, head_dim) for g in (slot_out[one],) + tuple(slot_grads)]
+        )
         grads_parts.append(lax.all_to_all(one_stack, "seq", split_axis=2, concat_axis=1, tiled=True))
-    grads_back = jnp.stack(grads_parts, axis=2).reshape(3, seq_count * most_slots, 1, token_count, head_dim)
-    all_back = (out_back, grads_back[0], grads_back[1], grads_back[2])
+    grads_back = jnp.stack(grads_parts, axis=2).reshape(4, seq_count * most_slots, 1, token_count, head_dim)
+    all_back = (grads_back[0], grads_back[1], grads_back[2], grads_back[3])
     attn_out = heads_to_tokens(all_back[0], select, token_count, head_count, head_dim)
     query_grad = heads_to_tokens(all_back[1], select, token_count, head_count, head_dim)
     key_grad = heads_to_tokens(all_back[2], select, token_count, head_count, head_dim)

time: 390 us -> 352 us (0.903)
  waiting for transfers between devices: 140 us -> 100 us
  blocking collectives: 0 us -> 37.4 us
  local copies, waits for them, and re-layouts: 72.5 us -> 54.7 us
  starting transfers between devices: 32.1 us -> 20.1 us
    all_gather x1, waiting for transfers between devices: 73.4 us -> 9.13 us  [on_device(): dy_rows = lax.all_gather(grad_out, 'seq', axis=1, tiled=True)[0]]
    all_to_all x0 -> x1, blocking collectives: none -> 37.4 us  [on_device(): lax.all_to_all(one_stack, 'seq', split_axis=2, concat_axis=1, tiled=True)]
    all_gather x1 -> x0, local copies, waits for them, and re-layouts: 28.5 us -> none  [on_device(): dy_rows = lax.all_gather(grad_out, 'seq', axis=1, tiled=True)[0]]
    all_to_all x1, waiting for transfers between devices: 0.01 us -> 26.1 us  [on_device(): lax.all_to_all(weight_copies, 'dp', split_axis=0, concat_axis=0, tiled=True)]
    all_to_all x2 -> x1, waiting for transfers between devices: 14.6 us -> 0.01 us  [on_device(): lax.all_to_all(one_stack, 'seq', split_axis=2, concat_axis=1, tiled=True)]
    all_to_all x1, waiting for transfers between devices: 51.4 us -> 64.3 us  [on_device(): lax.all_to_all(stacked, 'seq', split_axis=0, concat_axis=3, tiled=True)[0]]
    all_to_all x2 -> x1, starting transfers between devices: 14.5 us -> 4.55 us  [on_device(): lax.all_to_all(one_stack, 'seq', split_axis=2, concat_axis=1, tiled=True)]
    unnamed x29 -> x31, local copies, waits for them, and re-layouts: 18.4 us -> 22.7 us
  transfers between devices with their start and end apart: 7 -> 5, of which waited for: 3 -> 3; matrix products, arithmetic and copies ran while one was open for 29% -> 21% of each run, Pallas kernels for 22% -> 16%
where the time goes in v6:
time: 352 us; the launch traced here: 351 us
  waiting for transfers between devices  100 us (28%)
  Pallas kernels  85.4 us (24%)
  local copies, waits for them, and re-layouts  54.7 us (16%)
  blocking collectives  37.4 us (11%)
  matrix products  29.3 us (8%)
  starting transfers between devices  20.1 us (6%)
  between operations  14.3 us (4%)
  other arithmetic  9.61 us (3%)
    all_to_all x1, waiting for transfers between devices, on_device(): lax.all_to_all(stacked, 'seq', split_axis=0, concat_axis=3, tiled=True)[0]  64.3 us
    pallas_call x2, Pallas kernels, attn_backward(): pl.pallas_call(functools.partial(_bwd_kernel, nb=nb, scale=scale), grid=(...  55.2 us
    all_to_all x1, blocking collectives, on_device(): lax.all_to_all(one_stack, 'seq', split_axis=2, concat_axis=1, tiled=True)  37.4 us
    pallas_call x1, Pallas kernels, attn_forward(): pl.pallas_call(functools.partial(_fwd_kernel, scale=scale), grid=(slots,...  30.2 us
    all_to_all x1, waiting for transfers between devices, on_device(): lax.all_to_all(weight_copies, 'dp', split_axis=0, concat_axis=0, tiled=True)  26.1 us
    unnamed x31, local copies, waits for them, and re-layouts  22.7 us
    dot_general x1, matrix products, on_device(): jnp.einsum('sth,td->shd', slot_out, dy_rows, preferred_element_type=jnp.f...  14.1 us
    dot_general x1, matrix products, on_device(): jnp.einsum('td,shd->sth', dy_rows, weight_full, preferred_element_type=jn...  10.6 us
  transfers between devices with their start and end apart: 5, of which 3 were waited for; matrix products, arithmetic and copies ran while one was open for 21% of the time, Pallas kernels for 16%

profile of v6, /device:TPU:1, one launch (start us, length us, event | category | flops | bytes accessed | tf_op | source)
XLA Modules:
  0.0 351.0 jit_solution(927602781675065464)
XLA Ops:
  7.9 2.8 broadcast_in_dim.34
  10.7 6.1 %all-to-all-start.1 = ((bf16[8,2,128,640]{3,2,1,0:T(8,128)(2,1)}), bf16[8,2,128,640]{3,2,1,0:T(8,128)(2,1)S(1)}, u32[]{:S(2)}, u32[]{:S(2)}) async-start(bf16[8,2,128,640]{3,2,1,0:T(8,128)(2,1)} %broadcast_in_dim.34), calls=%async_computation.1 | async-start | bytes 5242880 | tf_op jit(solution)/shard_map/all_to_all | solution.py:142
  17.9 1.5 copy.159
  20.2 1.4 copy.162
  21.5 2.2 copy.156
  23.7 1.6 copy.157
  25.9 1.4 copy.161
  27.3 2.2 copy.154
  29.4 1.5 copy.155
  32.5 2.0 pad_maximum_fusion
  34.5 26.1 %all-to-all-done.1 = bf16[8,2,128,640]{3,2,1,0:T(8,128)(2,1)S(1)} async-done(((bf16[8,2,128,640]{3,2,1,0:T(8,128)(2,1)}), bf16[8,2,128,640]{3,2,1,0:T(8,128)(2,1)S(1)}, u32[]{:S(2)}, u32[]{:S(2)}) %all-to-all-start.1) | async-done | bytes 2621472 | tf_op jit(solution)/shard_map/all_to_all | solution.py:142
  60.6 1.5 copy-done
  62.1 9.2 %all-to-all-start = ((bf16[16,3,2,128,128]{4,3,2,1,0:T(8,128)(2,1)}), bf16[16,3,2,128,128]{4,3,2,1,0:T(8,128)(2,1)S(1)}, u32[]{:S(2)}, u32[]{:S(2)}) async-start(bf16[16,3,2,128,128]{4,3,2,1,0:T(8,128)(2,1)} %pad_maximum_fusion), calls=%async_computation | async-start | bytes 6291456 | tf_op jit(solution)/shard_map/all_to_all | solution.py:136
  71.9 3.7 %copy.197 = bf16[8,2,16,8,640]{4,3,0,2,1:T(8,128)(2,1)} copy(bf16[8,2,16,8,640]{4,3,2,1,0:T(8,128)(2,1)} %bitcast.120) | data formatting | bytes 5242880 | tf_op jit(solution)/shard_map/reshape | solution.py:148
  75.6 64.3 %all-to-all-done = bf16[16,3,2,128,128]{4,3,2,1,0:T(8,128)(2,1)S(1)} async-done(((bf16[16,3,2,128,128]{4,3,2,1,0:T(8,128)(2,1)}), bf16[16,3,2,128,128]{4,3,2,1,0:T(8,128)(2,1)S(1)}, u32[]{:S(2)}, u32[]{:S(2)}) %all-to-all-start) | async-done | bytes 3145760 | tf_op jit(solution)/shard_map/all_to_all | solution.py:136
  144.2 30.2 %shard_map.110 = bf16[2,2048,128]{2,1,0:T(8,128)(2,1)} custom-call(bf16[2,2048,128]{2,1,0:T(8,128)(2,1)} %bitcast.125, bf16[2,2048,128]{2,1,0:T(8,128)(2,1)} %bitcast.126, bf16[2,2048,128]{2,1,0:T(8,128)(2,1)} %bitcast.127, f32[2,16,1,2048]{3,2,1,0:T(1,128)} %bitcast.150), custom_call_target="tpu_custom_call" | custom-call | tf_op jit(solution)/shard_map/pallas_call | solution.py:66
  174.4 1.7 fusion.45
  177.3 9.1 %all-gather.2.cloned.1.call-done = bf16[1,2048,5120]{2,1,0:T(8,128)(2,1)} async-done(((bf16[1,128,5120]{2,1,0:T(8,128)(2,1)}), bf16[1,2048,5120]{2,1,0:T(8,128)(2,1)}) %all-gather.2.cloned.1.call-update) | async-done | bytes 20971536 | tf_op jit(solution)/shard_map/all_gather | solution.py:151
  186.4 10.6 %fusion.13 = bf16[2,2048,128]{2,1,0:T(8,128)(2,1)S(1)} fusion(bf16[2,128,5120]{2,1,0:T(8,128)(2,1)} %bitcast.135, bf16[1,2048,5120]{2,1,0:T(8,128)(2,1)} %all-gather.2.cloned.1.call-done), kind=kOutput, calls=%fused_computation.15 | convolution fusion | flops 5369233408 | bytes 24641536 | tf_op jit(solution)/shard_map/td,shd->sth/dot_general | solution.py:152
  198.9 27.6 %shard_map.112 = (bf16[1,2048,128]{2,1,0:T(8,128)(2,1)}, bf16[1,2048,128]{2,1,0:T(8,128)(2,1)}, bf16[1,2048,128]{2,1,0:T(8,128)(2,1)}) custom-call(bf16[1,2048,128]{2,1,0:T(8,128)(2,1)} %bitcast.148, bf16[1,2048,128]{2,1,0:T(8,128)(2,1)} %bitcast.147, bf16[1,2048,128]{2,1,0:T(8,128)(2,1)} %bitcast.146, f32[1,16,1,2048]{3,2,1,0:T(1,128)} %bitcast.158, ...), custom_call_target="tpu_custom_call" | custom-call | tf_op jit(solution)/shard_map/pallas_call | solution.py:84
  226.5 3.0 pad_maximum_fusion.2
  229.5 4.5 %all-to-all-start.3 = ((bf16[4,1,16,128,128]{4,3,1,0,2:T(8,128)(2,1)}), bf16[4,1,16,128,128]{4,3,1,0,2:T(8,128)(2,1)}, u32[]{:S(2)}, u32[]{:S(2)}) async-start(bf16[4,1,16,128,128]{4,3,1,0,2:T(8,128)(2,1)} %pad_maximum_fusion.2), calls=%async_computation.3 | async-start | bytes 4194304 | tf_op jit(solution)/shard_map/all_to_all | solution.py:176
  234.3 14.1 %fusion.7 = bf16[2,128,5120]{2,1,0:T(8,128)(2,1)} fusion(bf16[2,2048,128]{2,1,0:T(8,128)(2,1)S(1)} %copy-done.2, bf16[1,2048,5120]{2,1,0:T(8,128)(2,1)} %all-gather.2.cloned.1.call-done), kind=kOutput, calls=%fused_computation.5 | convolution fusion | flops 5371330560 | bytes 24641536 | tf_op jit(solution)/shard_map/sth,td->shd/dot_general | solution.py:156
  248.4 5.9 %copy.195 = bf16[2,128,5120]{1,0,2:T(2,128)(2,1)S(1)} copy(bf16[2,128,5120]{2,1,0:T(8,128)(2,1)} %fusion.7) | data formatting | bytes 5242880
  254.2 1.8 copy.200
  256.9 27.6 %shard_map.111 = (bf16[1,2048,128]{2,1,0:T(8,128)(2,1)}, bf16[1,2048,128]{2,1,0:T(8,128)(2,1)}, bf16[1,2048,128]{2,1,0:T(8,128)(2,1)}) custom-call(bf16[1,2048,128]{2,1,0:T(8,128)(2,1)} %bitcast.145, bf16[1,2048,128]{2,1,0:T(8,128)(2,1)} %bitcast.144, bf16[1,2048,128]{2,1,0:T(8,128)(2,1)} %bitcast.143, f32[1,16,1,2048]{3,2,1,0:T(1,128)} %bitcast.157, ...), custom_call_target="tpu_custom_call" | custom-call | tf_op jit(solution)/shard_map/pallas_call | solution.py:84
  284.4 1.6 pad_maximum_fusion.1
  286.1 37.4 %all_to_all.38 = bf16[4,1,16,128,128]{4,3,0,1,2:T(8,128)(2,1)S(1)} all-to-all(bf16[4,1,16,128,128]{4,3,0,1,2:T(8,128)(2,1)S(1)} %pad_maximum_fusion.1), channel_id=1, replica_groups=mesh['dp'=8,'seq'=16] {'seq'}, dimensions={2} | all-to-all | bytes 4194304 | tf_op jit(solution)/shard_map/all_to_all | solution.py:176
  323.5 1.7 pad_maximum_fusion.3
  326.3 1.3 fusion.16
  327.6 2.3 copy.179
  329.9 2.2 copy.187
  (64 shorter events, 26.7 us)
Async XLA Ops:
  7.2 179.3 %all-gather.2.cloned.1.call-start = ((), (), s32[]{:S(2)}) async-start(), calls=%async_computation.5 | async-start | bytes 22282240 | tf_op jit(solution)/shard_map/all_gather | solution.py:151
  10.7 6.1 %copy-start.7 = (bf16[1,128,2560]{2,1,0:T(8,128)(2,1)S(1)}, bf16[1,128,2560]{2,1,0:T(8,128)(2,1)}, u32[]{:S(2)}) copy-start(bf16[1,128,2560]{2,1,0:T(8,128)(2,1)} %param.9) | copy-start | bytes 1966084
  10.7 49.9 %all-to-all-start.1 = ((bf16[8,2,128,640]{3,2,1,0:T(8,128)(2,1)}), bf16[8,2,128,640]{3,2,1,0:T(8,128)(2,1)S(1)}, u32[]{:S(2)}, u32[]{:S(2)}) async-start(bf16[8,2,128,640]{3,2,1,0:T(8,128)(2,1)} %broadcast_in_dim.34), calls=%async_computation.1 | async-start | bytes 5242880 | tf_op jit(solution)/shard_map/all_to_all | solution.py:142
  16.8 2.6 copy-start.9
  30.9 1.2 copy-start.5
  31.0 1.5 copy-start.6
  34.5 36.9 %copy-start.8 = (s32[20,16,16]{0,2,1:T(8,128)S(1)}, s32[20,16,16]{0,2,1:T(8,128)}, u32[]{:S(2)}) copy-start(s32[20,16,16]{0,2,1:T(8,128)} %param.12) | copy-start | bytes 61444
  60.6 1.5 copy-start
  62.1 77.7 %all-to-all-start = ((bf16[16,3,2,128,128]{4,3,2,1,0:T(8,128)(2,1)}), bf16[16,3,2,128,128]{4,3,2,1,0:T(8,128)(2,1)S(1)}, u32[]{:S(2)}, u32[]{:S(2)}) async-start(bf16[16,3,2,128,128]{4,3,2,1,0:T(8,128)(2,1)} %pad_maximum_fusion), calls=%async_computation | async-start | bytes 6291456 | tf_op jit(solution)/shard_map/all_to_all | solution.py:136
  174.4 1.9 copy-start.1
  197.1 29.4 %copy-start.4 = (bf16[1,2048,128]{2,1,0:T(8,128)(2,1)S(1)}, bf16[1,2048,128]{2,1,0:T(8,128)(2,1)}, u32[]{:S(2)}) copy-start(bf16[1,2048,128]{2,1,0:T(8,128)(2,1)} %get-tuple-element.52.o_ref) | copy-start | bytes 1572868
  229.5 4.8 %copy-start.2 = (bf16[2,2048,128]{2,1,0:T(8,128)(2,1)S(1)}, bf16[2,2048,128]{2,1,0:T(8,128)(2,1)}, u32[]{:S(2)}) copy-start(bf16[2,2048,128]{2,1,0:T(8,128)(2,1)} %shard_map.110) | copy-start | bytes 3145732
  229.5 56.6 %all-to-all-start.3 = ((bf16[4,1,16,128,128]{4,3,1,0,2:T(8,128)(2,1)}), bf16[4,1,16,128,128]{4,3,1,0,2:T(8,128)(2,1)}, u32[]{:S(2)}, u32[]{:S(2)}) async-start(bf16[4,1,16,128,128]{4,3,1,0,2:T(8,128)(2,1)} %pad_maximum_fusion.2), calls=%async_computation.3 | async-start | bytes 4194304 | tf_op jit(solution)/shard_map/all_to_all | solution.py:176
  234.0 107.3 %reduce-scatter.4.cloned.1.call-start = ((), (), s32[]{:S(2)}) async-start(), calls=%async_computation.6 | async-start | bytes 2949120
  256.1 28.4 %copy-start.3 = (bf16[1,2048,128]{2,1,0:T(8,128)(2,1)S(1)}, bf16[1,2048,128]{2,1,0:T(8,128)(2,1)}, u32[]{:S(2)}) copy-start(bf16[1,2048,128]{2,1,0:T(8,128)(2,1)} %get-tuple-element.53.o_ref) | copy-start | bytes 1572868
Sparse Core Ops, SparseCore 0:
  10.4 175.9 all-gather.1
  256.2 40.7 reduce-scatter.3

commit v7 on v6

--- a/solution.py
+++ b/solution.py
@@ -15,7 +15,7 @@
 def _probs(q, k, bias, scale):
     sc = lax.dot_general(q, k, NT, preferred_element_type=jnp.float32) * scale + bias
     e = jnp.exp(sc - jnp.max(sc, axis=1, keepdims=True))
-    return e / jnp.sum(e, axis=1, keepdims=True)
+    return e * (1.0 / jnp.sum(e, axis=1, keepdims=True))
 
 
 def _fwd_kernel(q_ref, k_ref, v_ref, b_ref, o_ref, *, scale):
@@ -148,12 +148,21 @@
     weight_full = jnp.transpose(weight_parts, (1, 2, 0, 3)).reshape(
         most_slots, head_dim, dp_count * out_weight.shape[2]
     )
-    dy_rows = lax.all_gather(grad_out, "seq", axis=1, tiled=True)[0]
-    part = jnp.einsum(
-        "td,shd->sth", dy_rows, weight_full, preferred_element_type=jnp.float32
+    half = grad_out.shape[2] // 2
+    dy_first = lax.all_gather(grad_out[:, :, :half], "seq", axis=1, tiled=True)[0]
+    dy_second = lax.all_gather(grad_out[:, :, half:], "seq", axis=1, tiled=True)[0]
+    part = (
+        jnp.einsum("td,shd->sth", dy_first, weight_full[:, :, :half], preferred_element_type=jnp.float32)
+        + jnp.einsum("td,shd->sth", dy_second, weight_full[:, :, half:], preferred_element_type=jnp.float32)
     ).astype(jnp.bfloat16)
     grad_attn = part
-    weight_total = jnp.einsum("sth,td->shd", slot_out, dy_rows, preferred_element_type=jnp.float32)
+    weight_total = jnp.concatenate(
+        [
+            jnp.einsum("sth,td->shd", slot_out, dy_first, preferred_element_type=jnp.float32),
+            jnp.einsum("sth,td->shd", slot_out, dy_second, preferred_element_type=jnp.float32),
+        ],
+        axis=2,
+    )
     grad_attn, weight_total = (grad_attn, weight_total)
     weight_grad = lax.psum_scatter(
         (weight_total * grad_scale).astype(jnp.bfloat16), "dp", scatter_dimension=2, tiled=True

time: 352 us -> 375 us (1.065)
  waiting for transfers between devices: 100 us -> 120 us
    all_gather x1 -> x2, waiting for transfers between devices: 9.13 us -> 44 us  [the longest x1 44 us: on_device(): lax.all_gather(grad_out[:, :, :half], 'seq', axis=1, tiled=True)[0]]
    all_to_all x1, waiting for transfers between devices: 64.3 us -> 56.1 us  [on_device(): lax.all_to_all(stacked, 'seq', split_axis=0, concat_axis=3, tiled=True)[0]]
    all_to_all x1, waiting for transfers between devices: 26.1 us -> 18.9 us  [on_device(): lax.all_to_all(weight_copies, 'dp', split_axis=0, concat_axis=0, tiled=True)]
    dot_general x2 -> x4, matrix products: 24.7 us -> 25 us  [the longest x1 7.14 us: on_device(): jnp.einsum('td,shd->sth', dy_second, weight_full[:, :, half:], preferred_...]
    unnamed x31 -> x35, local copies, waits for them, and re-layouts: 22.7 us -> 22.8 us
  transfers between devices with their start and end apart: 5 -> 6, of which waited for: 3 -> 3; matrix products, arithmetic and copies ran while one was open for 21% -> 21% of each run, Pallas kernels for 16% -> 15%
where the time goes in v7:
time: 375 us; the launch traced here: 374 us
  waiting for transfers between devices  120 us (32%)
  Pallas kernels  85.5 us (23%)
  local copies, waits for them, and re-layouts  56.3 us (15%)
  blocking collectives  36.9 us (10%)
  matrix products  29.6 us (8%)
  starting transfers between devices  20.2 us (5%)
  between operations  14 us (4%)
  other arithmetic  11.4 us (3%)
    all_to_all x1, waiting for transfers between devices, on_device(): lax.all_to_all(stacked, 'seq', split_axis=0, concat_axis=3, tiled=True)[0]  56.1 us
    pallas_call x2, Pallas kernels, attn_backward(): pl.pallas_call(functools.partial(_bwd_kernel, nb=nb, scale=scale), grid=(...  55.3 us
    all_gather x1, waiting for transfers between devices, on_device(): lax.all_gather(grad_out[:, :, :half], 'seq', axis=1, tiled=True)[0]  44 us
    all_to_all x1, blocking collectives, on_device(): lax.all_to_all(one_stack, 'seq', split_axis=2, concat_axis=1, tiled=True)  36.9 us
    pallas_call x1, Pallas kernels, attn_forward(): pl.pallas_call(functools.partial(_fwd_kernel, scale=scale), grid=(slots,...  30.2 us
    unnamed x35, local copies, waits for them, and re-layouts  22.8 us
    all_to_all x1, waiting for transfers between devices, on_device(): lax.all_to_all(weight_copies, 'dp', split_axis=0, concat_axis=0, tiled=True)  18.9 us
    all_to_all x1, starting transfers between devices, on_device(): lax.all_to_all(stacked, 'seq', split_axis=0, concat_axis=3, tiled=True)[0]  9.26 us
  transfers between devices with their start and end apart: 6, of which 3 were waited for; matrix products, arithmetic and copies ran while one was open for 21% of the time, Pallas kernels for 15%

profile of v7, /device:TPU:1, one launch (start us, length us, event | category | flops | bytes accessed | tf_op | source)
XLA Modules:
  0.0 373.7 jit_solution(8452604572203444332)
XLA Ops:
  7.2 2.5 fusion.51
  10.5 1.9 broadcast_in_dim.34
  12.3 6.1 %all-to-all-start.1 = ((bf16[8,2,128,640]{3,2,1,0:T(8,128)(2,1)}), bf16[8,2,128,640]{3,2,1,0:T(8,128)(2,1)S(1)}, u32[]{:S(2)}, u32[]{:S(2)}) async-start(bf16[8,2,128,640]{3,2,1,0:T(8,128)(2,1)} %broadcast_in_dim.34), calls=%async_computation.1 | async-start | bytes 5242880 | tf_op jit(solution)/shard_map/all_to_all | solution.py:142
  19.5 1.5 copy.163
  23.1 2.2 copy.164
  25.3 1.6 copy.165
  28.9 2.2 copy.166
  34.1 2.0 pad_maximum_fusion
  36.1 18.9 %all-to-all-done.1 = bf16[8,2,128,640]{3,2,1,0:T(8,128)(2,1)S(1)} async-done(((bf16[8,2,128,640]{3,2,1,0:T(8,128)(2,1)}), bf16[8,2,128,640]{3,2,1,0:T(8,128)(2,1)S(1)}, u32[]{:S(2)}, u32[]{:S(2)}) %all-to-all-start.1) | async-done | bytes 2621472 | tf_op jit(solution)/shard_map/all_to_all | solution.py:142
  55.1 1.5 copy-done.2
  56.6 9.3 %all-to-all-start = ((bf16[16,3,2,128,128]{4,3,2,1,0:T(8,128)(2,1)}), bf16[16,3,2,128,128]{4,3,2,1,0:T(8,128)(2,1)S(1)}, u32[]{:S(2)}, u32[]{:S(2)}) async-start(bf16[16,3,2,128,128]{4,3,2,1,0:T(8,128)(2,1)} %pad_maximum_fusion), calls=%async_computation | async-start | bytes 6291456 | tf_op jit(solution)/shard_map/all_to_all | solution.py:136
  66.4 3.7 copy.209
  70.1 56.1 %all-to-all-done = bf16[16,3,2,128,128]{4,3,2,1,0:T(8,128)(2,1)S(1)} async-done(((bf16[16,3,2,128,128]{4,3,2,1,0:T(8,128)(2,1)}), bf16[16,3,2,128,128]{4,3,2,1,0:T(8,128)(2,1)S(1)}, u32[]{:S(2)}, u32[]{:S(2)}) %all-to-all-start) | async-done | bytes 3145760 | tf_op jit(solution)/shard_map/all_to_all | solution.py:136
  130.5 30.2 %shard_map.110 = bf16[2,2048,128]{2,1,0:T(8,128)(2,1)} custom-call(bf16[2,2048,128]{2,1,0:T(8,128)(2,1)} %bitcast.131, bf16[2,2048,128]{2,1,0:T(8,128)(2,1)} %bitcast.130, bf16[2,2048,128]{2,1,0:T(8,128)(2,1)} %bitcast.129, f32[2,16,1,2048]{3,2,1,0:T(1,128)} %bitcast.155), custom_call_target="tpu_custom_call" | custom-call | tf_op jit(solution)/shard_map/pallas_call | solution.py:66
  160.8 1.7 fusion.49
  163.7 7.1 %fusion.2 = f32[2,128,2048]{1,2,0:T(8,128)} fusion(bf16[1,2048,2560]{2,1,0:T(8,128)(2,1)} %all-gather.5.cloned.1.call-done, bf16[2,128,5120]{2,1,0:T(8,128)(2,1)} %bitcast.139), kind=kOutput, calls=%fused_computation.2 | convolution fusion | flops 2684354560 | bytes 13893632 | tf_op jit(solution)/shard_map/td,shd->sth/dot_general | solution.py:156
  170.8 44.0 %all-gather.3.cloned.1.call-done = bf16[1,2048,2560]{2,1,0:T(8,128)(2,1)} async-done(((bf16[1,128,2560]{2,1,0:T(8,128)(2,1)}), bf16[1,2048,2560]{2,1,0:T(8,128)(2,1)}) %all-gather.3.cloned.1.call-update) | async-done | bytes 10485776 | tf_op jit(solution)/shard_map/all_gather | solution.py:152
  214.8 6.5 %fusion.15 = bf16[2,2048,128]{2,1,0:T(8,128)(2,1)S(1)} fusion(f32[2,128,2048]{1,2,0:T(8,128)} %fusion.2, bf16[1,2048,2560]{2,1,0:T(8,128)(2,1)} %all-gather.3.cloned.1.call-done, bf16[2,128,5120]{2,1,0:T(8,128)(2,1)S(1)} %bitcast.140), kind=kOutput, calls=%fused_computation.20 | convolution fusion | flops 2685403136 | bytes 14942208 | tf_op jit(solution)/shard_map/td,shd->sth/dot_general | solution.py:155
  223.1 27.7 %shard_map.111 = (bf16[1,2048,128]{2,1,0:T(8,128)(2,1)}, bf16[1,2048,128]{2,1,0:T(8,128)(2,1)}, bf16[1,2048,128]{2,1,0:T(8,128)(2,1)}) custom-call(bf16[1,2048,128]{2,1,0:T(8,128)(2,1)} %bitcast.153, bf16[1,2048,128]{2,1,0:T(8,128)(2,1)} %bitcast.152, bf16[1,2048,128]{2,1,0:T(8,128)(2,1)} %bitcast.151, f32[1,16,1,2048]{3,2,1,0:T(1,128)} %bitcast.163, ...), custom_call_target="tpu_custom_call" | custom-call | tf_op jit(solution)/shard_map/pallas_call | solution.py:84
  250.8 3.0 pad_maximum_fusion.1
  253.7 4.6 %all-to-all-start.2 = ((bf16[4,1,16,128,128]{4,3,0,1,2:T(8,128)(2,1)}), bf16[4,1,16,128,128]{4,3,0,1,2:T(8,128)(2,1)}, u32[]{:S(2)}, u32[]{:S(2)}) async-start(bf16[4,1,16,128,128]{4,3,0,1,2:T(8,128)(2,1)} %pad_maximum_fusion.1), calls=%async_computation.2 | async-start | bytes 4194304 | tf_op jit(solution)/shard_map/all_to_all | solution.py:185
  258.6 5.6 %fusion.4 = f32[2,128,2560]{2,1,0:T(8,128)S(1)} fusion(bf16[2,2048,128]{2,1,0:T(8,128)(2,1)S(1)} %copy-done.1, bf16[1,2048,2560]{2,1,0:T(8,128)(2,1)} %all-gather.3.cloned.1.call-done), kind=kOutput, calls=%fused_computation.4 | convolution fusion | flops 2684354560 | bytes 14155776 | tf_op jit(solution)/shard_map/sth,td->shd/dot_general | solution.py:161
  264.2 5.7 %fusion = f32[2,128,2560]{2,1,0:T(8,128)S(1)} fusion(bf16[2,2048,128]{2,1,0:T(8,128)(2,1)S(1)} %copy-done.1, bf16[1,2048,2560]{2,1,0:T(8,128)(2,1)} %all-gather.5.cloned.1.call-done), kind=kOutput, calls=%fused_computation | convolution fusion | flops 2684354560 | bytes 14155776 | tf_op jit(solution)/shard_map/sth,td->shd/dot_general | solution.py:162
  269.9 1.9 fusion.8
  271.8 5.9 %copy.207 = bf16[2,128,5120]{1,0,2:T(2,128)(2,1)S(1)} copy(bf16[2,128,5120]{2,1,0:T(8,128)(2,1)} %fusion.8) | data formatting | bytes 5242880
  277.6 1.9 copy.212
  280.3 27.6 %shard_map.112 = (bf16[1,2048,128]{2,1,0:T(8,128)(2,1)}, bf16[1,2048,128]{2,1,0:T(8,128)(2,1)}, bf16[1,2048,128]{2,1,0:T(8,128)(2,1)}) custom-call(bf16[1,2048,128]{2,1,0:T(8,128)(2,1)} %bitcast.150, bf16[1,2048,128]{2,1,0:T(8,128)(2,1)} %bitcast.149, bf16[1,2048,128]{2,1,0:T(8,128)(2,1)} %bitcast.148, f32[1,16,1,2048]{3,2,1,0:T(1,128)} %bitcast.162, ...), custom_call_target="tpu_custom_call" | custom-call | tf_op jit(solution)/shard_map/pallas_call | solution.py:84
  307.9 1.6 pad_maximum_fusion.2
  309.5 36.9 %all_to_all.38 = bf16[4,1,16,128,128]{4,3,1,0,2:T(8,128)(2,1)S(1)} all-to-all(bf16[4,1,16,128,128]{4,3,1,0,2:T(8,128)(2,1)S(1)} %pad_maximum_fusion.2), channel_id=1, replica_groups=mesh['dp'=8,'seq'=16] {'seq'}, dimensions={2} | all-to-all | bytes 4194304 | tf_op jit(solution)/shard_map/all_to_all | solution.py:185
  346.4 1.7 pad_maximum_fusion.3
  350.6 2.3 copy.194
  352.9 2.2 copy.200
  (75 shorter events, 32.4 us)
Async XLA Ops:
  7.2 3.3 copy-start.9
  7.2 156.5 %all-gather.5.cloned.1.call-start = ((), (), s32[]{:S(2)}) async-start(), calls=%async_computation.6 | async-start | bytes 11141120 | tf_op jit(solution)/shard_map/all_gather | solution.py:153
  9.7 205.1 %all-gather.3.cloned.1.call-start = ((), (), s32[]{:S(2)}) async-start(), calls=%async_computation.5 | async-start | bytes 11141120 | tf_op jit(solution)/shard_map/all_gather | solution.py:152
  12.3 6.1 %copy-start.8 = (bf16[1,128,2560]{2,1,0:T(8,128)(2,1)S(1)}, bf16[1,128,2560]{2,1,0:T(8,128)(2,1)}, u32[]{:S(2)}) copy-start(bf16[1,128,2560]{2,1,0:T(8,128)(2,1)} %param.7) | copy-start | bytes 1966084
  12.3 42.8 %all-to-all-start.1 = ((bf16[8,2,128,640]{3,2,1,0:T(8,128)(2,1)}), bf16[8,2,128,640]{3,2,1,0:T(8,128)(2,1)S(1)}, u32[]{:S(2)}, u32[]{:S(2)}) async-start(bf16[8,2,128,640]{3,2,1,0:T(8,128)(2,1)} %broadcast_in_dim.34), calls=%async_computation.1 | async-start | bytes 5242880 | tf_op jit(solution)/shard_map/all_to_all | solution.py:142
  18.4 2.6 copy-start.11
  32.6 1.2 copy-start.5
  32.6 1.6 copy-start.6
  36.1 29.9 %copy-start.10 = (s32[20,16,16]{0,2,1:T(8,128)S(1)}, s32[20,16,16]{0,2,1:T(8,128)}, u32[]{:S(2)}) copy-start(s32[20,16,16]{0,2,1:T(8,128)} %param.12) | copy-start | bytes 61444
  55.1 1.5 copy-start.2
  56.6 69.6 %all-to-all-start = ((bf16[16,3,2,128,128]{4,3,2,1,0:T(8,128)(2,1)}), bf16[16,3,2,128,128]{4,3,2,1,0:T(8,128)(2,1)S(1)}, u32[]{:S(2)}, u32[]{:S(2)}) async-start(bf16[16,3,2,128,128]{4,3,2,1,0:T(8,128)(2,1)} %pad_maximum_fusion), calls=%async_computation | async-start | bytes 6291456 | tf_op jit(solution)/shard_map/all_to_all | solution.py:136
  160.8 1.9 copy-start
  163.7 51.1 %copy-start.7 = (bf16[8,2,16,8,640]{4,3,0,2,1:T(8,128)(2,1)S(1)}, bf16[8,2,16,8,640]{4,3,0,2,1:T(8,128)(2,1)}, u32[]{:S(2)}) copy-start(bf16[8,2,16,8,640]{4,3,0,2,1:T(8,128)(2,1)} %copy.209) | copy-start | bytes 7864324
  221.3 29.5 %copy-start.4 = (bf16[1,2048,128]{2,1,0:T(8,128)(2,1)S(1)}, bf16[1,2048,128]{2,1,0:T(8,128)(2,1)}, u32[]{:S(2)}) copy-start(bf16[1,2048,128]{2,1,0:T(8,128)(2,1)} %get-tuple-element.55.o_ref) | copy-start | bytes 1572868
  253.7 4.8 %copy-start.1 = (bf16[2,2048,128]{2,1,0:T(8,128)(2,1)S(1)}, bf16[2,2048,128]{2,1,0:T(8,128)(2,1)}, u32[]{:S(2)}) copy-start(bf16[2,2048,128]{2,1,0:T(8,128)(2,1)} %shard_map.110) | copy-start | bytes 3145732
  253.7 55.8 %all-to-all-start.2 = ((bf16[4,1,16,128,128]{4,3,0,1,2:T(8,128)(2,1)}), bf16[4,1,16,128,128]{4,3,0,1,2:T(8,128)(2,1)}, u32[]{:S(2)}, u32[]{:S(2)}) async-start(bf16[4,1,16,128,128]{4,3,0,1,2:T(8,128)(2,1)} %pad_maximum_fusion.1), calls=%async_computation.2 | async-start | bytes 4194304 | tf_op jit(solution)/shard_map/all_to_all | solution.py:185
  258.3 106.0 %reduce-scatter.4.cloned.1.call-start = ((), (), s32[]{:S(2)}) async-start(), calls=%async_computation.7 | async-start | bytes 2949120
  279.5 28.4 %copy-start.3 = (bf16[1,2048,128]{2,1,0:T(8,128)(2,1)S(1)}, bf16[1,2048,128]{2,1,0:T(8,128)(2,1)}, u32[]{:S(2)}) copy-start(bf16[1,2048,128]{2,1,0:T(8,128)(2,1)} %get-tuple-element.54.o_ref) | copy-start | bytes 1572868
Sparse Core Ops, SparseCore 0:
  11.0 114.4 all-gather.4
  128.6 86.1 all-gather.2
  279.6 41.0 reduce-scatter.3

commit v8 on v6

--- a/solution.py
+++ b/solution.py
@@ -18,15 +18,16 @@
     return e / jnp.sum(e, axis=1, keepdims=True)
 
 
-def _fwd_kernel(q_ref, k_ref, v_ref, b_ref, o_ref, *, scale):
+def _fwd_kernel(q_ref, k_ref, v_ref, b_ref, o_ref, p_ref, *, scale):
     prob = _probs(q_ref[0], k_ref[0], b_ref[0, 0], scale)
+    p_ref[0] = prob
     out = jnp.dot(prob.astype(jnp.bfloat16), v_ref[0], preferred_element_type=jnp.float32)
     o_ref[0] = out.astype(o_ref.dtype)
 
 
-def _bwd_kernel(q_ref, k_ref, v_ref, b_ref, o_ref, do_ref, dq_ref, dk_ref, dv_ref,
+def _bwd_kernel(q_ref, k_ref, v_ref, p_ref, o_ref, do_ref, dq_ref, dk_ref, dv_ref,
                 dk_scr, dv_scr, *, nb, scale):
-    qi = pl.program_id(1)
+    qi = pl.program_id(0)
 
     @pl.when(qi == 0)
     def _():
@@ -37,7 +38,7 @@
     k = k_ref[0]
     v = v_ref[0]
     do = do_ref[0]
-    prob = _probs(q, k, b_ref[0, 0], scale)
+    prob = p_ref[0]
     low = prob.astype(jnp.bfloat16)
     delta = jnp.sum(do.astype(jnp.float32) * o_ref[0].astype(jnp.float32), axis=1, keepdims=True)
     dv_scr[...] += lax.dot_general(low, do, TN, preferred_element_type=jnp.float32)
@@ -57,40 +58,44 @@
     return jnp.where(spread > 0, 0.0, -jnp.inf).astype(jnp.float32)[:, :, None, :]
 
 
-def attn_forward(bias, q, k, v, scale, interpret=False):
+def attn_forward(bias, q, k, v, scale):
     slots, length, hd = q.shape
     nb = length // TILE
     row = pl.BlockSpec((1, TILE, hd), lambda s, i: (s, i, 0))
     full = pl.BlockSpec((1, length, hd), lambda s, i: (s, 0, 0))
     brow = pl.BlockSpec((1, 1, 1, length), lambda s, i: (s, i, 0, 0))
+    prow = pl.BlockSpec((1, TILE, length), lambda s, i: (s, i, 0))
     return pl.pallas_call(
         functools.partial(_fwd_kernel, scale=scale),
         grid=(slots, nb),
         in_specs=[row, full, full, brow],
-        out_specs=row,
-        out_shape=jax.ShapeDtypeStruct(q.shape, jnp.bfloat16),
+        out_specs=[row, prow],
+        out_shape=(
+            jax.ShapeDtypeStruct(q.shape, jnp.bfloat16),
+            jax.ShapeDtypeStruct((slots, length, length), jnp.float32),
+        ),
         compiler_params=pltpu.CompilerParams(dimension_semantics=("arbitrary", "arbitrary")),
-        interpret=interpret,
     )(q, k, v, bias)
 
 
-def attn_backward(bias, q, k, v, o, do, scale, interpret=False):
+def attn_backward(prob, q, k, v, o, do, scale, slot):
     slots, length, hd = q.shape
     nb = length // TILE
-    row = pl.BlockSpec((1, TILE, hd), lambda s, i: (s, i, 0))
-    full = pl.BlockSpec((1, length, hd), lambda s, i: (s, 0, 0))
-    brow = pl.BlockSpec((1, 1, 1, length), lambda s, i: (s, i, 0, 0))
-    shape = jax.ShapeDtypeStruct(q.shape, jnp.bfloat16)
+    row = pl.BlockSpec((1, TILE, hd), lambda i: (slot, i, 0))
+    full = pl.BlockSpec((1, length, hd), lambda i: (slot, 0, 0))
+    prow = pl.BlockSpec((1, TILE, length), lambda i: (slot, i, 0))
+    out_row = pl.BlockSpec((1, TILE, hd), lambda i: (0, i, 0))
+    out_full = pl.BlockSpec((1, length, hd), lambda i: (0, 0, 0))
+    shape = jax.ShapeDtypeStruct((1, length, hd), jnp.bfloat16)
     return pl.pallas_call(
         functools.partial(_bwd_kernel, nb=nb, scale=scale),
-        grid=(slots, nb),
-        in_specs=[row, full, full, brow, row, row],
-        out_specs=[row, full, full],
+        grid=(nb,),
+        in_specs=[row, full, full, prow, row, row],
+        out_specs=[out_row, out_full, out_full],
         out_shape=(shape, shape, shape),
         scratch_shapes=[pltpu.VMEM((length, hd), jnp.float32), pltpu.VMEM((length, hd), jnp.float32)],
-        compiler_params=pltpu.CompilerParams(dimension_semantics=("arbitrary", "arbitrary")),
-        interpret=interpret,
-    )(q, k, v, bias, o, do)
+        compiler_params=pltpu.CompilerParams(dimension_semantics=("arbitrary",)),
+    )(q, k, v, prob, o, do)
 
 
 def slot_table(head_owner, most_slots, seq_count):
@@ -140,7 +145,7 @@
     dp_count = lax.axis_size("dp")
     weight_copies = jnp.broadcast_to(out_weight[None], (dp_count,) + out_weight.shape)
     weight_parts = lax.all_to_all(weight_copies, "dp", split_axis=0, concat_axis=0, tiled=True)
-    slot_out = attn_forward(bias, slot_query, slot_key, slot_value, score_scale)
+    slot_out, slot_prob = attn_forward(bias, slot_query, slot_key, slot_value, score_scale)
 
     def back_layout(stacked):
         return stacked.reshape(most_slots, seq_count, token_count, head_dim)
@@ -158,24 +163,29 @@
     weight_grad = lax.psum_scatter(
         (weight_total * grad_scale).astype(jnp.bfloat16), "dp", scatter_dimension=2, tiled=True
     ).astype(jnp.float32)
-    grads_parts = []
+    def to_owners(tensors):
+        one_stack = jnp.stack([t.reshape(seq_count, token_count, head_dim) for t in tensors])
+        return lax.all_to_all(one_stack, "seq", split_axis=1, concat_axis=1, tiled=True)
+
+    sent = []
     for slot_number in range(most_slots):
-        one = slice(slot_number, slot_number + 1)
         slot_grads = attn_backward(
-            bias[one],
-            slot_query[one],
-            slot_key[one],
-            slot_value[one],
-            slot_out[one],
-            grad_attn[one],
-            score_scale,
+            slot_prob, slot_query, slot_key, slot_value, slot_out, grad_attn, score_scale, slot_number
         )
-        one_stack = jnp.stack(
-            [g.reshape(1, seq_count, token_count, head_dim) for g in (slot_out[one],) + tuple(slot_grads)]
+        if slot_number == 0:
+            sent.append(to_owners(tuple(slot_out) + tuple(slot_grads)))
+        else:
+            sent.append(to_owners(slot_grads))
+    base = most_slots
+
+    def merged(pieces):
+        return jnp.stack(pieces, axis=1).reshape(seq_count * most_slots, 1, token_count, head_dim)
+
+    all_back = [merged([sent[0][number] for number in range(most_slots)])]
+    for which in range(3):
+        all_back.append(
+            merged([sent[0][base + which]] + [sent[number][which] for number in range(1, most_slots)])
         )
-        grads_parts.append(lax.all_to_all(one_stack, "seq", split_axis=2, concat_axis=1, tiled=True))
-    grads_back = jnp.stack(grads_parts, axis=2).reshape(4, seq_count * most_slots, 1, token_count, head_dim)
-    all_back = (grads_back[0], grads_back[1], grads_back[2], grads_back[3])
     attn_out = heads_to_tokens(all_back[0], select, token_count, head_count, head_dim)
     query_grad = heads_to_tokens(all_back[1], select, token_count, head_count, head_dim)
     key_grad = heads_to_tokens(all_back[2], select, token_count, head_count, head_dim)

time: 352 us -> 351 us (level)
  blocking collectives: 37.4 us -> 0 us
  waiting for transfers between devices: 100 us -> 136 us
  Pallas kernels: 85.4 us -> 72.5 us
  local copies, waits for them, and re-layouts: 54.7 us -> 62.4 us
  starting transfers between devices: 20.1 us -> 26.6 us
    all_to_all x1 -> x0, blocking collectives: 37.4 us -> none  [on_device(): lax.all_to_all(one_stack, 'seq', split_axis=2, concat_axis=1, tiled=True)]
    all_to_all x1 -> x2, waiting for transfers between devices: 0.01 us -> 33.1 us  [to_owners(): lax.all_to_all(one_stack, 'seq', split_axis=1, concat_axis=1, tiled=True)]
    pallas_call x2, Pallas kernels: 55.2 us -> 41.8 us  [attn_backward(): pl.pallas_call(functools.partial(_bwd_kernel, nb=nb, scale=scale), grid=(...]
    another operation x0 -> x8, local copies, waits for them, and re-layouts: none -> 10.1 us  [the longest x6 8.05 us: merged(): jnp.stack(pieces, axis=1)]
    unnamed x31 -> x41, local copies, waits for them, and re-layouts: 22.7 us -> 31.9 us
    slice x8 -> x0, local copies, waits for them, and re-layouts: 8.12 us -> none  [the longest x4 4.32 us: on_device(): all_back = (grads_back[0], grads_back[1], grads_back[2], grads_back[3])]
    all_to_all x1 -> x2, starting transfers between devices: 4.55 us -> 11 us  [to_owners(): lax.all_to_all(one_stack, 'seq', split_axis=1, concat_axis=1, tiled=True)]
  transfers between devices with their start and end apart: 5 -> 6, of which waited for: 3 -> 4; matrix products, arithmetic and copies ran while one was open for 21% -> 23% of each run, Pallas kernels for 16% -> 15%
where the time goes in v8:
time: 351 us; the launch traced here: 347 us
  waiting for transfers between devices  136 us (39%)
  Pallas kernels  72.5 us (21%)
  local copies, waits for them, and re-layouts  62.4 us (18%)
  matrix products  28.5 us (8%)
  starting transfers between devices  26.6 us (8%)
  between operations  14.3 us (4%)
  other arithmetic  7.44 us (2%)
    all_to_all x1, waiting for transfers between devices, on_device(): lax.all_to_all(stacked, 'seq', split_axis=0, concat_axis=3, tiled=True)[0]  64.3 us
    pallas_call x2, Pallas kernels, attn_backward(): pl.pallas_call(functools.partial(_bwd_kernel, nb=nb, scale=scale), grid=(...  41.8 us
    all_to_all x2, waiting for transfers between devices, to_owners(): lax.all_to_all(one_stack, 'seq', split_axis=1, concat_axis=1, tiled=True)  33.1 us
    unnamed x41, local copies, waits for them, and re-layouts  31.9 us
    pallas_call x1, Pallas kernels, attn_forward(): pl.pallas_call(functools.partial(_fwd_kernel, scale=scale), grid=(slots,...  30.8 us
    all_to_all x1, waiting for transfers between devices, on_device(): lax.all_to_all(weight_copies, 'dp', split_axis=0, concat_axis=0, tiled=True)  26.1 us
    dot_general x1, matrix products, on_device(): jnp.einsum('sth,td->shd', slot_out, dy_rows, preferred_element_type=jnp.f...  14.1 us
    all_gather x1, waiting for transfers between devices, on_device(): dy_rows = lax.all_gather(grad_out, 'seq', axis=1, tiled=True)[0]  11.5 us
  transfers between devices with their start and end apart: 6, of which 4 were waited for; matrix products, arithmetic and copies ran while one was open for 23% of the time, Pallas kernels for 15%

profile of v8, /device:TPU:1, one launch (start us, length us, event | category | flops | bytes accessed | tf_op | source)
XLA Modules:
  0.0 347.5 jit_solution(17275683430538794779)
XLA Ops:
  7.9 2.8 broadcast_in_dim.15
  10.7 6.1 %all-to-all-start.1 = ((bf16[8,2,128,640]{3,2,1,0:T(8,128)(2,1)}), bf16[8,2,128,640]{3,2,1,0:T(8,128)(2,1)S(1)}, u32[]{:S(2)}, u32[]{:S(2)}) async-start(bf16[8,2,128,640]{3,2,1,0:T(8,128)(2,1)} %broadcast_in_dim.15), calls=%async_computation.1 | async-start | bytes 5242880 | tf_op jit(solution)/shard_map/all_to_all | solution.py:147
  17.8 1.5 copy.155
  20.1 1.4 copy.160
  21.5 2.2 copy.156
  23.6 1.6 copy.157
  25.8 1.4 copy.161
  27.2 2.2 copy.158
  29.4 1.5 copy.159
  32.4 2.0 pad_maximum_fusion
  34.4 26.1 %all-to-all-done.1 = bf16[8,2,128,640]{3,2,1,0:T(8,128)(2,1)S(1)} async-done(((bf16[8,2,128,640]{3,2,1,0:T(8,128)(2,1)}), bf16[8,2,128,640]{3,2,1,0:T(8,128)(2,1)S(1)}, u32[]{:S(2)}, u32[]{:S(2)}) %all-to-all-start.1) | async-done | bytes 2621472 | tf_op jit(solution)/shard_map/all_to_all | solution.py:147
  60.5 1.5 copy-done.1
  62.0 9.3 %all-to-all-start = ((bf16[16,3,2,128,128]{4,3,2,1,0:T(8,128)(2,1)}), bf16[16,3,2,128,128]{4,3,2,1,0:T(8,128)(2,1)S(1)}, u32[]{:S(2)}, u32[]{:S(2)}) async-start(bf16[16,3,2,128,128]{4,3,2,1,0:T(8,128)(2,1)} %pad_maximum_fusion), calls=%async_computation | async-start | bytes 6291456 | tf_op jit(solution)/shard_map/all_to_all | solution.py:141
  71.8 3.7 %copy.205 = bf16[8,2,16,8,640]{4,3,0,2,1:T(8,128)(2,1)} copy(bf16[8,2,16,8,640]{4,3,2,1,0:T(8,128)(2,1)} %bitcast.140) | data formatting | bytes 5242880 | tf_op jit(solution)/shard_map/reshape | solution.py:153
  75.4 64.3 %all-to-all-done = bf16[16,3,2,128,128]{4,3,2,1,0:T(8,128)(2,1)S(1)} async-done(((bf16[16,3,2,128,128]{4,3,2,1,0:T(8,128)(2,1)}), bf16[16,3,2,128,128]{4,3,2,1,0:T(8,128)(2,1)S(1)}, u32[]{:S(2)}, u32[]{:S(2)}) %all-to-all-start) | async-done | bytes 3145760 | tf_op jit(solution)/shard_map/all_to_all | solution.py:141
  144.1 30.8 %shard_map.110 = (bf16[2,2048,128]{2,1,0:T(8,128)(2,1)}, f32[2,2048,2048]{2,1,0:T(8,128)}) custom-call(bf16[2,2048,128]{2,1,0:T(8,128)(2,1)} %bitcast.135, bf16[2,2048,128]{2,1,0:T(8,128)(2,1)} %bitcast.132, bf16[2,2048,128]{2,1,0:T(8,128)(2,1)} %bitcast.129, f32[2,16,1,2048]{3,2,1,0:T(1,128)} %bitcast.160), custom_call_target="tpu_custom_call" | custom-call | tf_op jit(solution)/shard_map/pallas_call | solution.py:68
  174.9 11.5 %all-gather.2.cloned.1.call-done = bf16[1,2048,5120]{2,1,0:T(8,128)(2,1)} async-done(((bf16[1,128,5120]{2,1,0:T(8,128)(2,1)}), bf16[1,2048,5120]{2,1,0:T(8,128)(2,1)}) %all-gather.2.cloned.1.call-update) | async-done | bytes 20971536 | tf_op jit(solution)/shard_map/all_gather | solution.py:156
  186.4 10.7 %fusion.13.do_ref = bf16[2,2048,128]{2,1,0:T(8,128)(2,1)} fusion(bf16[2,128,5120]{2,1,0:T(8,128)(2,1)S(1)} %bitcast.149, bf16[1,2048,5120]{2,1,0:T(8,128)(2,1)} %all-gather.2.cloned.1.call-done), kind=kOutput, calls=%fused_computation.9 | convolution fusion | flops 5369233408 | bytes 24641536 | tf_op jit(solution)/shard_map/td,shd->sth/dot_general | solution.py:157
  197.1 20.8 %shard_map.112 = (bf16[1,2048,128]{2,1,0:T(8,128)(2,1)}, bf16[1,2048,128]{2,1,0:T(8,128)(2,1)}, bf16[1,2048,128]{2,1,0:T(8,128)(2,1)}) custom-call(bf16[2,2048,128]{2,1,0:T(8,128)(2,1)} %bitcast.136, bf16[2,2048,128]{2,1,0:T(8,128)(2,1)} %bitcast.133, bf16[2,2048,128]{2,1,0:T(8,128)(2,1)} %bitcast.130, f32[2,2048,2048]{2,1,0:T(8,128)} %get-tuple-element.14.p_ref, ...), custom_call_target="tpu_custom_call" | custom-call | tf_op jit(solution)/shard_map/pallas_call | solution.py:90
  217.9 2.8 pad_maximum_fusion.1
  220.7 3.8 %all-to-all-start.3 = ((bf16[3,16,128,128]{3,2,0,1:T(8,128)(2,1)}), bf16[3,16,128,128]{3,2,0,1:T(8,128)(2,1)S(1)}, u32[]{:S(2)}, u32[]{:S(2)}) async-start(bf16[3,16,128,128]{3,2,0,1:T(8,128)(2,1)} %pad_maximum_fusion.1), calls=%async_computation.3 | async-start | bytes 3145728 | tf_op jit(solution)/shard_map/all_to_all | solution.py:168
  224.7 14.1 %fusion.7 = bf16[2,128,5120]{2,1,0:T(8,128)(2,1)} fusion(bf16[2,2048,128]{2,1,0:T(8,128)(2,1)S(1)} %copy-done, bf16[1,2048,5120]{2,1,0:T(8,128)(2,1)} %all-gather.2.cloned.1.call-done), kind=kOutput, calls=%fused_computation.5 | convolution fusion | flops 5371330560 | bytes 24641536 | tf_op jit(solution)/shard_map/sth,td->shd/dot_general | solution.py:161
  238.8 7.4 %copy.199 = bf16[2,128,5120]{1,0,2:T(2,128)(2,1)} copy(bf16[2,128,5120]{2,1,0:T(8,128)(2,1)} %fusion.7) | data formatting | bytes 5242880
  246.2 3.5 %copy.208 = bf16[640,8,2,128]{3,1,2,0:T(8,128)(2,1)} copy(bf16[640,8,2,128]{3,2,1,0:T(2,128)(2,1)} %bitcast.141) | data formatting | bytes 5242880
  251.6 21.0 %shard_map.111 = (bf16[1,2048,128]{2,1,0:T(8,128)(2,1)}, bf16[1,2048,128]{2,1,0:T(8,128)(2,1)}, bf16[1,2048,128]{2,1,0:T(8,128)(2,1)}) custom-call(bf16[2,2048,128]{2,1,0:T(8,128)(2,1)} %bitcast.137, bf16[2,2048,128]{2,1,0:T(8,128)(2,1)} %bitcast.134, bf16[2,2048,128]{2,1,0:T(8,128)(2,1)} %bitcast.131, f32[2,2048,2048]{2,1,0:T(8,128)} %get-tuple-element.14.p_ref, ...), custom_call_target="tpu_custom_call" | custom-call | tf_op jit(solution)/shard_map/pallas_call | solution.py:90
  272.6 2.0 constant_dynamic-update-slice_fusion.2
  274.5 2.0 constant_dynamic-update-slice_fusion.1
  276.5 2.0 constant_dynamic-update-slice_fusion
  279.6 7.3 %all-to-all-start.2 = ((bf16[5,16,128,128]{3,2,0,1:T(8,128)(2,1)}), bf16[5,16,128,128]{3,2,0,1:T(8,128)(2,1)S(1)}, u32[]{:S(2)}, u32[]{:S(2)}) async-start(bf16[5,16,128,128]{3,2,0,1:T(8,128)(2,1)} %constant_dynamic-update-slice_fusion), calls=%async_computation.2 | async-start | bytes 5242880 | tf_op jit(solution)/shard_map/all_to_all | solution.py:168
  286.9 2.6 slice_bitcast_fusion
  289.4 33.1 %all-to-all-done.2 = bf16[5,16,128,128]{3,2,0,1:T(8,128)(2,1)S(1)} async-done(((bf16[5,16,128,128]{3,2,0,1:T(8,128)(2,1)}), bf16[5,16,128,128]{3,2,0,1:T(8,128)(2,1)S(1)}, u32[]{:S(2)}, u32[]{:S(2)}) %all-to-all-start.2) | async-done | bytes 2621472 | tf_op jit(solution)/shard_map/all_to_all | solution.py:168
  330.4 1.2 pad_maximum_fusion.2
  (73 shorter events, 29.5 us)
Async XLA Ops:
  7.2 179.2 %all-gather.2.cloned.1.call-start = ((), (), s32[]{:S(2)}) async-start(), calls=%async_computation.5 | async-start | bytes 22282240 | tf_op jit(solution)/shard_map/all_gather | solution.py:156
  10.7 6.1 %copy-start.10 = (bf16[1,128,2560]{2,1,0:T(8,128)(2,1)S(1)}, bf16[1,128,2560]{2,1,0:T(8,128)(2,1)}, u32[]{:S(2)}) copy-start(bf16[1,128,2560]{2,1,0:T(8,128)(2,1)} %param.7) | copy-start | bytes 1966084
  10.7 49.8 %all-to-all-start.1 = ((bf16[8,2,128,640]{3,2,1,0:T(8,128)(2,1)}), bf16[8,2,128,640]{3,2,1,0:T(8,128)(2,1)S(1)}, u32[]{:S(2)}, u32[]{:S(2)}) async-start(bf16[8,2,128,640]{3,2,1,0:T(8,128)(2,1)} %broadcast_in_dim.15), calls=%async_computation.1 | async-start | bytes 5242880 | tf_op jit(solution)/shard_map/all_to_all | solution.py:147
  16.8 2.6 copy-start.12
  30.9 1.2 copy-start.3
  30.9 1.5 copy-start.4
  34.4 37.0 %copy-start.11 = (s32[20,16,16]{0,2,1:T(8,128)S(1)}, s32[20,16,16]{0,2,1:T(8,128)}, u32[]{:S(2)}) copy-start(s32[20,16,16]{0,2,1:T(8,128)} %param.12) | copy-start | bytes 61444
  60.5 1.5 copy-start.1
  62.0 77.8 %all-to-all-start = ((bf16[16,3,2,128,128]{4,3,2,1,0:T(8,128)(2,1)}), bf16[16,3,2,128,128]{4,3,2,1,0:T(8,128)(2,1)S(1)}, u32[]{:S(2)}, u32[]{:S(2)}) async-start(bf16[16,3,2,128,128]{4,3,2,1,0:T(8,128)(2,1)} %pad_maximum_fusion), calls=%async_computation | async-start | bytes 6291456 | tf_op jit(solution)/shard_map/all_to_all | solution.py:141
  142.2 44.2 %copy-start.5 = (bf16[8,2,16,8,640]{4,3,0,2,1:T(8,128)(2,1)S(1)}, bf16[8,2,16,8,640]{4,3,0,2,1:T(8,128)(2,1)}, u32[]{:S(2)}) copy-start(bf16[8,2,16,8,640]{4,3,0,2,1:T(8,128)(2,1)} %copy.205) | copy-start | bytes 7864324
  217.9 6.8 %copy-start = (bf16[2,2048,128]{2,1,0:T(8,128)(2,1)S(1)}, bf16[2,2048,128]{2,1,0:T(8,128)(2,1)}, u32[]{:S(2)}) copy-start(bf16[2,2048,128]{2,1,0:T(8,128)(2,1)} %get-tuple-element.13.o_ref) | copy-start | bytes 3145732
  220.7 57.7 %all-to-all-start.3 = ((bf16[3,16,128,128]{3,2,0,1:T(8,128)(2,1)}), bf16[3,16,128,128]{3,2,0,1:T(8,128)(2,1)S(1)}, u32[]{:S(2)}, u32[]{:S(2)}) async-start(bf16[3,16,128,128]{3,2,0,1:T(8,128)(2,1)} %pad_maximum_fusion.1), calls=%async_computation.3 | async-start | bytes 3145728 | tf_op jit(solution)/shard_map/all_to_all | solution.py:168
  224.4 113.3 %reduce-scatter.4.cloned.1.call-start = ((), (), s32[]{:S(2)}) async-start(), calls=%async_computation.6 | async-start | bytes 2949120
  278.4 1.2 copy-start.2
  279.6 43.0 %all-to-all-start.2 = ((bf16[5,16,128,128]{3,2,0,1:T(8,128)(2,1)}), bf16[5,16,128,128]{3,2,0,1:T(8,128)(2,1)S(1)}, u32[]{:S(2)}, u32[]{:S(2)}) async-start(bf16[5,16,128,128]{3,2,0,1:T(8,128)(2,1)} %constant_dynamic-update-slice_fusion), calls=%async_computation.2 | async-start | bytes 5242880 | tf_op jit(solution)/shard_map/all_to_all | solution.py:168
  322.6 1.2 copy-start.8
  322.6 1.4 copy-start.9
  328.3 2.0 copy-start.6
  328.3 2.0 copy-start.7
Sparse Core Ops, SparseCore 0:
  10.4 175.8 all-gather.1
  249.9 40.4 reduce-scatter.3

commit v9 on v8

--- a/solution.py
+++ b/solution.py
@@ -159,7 +159,7 @@
     ).astype(jnp.bfloat16)
     grad_attn = part
     weight_total = jnp.einsum("sth,td->shd", slot_out, dy_rows, preferred_element_type=jnp.float32)
-    grad_attn, weight_total = (grad_attn, weight_total)
+    grad_attn, weight_total = lax.optimization_barrier((grad_attn, weight_total))
     weight_grad = lax.psum_scatter(
         (weight_total * grad_scale).astype(jnp.bfloat16), "dp", scatter_dimension=2, tiled=True
     ).astype(jnp.float32)

time: 351 us -> 348 us (level)
  local copies, waits for them, and re-layouts: 62.4 us -> 56.7 us
  matrix products: 28.5 us -> 24.3 us
  other arithmetic: 7.44 us -> 11.6 us
    dot_general x1, matrix products: 14.1 us -> 7.46 us  [on_device(): jnp.einsum('sth,td->shd', slot_out, dy_rows, preferred_element_type=jnp.f...]
    unnamed x41 -> x45, local copies, waits for them, and re-layouts: 31.9 us -> 27 us
    convert_element_type x0 -> x1, other arithmetic: none -> 4.35 us  [on_device(): (weight_total * grad_scale).astype(jnp.bfloat16)]
  transfers between devices with their start and end apart: 6 -> 6, of which waited for: 4 -> 4; matrix products, arithmetic and copies ran while one was open for 23% -> 18% of each run, Pallas kernels for 15% -> 15%
where the time goes in v9:
time: 348 us; the launch traced here: 345 us
  waiting for transfers between devices  139 us (40%)
  Pallas kernels  72.5 us (21%)
  local copies, waits for them, and re-layouts  56.7 us (16%)
  starting transfers between devices  27.1 us (8%)
  matrix products  24.3 us (7%)
  between operations  14.3 us (4%)
  other arithmetic  11.6 us (3%)
    all_to_all x1, waiting for transfers between devices, on_device(): lax.all_to_all(stacked, 'seq', split_axis=0, concat_axis=3, tiled=True)[0]  64.3 us
    pallas_call x2, Pallas kernels, attn_backward(): pl.pallas_call(functools.partial(_bwd_kernel, nb=nb, scale=scale), grid=(...  41.7 us
    all_to_all x2, waiting for transfers between devices, to_owners(): lax.all_to_all(one_stack, 'seq', split_axis=1, concat_axis=1, tiled=True)  36.2 us
    pallas_call x1, Pallas kernels, attn_forward(): pl.pallas_call(functools.partial(_fwd_kernel, scale=scale), grid=(slots,...  30.8 us
    unnamed x45, local copies, waits for them, and re-layouts  27 us
    all_to_all x1, waiting for transfers between devices, on_device(): lax.all_to_all(weight_copies, 'dp', split_axis=0, concat_axis=0, tiled=True)  26.1 us
    dot_general x1, matrix products, on_device(): jnp.einsum('td,shd->sth', dy_rows, weight_full, preferred_element_type=jn...  13.2 us
    all_to_all x2, starting transfers between devices, to_owners(): lax.all_to_all(one_stack, 'seq', split_axis=1, concat_axis=1, tiled=True)  11.7 us
  transfers between devices with their start and end apart: 6, of which 4 were waited for; matrix products, arithmetic and copies ran while one was open for 18% of the time, Pallas kernels for 15%

profile of v9, /device:TPU:1, one launch (start us, length us, event | category | flops | bytes accessed | tf_op | source)
XLA Modules:
  0.0 345.3 jit_solution(948302143642773406)
XLA Ops:
  7.9 2.8 broadcast_in_dim.15
  10.7 6.1 %all-to-all-start.1 = ((bf16[8,2,128,640]{3,2,1,0:T(8,128)(2,1)}), bf16[8,2,128,640]{3,2,1,0:T(8,128)(2,1)S(1)}, u32[]{:S(2)}, u32[]{:S(2)}) async-start(bf16[8,2,128,640]{3,2,1,0:T(8,128)(2,1)} %broadcast_in_dim.15), calls=%async_computation.1 | async-start | bytes 5242880 | tf_op jit(solution)/shard_map/all_to_all | solution.py:147
  17.8 1.5 copy.155
  20.1 1.4 copy.160
  21.5 2.2 copy.156
  23.6 1.6 copy.157
  25.8 1.4 copy.161
  27.2 2.2 copy.158
  29.3 1.5 copy.159
  32.4 2.0 pad_maximum_fusion
  34.4 26.1 %all-to-all-done.1 = bf16[8,2,128,640]{3,2,1,0:T(8,128)(2,1)S(1)} async-done(((bf16[8,2,128,640]{3,2,1,0:T(8,128)(2,1)}), bf16[8,2,128,640]{3,2,1,0:T(8,128)(2,1)S(1)}, u32[]{:S(2)}, u32[]{:S(2)}) %all-to-all-start.1) | async-done | bytes 2621472 | tf_op jit(solution)/shard_map/all_to_all | solution.py:147
  60.5 1.5 copy-done.3
  62.0 9.3 %all-to-all-start = ((bf16[16,3,2,128,128]{4,3,2,1,0:T(8,128)(2,1)}), bf16[16,3,2,128,128]{4,3,2,1,0:T(8,128)(2,1)S(1)}, u32[]{:S(2)}, u32[]{:S(2)}) async-start(bf16[16,3,2,128,128]{4,3,2,1,0:T(8,128)(2,1)} %pad_maximum_fusion), calls=%async_computation | async-start | bytes 6291456 | tf_op jit(solution)/shard_map/all_to_all | solution.py:141
  71.8 3.6 %copy.205 = bf16[8,2,16,8,640]{4,3,0,2,1:T(8,128)(2,1)} copy(bf16[8,2,16,8,640]{4,3,2,1,0:T(8,128)(2,1)} %bitcast.136) | data formatting | bytes 5242880 | tf_op jit(solution)/shard_map/reshape | solution.py:153
  75.4 64.3 %all-to-all-done = bf16[16,3,2,128,128]{4,3,2,1,0:T(8,128)(2,1)S(1)} async-done(((bf16[16,3,2,128,128]{4,3,2,1,0:T(8,128)(2,1)}), bf16[16,3,2,128,128]{4,3,2,1,0:T(8,128)(2,1)S(1)}, u32[]{:S(2)}, u32[]{:S(2)}) %all-to-all-start) | async-done | bytes 3145760 | tf_op jit(solution)/shard_map/all_to_all | solution.py:141
  144.1 30.8 %shard_map.110 = (bf16[2,2048,128]{2,1,0:T(8,128)(2,1)}, f32[2,2048,2048]{2,1,0:T(8,128)}) custom-call(bf16[2,2048,128]{2,1,0:T(8,128)(2,1)} %bitcast.131, bf16[2,2048,128]{2,1,0:T(8,128)(2,1)} %bitcast.128, bf16[2,2048,128]{2,1,0:T(8,128)(2,1)} %bitcast.125, f32[2,16,1,2048]{3,2,1,0:T(1,128)} %bitcast.156), custom_call_target="tpu_custom_call" | custom-call | tf_op jit(solution)/shard_map/pallas_call | solution.py:68
  174.9 11.5 %all-gather.2.cloned.1.call-done = bf16[1,2048,5120]{2,1,0:T(8,128)(2,1)} async-done(((bf16[1,128,5120]{2,1,0:T(8,128)(2,1)}), bf16[1,2048,5120]{2,1,0:T(8,128)(2,1)}) %all-gather.2.cloned.1.call-update) | async-done | bytes 20971536 | tf_op jit(solution)/shard_map/all_gather | solution.py:156
  186.4 13.2 %fusion.7.do_ref = bf16[2,2048,128]{2,1,0:T(8,128)(2,1)} fusion(bf16[2,128,5120]{2,1,0:T(8,128)(2,1)S(1)} %bitcast.145, bf16[1,2048,5120]{2,1,0:T(8,128)(2,1)} %all-gather.2.cloned.1.call-done), kind=kOutput, calls=%fused_computation.8 | convolution fusion | flops 5369233408 | bytes 24641536 | tf_op jit(solution)/shard_map/td,shd->sth/dot_general | solution.py:157
  199.8 7.5 %fusion = f32[2,128,5120]{2,1,0:T(8,128)} fusion(bf16[2,2048,128]{2,1,0:T(8,128)(2,1)S(1)} %copy-done.1, bf16[1,2048,5120]{2,1,0:T(8,128)(2,1)S(1)} %copy-done), kind=kOutput, calls=%fused_computation | convolution fusion | flops 5368709120 | bytes 27262976 | tf_op jit(solution)/shard_map/sth,td->shd/dot_general | solution.py:161
  207.2 20.8 %shard_map.112 = (bf16[1,2048,128]{2,1,0:T(8,128)(2,1)}, bf16[1,2048,128]{2,1,0:T(8,128)(2,1)}, bf16[1,2048,128]{2,1,0:T(8,128)(2,1)}) custom-call(bf16[2,2048,128]{2,1,0:T(8,128)(2,1)} %bitcast.132, bf16[2,2048,128]{2,1,0:T(8,128)(2,1)} %bitcast.129, bf16[2,2048,128]{2,1,0:T(8,128)(2,1)} %bitcast.126, f32[2,2048,2048]{2,1,0:T(8,128)} %get-tuple-element.16.p_ref, ...), custom_call_target="tpu_custom_call" | custom-call | tf_op jit(solution)/shard_map/pallas_call | solution.py:90
  228.0 2.7 pad_maximum_fusion.1
  230.7 4.4 %all-to-all-start.3 = ((bf16[3,16,128,128]{3,2,0,1:T(8,128)(2,1)}), bf16[3,16,128,128]{3,2,0,1:T(8,128)(2,1)}, u32[]{:S(2)}, u32[]{:S(2)}) async-start(bf16[3,16,128,128]{3,2,0,1:T(8,128)(2,1)} %pad_maximum_fusion.1), calls=%async_computation.3 | async-start | bytes 3145728 | tf_op jit(solution)/shard_map/all_to_all | solution.py:168
  235.2 4.3 %multiply_convert_fusion = bf16[2,128,5120]{2,1,0:T(8,128)(2,1)} fusion(f32[2,128,5120]{2,1,0:T(8,128)} %fusion), kind=kLoop, calls=%fused_computation.4 | loop fusion | flops 2621440 | bytes 7864320 | tf_op jit(solution)/shard_map/convert_element_type | solution.py:164
  239.5 5.9 %copy.199 = bf16[2,128,5120]{1,0,2:T(2,128)(2,1)S(1)} copy(bf16[2,128,5120]{2,1,0:T(8,128)(2,1)} %multiply_convert_fusion) | data formatting | bytes 5242880
  245.4 1.8 copy.208
  247.2 1.2 copy-done.2
  248.6 20.9 %shard_map.111 = (bf16[1,2048,128]{2,1,0:T(8,128)(2,1)}, bf16[1,2048,128]{2,1,0:T(8,128)(2,1)}, bf16[1,2048,128]{2,1,0:T(8,128)(2,1)}) custom-call(bf16[2,2048,128]{2,1,0:T(8,128)(2,1)} %bitcast.133, bf16[2,2048,128]{2,1,0:T(8,128)(2,1)} %bitcast.130, bf16[2,2048,128]{2,1,0:T(8,128)(2,1)} %bitcast.127, f32[2,2048,2048]{2,1,0:T(8,128)} %get-tuple-element.16.p_ref, ...), custom_call_target="tpu_custom_call" | custom-call | tf_op jit(solution)/shard_map/pallas_call | solution.py:90
  272.9 1.5 copy-done.6
  274.4 7.3 %all-to-all-start.2 = ((bf16[5,16,128,128]{3,2,0,1:T(8,128)(2,1)}), bf16[5,16,128,128]{3,2,0,1:T(8,128)(2,1)S(1)}, u32[]{:S(2)}, u32[]{:S(2)}) async-start(bf16[5,16,128,128]{3,2,0,1:T(8,128)(2,1)} %copy-done.6), calls=%async_computation.2 | async-start | bytes 5242880 | tf_op jit(solution)/shard_map/all_to_all | solution.py:168
  281.7 2.6 slice_bitcast_fusion
  284.3 36.2 %all-to-all-done.2 = bf16[5,16,128,128]{3,2,0,1:T(8,128)(2,1)S(1)} async-done(((bf16[5,16,128,128]{3,2,0,1:T(8,128)(2,1)}), bf16[5,16,128,128]{3,2,0,1:T(8,128)(2,1)S(1)}, u32[]{:S(2)}, u32[]{:S(2)}) %all-to-all-start.2) | async-done | bytes 2621472 | tf_op jit(solution)/shard_map/all_to_all | solution.py:168
  328.3 1.2 pad_maximum_fusion.2
  (78 shorter events, 30.0 us)
Async XLA Ops:
  7.2 179.2 %all-gather.2.cloned.1.call-start = ((), (), s32[]{:S(2)}) async-start(), calls=%async_computation.5 | async-start | bytes 22282240 | tf_op jit(solution)/shard_map/all_gather | solution.py:156
  10.7 6.1 %copy-start.12 = (bf16[1,128,2560]{2,1,0:T(8,128)(2,1)S(1)}, bf16[1,128,2560]{2,1,0:T(8,128)(2,1)}, u32[]{:S(2)}) copy-start(bf16[1,128,2560]{2,1,0:T(8,128)(2,1)} %param.7) | copy-start | bytes 1966084
  10.7 49.8 %all-to-all-start.1 = ((bf16[8,2,128,640]{3,2,1,0:T(8,128)(2,1)}), bf16[8,2,128,640]{3,2,1,0:T(8,128)(2,1)S(1)}, u32[]{:S(2)}, u32[]{:S(2)}) async-start(bf16[8,2,128,640]{3,2,1,0:T(8,128)(2,1)} %broadcast_in_dim.15), calls=%async_computation.1 | async-start | bytes 5242880 | tf_op jit(solution)/shard_map/all_to_all | solution.py:147
  16.8 2.6 copy-start.14
  30.8 1.2 copy-start.4
  30.9 1.5 copy-start.5
  34.4 37.1 %copy-start.13 = (s32[20,16,16]{0,2,1:T(8,128)S(1)}, s32[20,16,16]{0,2,1:T(8,128)}, u32[]{:S(2)}) copy-start(s32[20,16,16]{0,2,1:T(8,128)} %param.12) | copy-start | bytes 61444
  60.5 1.5 copy-start.3
  62.0 77.8 %all-to-all-start = ((bf16[16,3,2,128,128]{4,3,2,1,0:T(8,128)(2,1)}), bf16[16,3,2,128,128]{4,3,2,1,0:T(8,128)(2,1)S(1)}, u32[]{:S(2)}, u32[]{:S(2)}) async-start(bf16[16,3,2,128,128]{4,3,2,1,0:T(8,128)(2,1)} %pad_maximum_fusion), calls=%async_computation | async-start | bytes 6291456 | tf_op jit(solution)/shard_map/all_to_all | solution.py:141
  142.2 44.2 %copy-start.7 = (bf16[8,2,16,8,640]{4,3,0,2,1:T(8,128)(2,1)S(1)}, bf16[8,2,16,8,640]{4,3,0,2,1:T(8,128)(2,1)}, u32[]{:S(2)}) copy-start(bf16[8,2,16,8,640]{4,3,0,2,1:T(8,128)(2,1)} %copy.205) | copy-start | bytes 7864324
  186.4 13.2 %copy-start = (bf16[1,2048,5120]{2,1,0:T(8,128)(2,1)S(1)}, bf16[1,2048,5120]{2,1,0:T(8,128)(2,1)}, u32[]{:S(2)}) copy-start(bf16[1,2048,5120]{2,1,0:T(8,128)(2,1)} %all-gather.2.cloned.1.call-done) | copy-start | bytes 62914564
  186.4 13.4 %copy-start.1 = (bf16[2,2048,128]{2,1,0:T(8,128)(2,1)S(1)}, bf16[2,2048,128]{2,1,0:T(8,128)(2,1)}, u32[]{:S(2)}) copy-start(bf16[2,2048,128]{2,1,0:T(8,128)(2,1)} %get-tuple-element.15.o_ref) | copy-start | bytes 3145732
  230.7 43.7 %all-to-all-start.3 = ((bf16[3,16,128,128]{3,2,0,1:T(8,128)(2,1)}), bf16[3,16,128,128]{3,2,0,1:T(8,128)(2,1)}, u32[]{:S(2)}, u32[]{:S(2)}) async-start(bf16[3,16,128,128]{3,2,0,1:T(8,128)(2,1)} %pad_maximum_fusion.1), calls=%async_computation.3 | async-start | bytes 3145728 | tf_op jit(solution)/shard_map/all_to_all | solution.py:168
  235.1 100.5 %reduce-scatter.4.cloned.1.call-start = ((), (), s32[]{:S(2)}) async-start(), calls=%async_computation.6 | async-start | bytes 2949120
  247.2 1.2 copy-start.2
  272.9 1.5 copy-start.6
  274.4 46.0 %all-to-all-start.2 = ((bf16[5,16,128,128]{3,2,0,1:T(8,128)(2,1)}), bf16[5,16,128,128]{3,2,0,1:T(8,128)(2,1)S(1)}, u32[]{:S(2)}, u32[]{:S(2)}) async-start(bf16[5,16,128,128]{3,2,0,1:T(8,128)(2,1)} %copy-done.6), calls=%async_computation.2 | async-start | bytes 5242880 | tf_op jit(solution)/shard_map/all_to_all | solution.py:168
  320.4 1.2 copy-start.10
  320.4 1.4 copy-start.11
  326.2 2.0 copy-start.8
  326.2 2.0 copy-start.9
Sparse Core Ops, SparseCore 0:
  10.4 175.8 all-gather.1
  247.3 42.7 reduce-scatter.3

commit v10 on v9

--- a/solution.py
+++ b/solution.py
@@ -107,9 +107,9 @@
     return slot_index[:, None] == jnp.arange(seq_count * most_slots, dtype=jnp.int32)[None, :]
 
 
-def heads_to_tokens(received, select, token_count, head_count, head_dim):
-    merged = jnp.einsum("jtd,hj->thd", received[:, 0], select, preferred_element_type=jnp.float32)
-    return merged.astype(jnp.bfloat16).reshape(1, token_count, head_count * head_dim)
+def heads_to_tokens(received, head_slots, token_count, head_count, head_dim):
+    picked = jnp.take(received[:, 0], head_slots, axis=0)
+    return jnp.transpose(picked, (1, 0, 2)).reshape(1, token_count, head_count * head_dim)
 
 
 def on_device(query_tok, key_tok, value_tok, grad_out, out_weight, block_mask, head_owner):
@@ -122,6 +122,7 @@
     score_scale = head_dim ** (-0.5)
     grad_scale = (lax.axis_size("dp") * length) ** (-0.5)
     table = slot_table(head_owner, most_slots, seq_count)
+    head_slots = jnp.argmax(table, axis=1).astype(jnp.int32)
     select = table.astype(jnp.bfloat16)
     my_first = lax.axis_index("seq") * most_slots
     local_select = lax.dynamic_slice_in_dim(table.astype(jnp.float32), my_first, most_slots, 1)
@@ -186,10 +187,10 @@
         all_back.append(
             merged([sent[0][base + which]] + [sent[number][which] for number in range(1, most_slots)])
         )
-    attn_out = heads_to_tokens(all_back[0], select, token_count, head_count, head_dim)
-    query_grad = heads_to_tokens(all_back[1], select, token_count, head_count, head_dim)
-    key_grad = heads_to_tokens(all_back[2], select, token_count, head_count, head_dim)
-    value_grad = heads_to_tokens(all_back[3], select, token_count, head_count, head_dim)
+    attn_out = heads_to_tokens(all_back[0], head_slots, token_count, head_count, head_dim)
+    query_grad = heads_to_tokens(all_back[1], head_slots, token_count, head_count, head_dim)
+    key_grad = heads_to_tokens(all_back[2], head_slots, token_count, head_count, head_dim)
+    value_grad = heads_to_tokens(all_back[3], head_slots, token_count, head_count, head_dim)
     return (attn_out, query_grad, key_grad, value_grad, weight_grad)
 
 

time: 348 us -> 348 us (level)
  waiting for transfers between devices: 139 us -> 134 us
  other arithmetic: 11.6 us -> 15.4 us
    all_to_all x2, waiting for transfers between devices: 36.2 us -> 31.4 us  [to_owners(): lax.all_to_all(one_stack, 'seq', split_axis=1, concat_axis=1, tiled=True)]
    another operation x6 -> x2, local copies, waits for them, and re-layouts: 8.06 us -> 3.63 us  [merged(): jnp.stack(pieces, axis=1)]
    gather x0 -> x4, local copies, waits for them, and re-layouts: none -> 4.35 us  [heads_to_tokens(): picked = jnp.take(received[:, 0], head_slots, axis=0)]
    unnamed x45 -> x39, local copies, waits for them, and re-layouts: 27 us -> 28.8 us
  transfers between devices with their start and end apart: 6 -> 6, of which waited for: 4 -> 4; matrix products, arithmetic and copies ran while one was open for 18% -> 17% of each run, Pallas kernels for 15% -> 21%
where the time goes in v10:
time: 348 us; the launch traced here: 345 us
  waiting for transfers between devices  134 us (39%)
  Pallas kernels  72.5 us (21%)
  local copies, waits for them, and re-layouts  59.9 us (17%)
  starting transfers between devices  26.6 us (8%)
  matrix products  22.2 us (6%)
  other arithmetic  15.4 us (4%)
  between operations  14.3 us (4%)
    all_to_all x1, waiting for transfers between devices, on_device(): lax.all_to_all(stacked, 'seq', split_axis=0, concat_axis=3, tiled=True)[0]  64.3 us
    pallas_call x2, Pallas kernels, attn_backward(): pl.pallas_call(functools.partial(_bwd_kernel, nb=nb, scale=scale), grid=(...  41.8 us
    all_to_all x2, waiting for transfers between devices, to_owners(): lax.all_to_all(one_stack, 'seq', split_axis=1, concat_axis=1, tiled=True)  31.4 us
    pallas_call x1, Pallas kernels, attn_forward(): pl.pallas_call(functools.partial(_fwd_kernel, scale=scale), grid=(slots,...  30.7 us
    unnamed x39, local copies, waits for them, and re-layouts  28.8 us
    all_to_all x1, waiting for transfers between devices, on_device(): lax.all_to_all(weight_copies, 'dp', split_axis=0, concat_axis=0, tiled=True)  26.4 us
    dot_general x1, matrix products, on_device(): jnp.einsum('td,shd->sth', dy_rows, weight_full, preferred_element_type=jn...  13.2 us
    all_gather x1, waiting for transfers between devices, on_device(): dy_rows = lax.all_gather(grad_out, 'seq', axis=1, tiled=True)[0]  11.4 us
  transfers between devices with their start and end apart: 6, of which 4 were waited for; matrix products, arithmetic and copies ran while one was open for 17% of the time, Pallas kernels for 21%

profile of v10, /device:TPU:1, one launch (start us, length us, event | category | flops | bytes accessed | tf_op | source)
XLA Modules:
  0.0 345.0 jit_solution(14931446798815649824)
XLA Ops:
  7.9 2.8 broadcast_in_dim.38
  10.7 6.1 %all-to-all-start.1 = ((bf16[8,2,128,640]{3,2,1,0:T(8,128)(2,1)}), bf16[8,2,128,640]{3,2,1,0:T(8,128)(2,1)S(1)}, u32[]{:S(2)}, u32[]{:S(2)}) async-start(bf16[8,2,128,640]{3,2,1,0:T(8,128)(2,1)} %broadcast_in_dim.38), calls=%async_computation.1 | async-start | bytes 5242880 | tf_op jit(solution)/shard_map/all_to_all | solution.py:148
  21.4 2.2 copy.94
  23.5 1.6 copy.96
  27.0 2.2 copy.97
  32.2 2.0 pad_maximum_fusion
  34.2 26.4 %all-to-all-done.1 = bf16[8,2,128,640]{3,2,1,0:T(8,128)(2,1)S(1)} async-done(((bf16[8,2,128,640]{3,2,1,0:T(8,128)(2,1)}), bf16[8,2,128,640]{3,2,1,0:T(8,128)(2,1)S(1)}, u32[]{:S(2)}, u32[]{:S(2)}) %all-to-all-start.1) | async-done | bytes 2621472 | tf_op jit(solution)/shard_map/all_to_all | solution.py:148
  60.6 1.5 copy-done.3
  62.1 9.2 %all-to-all-start = ((bf16[16,3,2,128,128]{4,3,2,1,0:T(8,128)(2,1)}), bf16[16,3,2,128,128]{4,3,2,1,0:T(8,128)(2,1)S(1)}, u32[]{:S(2)}, u32[]{:S(2)}) async-start(bf16[16,3,2,128,128]{4,3,2,1,0:T(8,128)(2,1)} %pad_maximum_fusion), calls=%async_computation | async-start | bytes 6291456 | tf_op jit(solution)/shard_map/all_to_all | solution.py:142
  71.9 3.6 %copy.152 = bf16[8,2,16,8,640]{4,3,0,2,1:T(8,128)(2,1)} copy(bf16[8,2,16,8,640]{4,3,2,1,0:T(8,128)(2,1)} %bitcast.134) | data formatting | bytes 5242880 | tf_op jit(solution)/shard_map/reshape | solution.py:154
  75.6 64.3 %all-to-all-done = bf16[16,3,2,128,128]{4,3,2,1,0:T(8,128)(2,1)S(1)} async-done(((bf16[16,3,2,128,128]{4,3,2,1,0:T(8,128)(2,1)}), bf16[16,3,2,128,128]{4,3,2,1,0:T(8,128)(2,1)S(1)}, u32[]{:S(2)}, u32[]{:S(2)}) %all-to-all-start) | async-done | bytes 3145760 | tf_op jit(solution)/shard_map/all_to_all | solution.py:142
  144.2 30.7 %shard_map.110 = (bf16[2,2048,128]{2,1,0:T(8,128)(2,1)}, f32[2,2048,2048]{2,1,0:T(8,128)}) custom-call(bf16[2,2048,128]{2,1,0:T(8,128)(2,1)} %bitcast.129, bf16[2,2048,128]{2,1,0:T(8,128)(2,1)} %bitcast.126, bf16[2,2048,128]{2,1,0:T(8,128)(2,1)} %bitcast.123, f32[2,16,1,2048]{3,2,1,0:T(1,128)} %bitcast.154), custom_call_target="tpu_custom_call" | custom-call | tf_op jit(solution)/shard_map/pallas_call | solution.py:68
  175.0 11.4 %all-gather.2.cloned.1.call-done = bf16[1,2048,5120]{2,1,0:T(8,128)(2,1)} async-done(((bf16[1,128,5120]{2,1,0:T(8,128)(2,1)}), bf16[1,2048,5120]{2,1,0:T(8,128)(2,1)}) %all-gather.2.cloned.1.call-update) | async-done | bytes 20971536 | tf_op jit(solution)/shard_map/all_gather | solution.py:157
  186.4 13.2 %fusion.7.do_ref = bf16[2,2048,128]{2,1,0:T(8,128)(2,1)} fusion(bf16[2,128,5120]{2,1,0:T(8,128)(2,1)S(1)} %bitcast.143, bf16[1,2048,5120]{2,1,0:T(8,128)(2,1)} %all-gather.2.cloned.1.call-done), kind=kOutput, calls=%fused_computation.12 | convolution fusion | flops 5369233408 | bytes 24641536 | tf_op jit(solution)/shard_map/td,shd->sth/dot_general | solution.py:158
  199.8 7.5 %fusion = f32[2,128,5120]{2,1,0:T(8,128)} fusion(bf16[2,2048,128]{2,1,0:T(8,128)(2,1)S(1)} %copy-done.1, bf16[1,2048,5120]{2,1,0:T(8,128)(2,1)S(1)} %copy-done), kind=kOutput, calls=%fused_computation.4 | convolution fusion | flops 5368709120 | bytes 27262976 | tf_op jit(solution)/shard_map/sth,td->shd/dot_general | solution.py:162
  207.2 4.4 %multiply_convert_fusion = bf16[2,128,5120]{2,1,0:T(8,128)(2,1)} fusion(f32[2,128,5120]{2,1,0:T(8,128)} %fusion), kind=kLoop, calls=%fused_computation.8 | loop fusion | flops 2621440 | bytes 7864320 | tf_op jit(solution)/shard_map/convert_element_type | solution.py:165
  211.6 5.9 %copy.142 = bf16[2,128,5120]{1,0,2:T(2,128)(2,1)S(1)} copy(bf16[2,128,5120]{2,1,0:T(8,128)(2,1)} %multiply_convert_fusion) | data formatting | bytes 5242880
  217.4 1.8 copy.155
  219.3 20.9 %shard_map.112 = (bf16[1,2048,128]{2,1,0:T(8,128)(2,1)}, bf16[1,2048,128]{2,1,0:T(8,128)(2,1)}, bf16[1,2048,128]{2,1,0:T(8,128)(2,1)}) custom-call(bf16[2,2048,128]{2,1,0:T(8,128)(2,1)} %bitcast.130, bf16[2,2048,128]{2,1,0:T(8,128)(2,1)} %bitcast.127, bf16[2,2048,128]{2,1,0:T(8,128)(2,1)} %bitcast.124, f32[2,2048,2048]{2,1,0:T(8,128)} %get-tuple-element.18.p_ref, ...), custom_call_target="tpu_custom_call" | custom-call | tf_op jit(solution)/shard_map/pallas_call | solution.py:90
  240.2 2.8 pad_maximum_fusion.1
  243.0 3.8 %all-to-all-start.3 = ((bf16[3,16,128,128]{3,2,0,1:T(8,128)(2,1)}), bf16[3,16,128,128]{3,2,0,1:T(8,128)(2,1)S(1)}, u32[]{:S(2)}, u32[]{:S(2)}) async-start(bf16[3,16,128,128]{3,2,0,1:T(8,128)(2,1)} %pad_maximum_fusion.1), calls=%async_computation.3 | async-start | bytes 3145728 | tf_op jit(solution)/shard_map/all_to_all | solution.py:169
  248.7 20.9 %shard_map.111 = (bf16[1,2048,128]{2,1,0:T(8,128)(2,1)}, bf16[1,2048,128]{2,1,0:T(8,128)(2,1)}, bf16[1,2048,128]{2,1,0:T(8,128)(2,1)}) custom-call(bf16[2,2048,128]{2,1,0:T(8,128)(2,1)} %bitcast.131, bf16[2,2048,128]{2,1,0:T(8,128)(2,1)} %bitcast.128, bf16[2,2048,128]{2,1,0:T(8,128)(2,1)} %bitcast.125, f32[2,2048,2048]{2,1,0:T(8,128)} %get-tuple-element.18.p_ref, ...), custom_call_target="tpu_custom_call" | custom-call | tf_op jit(solution)/shard_map/pallas_call | solution.py:90
  269.6 2.0 constant_dynamic-update-slice_fusion.2
  271.6 2.0 constant_dynamic-update-slice_fusion.1
  273.6 2.0 constant_dynamic-update-slice_fusion
  276.7 7.3 %all-to-all-start.2 = ((bf16[5,16,128,128]{3,2,0,1:T(8,128)(2,1)}), bf16[5,16,128,128]{3,2,0,1:T(8,128)(2,1)S(1)}, u32[]{:S(2)}, u32[]{:S(2)}) async-start(bf16[5,16,128,128]{3,2,0,1:T(8,128)(2,1)} %constant_dynamic-update-slice_fusion), calls=%async_computation.2 | async-start | bytes 5242880 | tf_op jit(solution)/shard_map/all_to_all | solution.py:169
  284.6 2.5 slice_bitcast_fusion
  287.1 31.4 %all-to-all-done.2 = bf16[5,16,128,128]{3,2,0,1:T(8,128)(2,1)S(1)} async-done(((bf16[5,16,128,128]{3,2,0,1:T(8,128)(2,1)}), bf16[5,16,128,128]{3,2,0,1:T(8,128)(2,1)S(1)}, u32[]{:S(2)}, u32[]{:S(2)}) %all-to-all-start.2) | async-done | bytes 2621472 | tf_op jit(solution)/shard_map/all_to_all | solution.py:169
  321.1 1.7 pad_maximum_fusion.3
  322.9 1.5 gather_fusion.1
  324.4 1.5 gather_fusion.2
  325.9 2.6 select_bitcast_fusion
  (73 shorter events, 31.3 us)
Async XLA Ops:
  7.2 179.2 %all-gather.2.cloned.1.call-start = ((), (), s32[]{:S(2)}) async-start(), calls=%async_computation.5 | async-start | bytes 22282240 | tf_op jit(solution)/shard_map/all_gather | solution.py:157
  10.7 6.1 %copy-start.9 = (bf16[1,128,2560]{2,1,0:T(8,128)(2,1)S(1)}, bf16[1,128,2560]{2,1,0:T(8,128)(2,1)}, u32[]{:S(2)}) copy-start(bf16[1,128,2560]{2,1,0:T(8,128)(2,1)} %param.9) | copy-start | bytes 1966084
  10.7 49.9 %all-to-all-start.1 = ((bf16[8,2,128,640]{3,2,1,0:T(8,128)(2,1)}), bf16[8,2,128,640]{3,2,1,0:T(8,128)(2,1)S(1)}, u32[]{:S(2)}, u32[]{:S(2)}) async-start(bf16[8,2,128,640]{3,2,1,0:T(8,128)(2,1)} %broadcast_in_dim.38), calls=%async_computation.1 | async-start | bytes 5242880 | tf_op jit(solution)/shard_map/all_to_all | solution.py:148
  16.8 2.6 copy-start.11
  30.6 1.2 copy-start.5
  30.6 1.5 copy-start.6
  34.2 37.5 %copy-start.10 = (s32[20,16,16]{0,2,1:T(8,128)S(1)}, s32[20,16,16]{0,2,1:T(8,128)}, u32[]{:S(2)}) copy-start(s32[20,16,16]{0,2,1:T(8,128)} %param.14) | copy-start | bytes 61444
  60.6 1.5 copy-start.3
  62.1 77.7 %all-to-all-start = ((bf16[16,3,2,128,128]{4,3,2,1,0:T(8,128)(2,1)}), bf16[16,3,2,128,128]{4,3,2,1,0:T(8,128)(2,1)S(1)}, u32[]{:S(2)}, u32[]{:S(2)}) async-start(bf16[16,3,2,128,128]{4,3,2,1,0:T(8,128)(2,1)} %pad_maximum_fusion), calls=%async_computation | async-start | bytes 6291456 | tf_op jit(solution)/shard_map/all_to_all | solution.py:142
  71.3 264.1 %reduce-scatter.4.cloned.1.call-start = ((), (), s32[]{:S(2)}) async-start(), calls=%async_computation.6 | async-start | bytes 2949120
  142.3 44.1 %copy-start.7 = (bf16[8,2,16,8,640]{4,3,0,2,1:T(8,128)(2,1)S(1)}, bf16[8,2,16,8,640]{4,3,0,2,1:T(8,128)(2,1)}, u32[]{:S(2)}) copy-start(bf16[8,2,16,8,640]{4,3,0,2,1:T(8,128)(2,1)} %copy.152) | copy-start | bytes 7864324
  186.4 13.2 %copy-start = (bf16[1,2048,5120]{2,1,0:T(8,128)(2,1)S(1)}, bf16[1,2048,5120]{2,1,0:T(8,128)(2,1)}, u32[]{:S(2)}) copy-start(bf16[1,2048,5120]{2,1,0:T(8,128)(2,1)} %all-gather.2.cloned.1.call-done) | copy-start | bytes 62914564
  186.4 13.3 %copy-start.1 = (bf16[2,2048,128]{2,1,0:T(8,128)(2,1)S(1)}, bf16[2,2048,128]{2,1,0:T(8,128)(2,1)}, u32[]{:S(2)}) copy-start(bf16[2,2048,128]{2,1,0:T(8,128)(2,1)} %get-tuple-element.17.o_ref) | copy-start | bytes 3145732
  240.2 6.6 %copy-start.2 = (bf16[2,2048,128]{2,1,0:T(8,128)(2,1)S(1)}, bf16[2,2048,128]{2,1,0:T(8,128)(2,1)}, u32[]{:S(2)}) copy-start(bf16[2,2048,128]{2,1,0:T(8,128)(2,1)} %get-tuple-element.17.o_ref) | copy-start | bytes 3145732
  243.0 32.5 %all-to-all-start.3 = ((bf16[3,16,128,128]{3,2,0,1:T(8,128)(2,1)}), bf16[3,16,128,128]{3,2,0,1:T(8,128)(2,1)S(1)}, u32[]{:S(2)}, u32[]{:S(2)}) async-start(bf16[3,16,128,128]{3,2,0,1:T(8,128)(2,1)} %pad_maximum_fusion.1), calls=%async_computation.3 | async-start | bytes 3145728 | tf_op jit(solution)/shard_map/all_to_all | solution.py:169
  275.6 1.2 copy-start.4
  276.7 41.7 %all-to-all-start.2 = ((bf16[5,16,128,128]{3,2,0,1:T(8,128)(2,1)}), bf16[5,16,128,128]{3,2,0,1:T(8,128)(2,1)S(1)}, u32[]{:S(2)}, u32[]{:S(2)}) async-start(bf16[5,16,128,128]{3,2,0,1:T(8,128)(2,1)} %constant_dynamic-update-slice_fusion), calls=%async_computation.2 | async-start | bytes 5242880 | tf_op jit(solution)/shard_map/all_to_all | solution.py:169
  328.5 2.6 copy-start.8
Sparse Core Ops, SparseCore 0:
  10.4 175.9 all-gather.1
  219.4 40.6 reduce-scatter.3

commit v11 on v10

--- a/solution.py
+++ b/solution.py
@@ -20,7 +20,7 @@
 
 def _fwd_kernel(q_ref, k_ref, v_ref, b_ref, o_ref, p_ref, *, scale):
     prob = _probs(q_ref[0], k_ref[0], b_ref[0, 0], scale)
-    p_ref[0] = prob
+    p_ref[0] = prob.T
     out = jnp.dot(prob.astype(jnp.bfloat16), v_ref[0], preferred_element_type=jnp.float32)
     o_ref[0] = out.astype(o_ref.dtype)
 
@@ -38,14 +38,15 @@
     k = k_ref[0]
     v = v_ref[0]
     do = do_ref[0]
-    prob = p_ref[0]
-    low = prob.astype(jnp.bfloat16)
-    delta = jnp.sum(do.astype(jnp.float32) * o_ref[0].astype(jnp.float32), axis=1, keepdims=True)
-    dv_scr[...] += lax.dot_general(low, do, TN, preferred_element_type=jnp.float32)
-    dp = lax.dot_general(do, v, NT, preferred_element_type=jnp.float32)
-    ds = (prob * (dp - delta) * scale).astype(jnp.bfloat16)
-    dq_ref[0] = jnp.dot(ds, k, preferred_element_type=jnp.float32).astype(dq_ref.dtype)
-    dk_scr[...] += lax.dot_general(ds, q, TN, preferred_element_type=jnp.float32)
+    prob_t = p_ref[0]
+    low_t = prob_t.astype(jnp.bfloat16)
+    product = do.astype(jnp.float32) * o_ref[0].astype(jnp.float32)
+    delta_row = jnp.sum(product.T, axis=0, keepdims=True)
+    dv_scr[...] += jnp.dot(low_t, do, preferred_element_type=jnp.float32)
+    dp_t = lax.dot_general(v, do, NT, preferred_element_type=jnp.float32)
+    ds_t = (prob_t * (dp_t - delta_row) * scale).astype(jnp.bfloat16)
+    dq_ref[0] = lax.dot_general(ds_t, k, TN, preferred_element_type=jnp.float32).astype(dq_ref.dtype)
+    dk_scr[...] += jnp.dot(ds_t, q, preferred_element_type=jnp.float32)
 
     @pl.when(qi == nb - 1)
     def _():
@@ -64,7 +65,7 @@
     row = pl.BlockSpec((1, TILE, hd), lambda s, i: (s, i, 0))
     full = pl.BlockSpec((1, length, hd), lambda s, i: (s, 0, 0))
     brow = pl.BlockSpec((1, 1, 1, length), lambda s, i: (s, i, 0, 0))
-    prow = pl.BlockSpec((1, TILE, length), lambda s, i: (s, i, 0))
+    prow = pl.BlockSpec((1, length, TILE), lambda s, i: (s, 0, i))
     return pl.pallas_call(
         functools.partial(_fwd_kernel, scale=scale),
         grid=(slots, nb),
@@ -83,7 +84,7 @@
     nb = length // TILE
     row = pl.BlockSpec((1, TILE, hd), lambda i: (slot, i, 0))
     full = pl.BlockSpec((1, length, hd), lambda i: (slot, 0, 0))
-    prow = pl.BlockSpec((1, TILE, length), lambda i: (slot, i, 0))
+    prow = pl.BlockSpec((1, length, TILE), lambda i: (slot, 0, i))
     out_row = pl.BlockSpec((1, TILE, hd), lambda i: (0, i, 0))
     out_full = pl.BlockSpec((1, length, hd), lambda i: (0, 0, 0))
     shape = jax.ShapeDtypeStruct((1, length, hd), jnp.bfloat16)

time: 348 us -> 348 us (level)
  Pallas kernels: 72.5 us -> 76.5 us
  transfers between devices with their start and end apart: 6 -> 6, of which waited for: 4 -> 4; matrix products, arithmetic and copies ran while one was open for 17% -> 17% of each run, Pallas kernels for 21% -> 22%
where the time goes in v11:
time: 348 us; the launch traced here: 346 us
  waiting for transfers between devices  131 us (38%)
  Pallas kernels  76.5 us (22%)
  local copies, waits for them, and re-layouts  59.9 us (17%)
  starting transfers between devices  26.5 us (8%)
  matrix products  22.2 us (6%)
  other arithmetic  15.4 us (4%)
  between operations  14.3 us (4%)
    all_to_all x1, waiting for transfers between devices, on_device(): lax.all_to_all(stacked, 'seq', split_axis=0, concat_axis=3, tiled=True)[0]  64.3 us
    pallas_call x2, Pallas kernels, attn_backward(): pl.pallas_call(functools.partial(_bwd_kernel, nb=nb, scale=scale), grid=(...  42.3 us
    pallas_call x1, Pallas kernels, attn_forward(): pl.pallas_call(functools.partial(_fwd_kernel, scale=scale), grid=(slots,...  34.2 us
    all_to_all x2, waiting for transfers between devices, to_owners(): lax.all_to_all(one_stack, 'seq', split_axis=1, concat_axis=1, tiled=True)  31.4 us
    unnamed x39, local copies, waits for them, and re-layouts  28.8 us
    all_to_all x1, waiting for transfers between devices, on_device(): lax.all_to_all(weight_copies, 'dp', split_axis=0, concat_axis=0, tiled=True)  26.4 us
    dot_general x1, matrix products, on_device(): jnp.einsum('td,shd->sth', dy_rows, weight_full, preferred_element_type=jn...  13.2 us
    all_to_all x2, starting transfers between devices, to_owners(): lax.all_to_all(one_stack, 'seq', split_axis=1, concat_axis=1, tiled=True)  11.1 us
  transfers between devices with their start and end apart: 6, of which 4 were waited for; matrix products, arithmetic and copies ran while one was open for 17% of the time, Pallas kernels for 22%

profile of v11, /device:TPU:1, one launch (start us, length us, event | category | flops | bytes accessed | tf_op | source)
XLA Modules:
  0.0 345.6 jit_solution(17303193185910532241)
XLA Ops:
  7.9 2.8 broadcast_in_dim.38
  10.7 6.1 %all-to-all-start.1 = ((bf16[8,2,128,640]{3,2,1,0:T(8,128)(2,1)}), bf16[8,2,128,640]{3,2,1,0:T(8,128)(2,1)S(1)}, u32[]{:S(2)}, u32[]{:S(2)}) async-start(bf16[8,2,128,640]{3,2,1,0:T(8,128)(2,1)} %broadcast_in_dim.38), calls=%async_computation.1 | async-start | bytes 5242880 | tf_op jit(solution)/shard_map/all_to_all | solution.py:149
  21.4 2.2 copy.94
  23.5 1.6 copy.96
  27.0 2.2 copy.97
  32.2 2.0 pad_maximum_fusion
  34.2 26.4 %all-to-all-done.1 = bf16[8,2,128,640]{3,2,1,0:T(8,128)(2,1)S(1)} async-done(((bf16[8,2,128,640]{3,2,1,0:T(8,128)(2,1)}), bf16[8,2,128,640]{3,2,1,0:T(8,128)(2,1)S(1)}, u32[]{:S(2)}, u32[]{:S(2)}) %all-to-all-start.1) | async-done | bytes 2621472 | tf_op jit(solution)/shard_map/all_to_all | solution.py:149
  60.6 1.5 copy-done.3
  62.1 9.2 %all-to-all-start = ((bf16[16,3,2,128,128]{4,3,2,1,0:T(8,128)(2,1)}), bf16[16,3,2,128,128]{4,3,2,1,0:T(8,128)(2,1)S(1)}, u32[]{:S(2)}, u32[]{:S(2)}) async-start(bf16[16,3,2,128,128]{4,3,2,1,0:T(8,128)(2,1)} %pad_maximum_fusion), calls=%async_computation | async-start | bytes 6291456 | tf_op jit(solution)/shard_map/all_to_all | solution.py:143
  71.9 3.6 %copy.152 = bf16[8,2,16,8,640]{4,3,0,2,1:T(8,128)(2,1)} copy(bf16[8,2,16,8,640]{4,3,2,1,0:T(8,128)(2,1)} %bitcast.134) | data formatting | bytes 5242880 | tf_op jit(solution)/shard_map/reshape | solution.py:155
  75.6 64.3 %all-to-all-done = bf16[16,3,2,128,128]{4,3,2,1,0:T(8,128)(2,1)S(1)} async-done(((bf16[16,3,2,128,128]{4,3,2,1,0:T(8,128)(2,1)}), bf16[16,3,2,128,128]{4,3,2,1,0:T(8,128)(2,1)S(1)}, u32[]{:S(2)}, u32[]{:S(2)}) %all-to-all-start) | async-done | bytes 3145760 | tf_op jit(solution)/shard_map/all_to_all | solution.py:143
  144.2 34.2 %shard_map.110 = (bf16[2,2048,128]{2,1,0:T(8,128)(2,1)}, f32[2,2048,2048]{2,1,0:T(8,128)}) custom-call(bf16[2,2048,128]{2,1,0:T(8,128)(2,1)} %bitcast.129, bf16[2,2048,128]{2,1,0:T(8,128)(2,1)} %bitcast.126, bf16[2,2048,128]{2,1,0:T(8,128)(2,1)} %bitcast.123, f32[2,16,1,2048]{3,2,1,0:T(1,128)} %bitcast.154), custom_call_target="tpu_custom_call" | custom-call | tf_op jit(solution)/shard_map/pallas_call | solution.py:69
  178.4 8.0 %all-gather.2.cloned.1.call-done = bf16[1,2048,5120]{2,1,0:T(8,128)(2,1)} async-done(((bf16[1,128,5120]{2,1,0:T(8,128)(2,1)}), bf16[1,2048,5120]{2,1,0:T(8,128)(2,1)}) %all-gather.2.cloned.1.call-update) | async-done | bytes 20971536 | tf_op jit(solution)/shard_map/all_gather | solution.py:158
  186.4 13.2 %fusion.7.do_ref = bf16[2,2048,128]{2,1,0:T(8,128)(2,1)} fusion(bf16[2,128,5120]{2,1,0:T(8,128)(2,1)S(1)} %bitcast.143, bf16[1,2048,5120]{2,1,0:T(8,128)(2,1)} %all-gather.2.cloned.1.call-done), kind=kOutput, calls=%fused_computation.12 | convolution fusion | flops 5369233408 | bytes 24641536 | tf_op jit(solution)/shard_map/td,shd->sth/dot_general | solution.py:159
  199.8 7.5 %fusion = f32[2,128,5120]{2,1,0:T(8,128)} fusion(bf16[2,2048,128]{2,1,0:T(8,128)(2,1)S(1)} %copy-done.1, bf16[1,2048,5120]{2,1,0:T(8,128)(2,1)S(1)} %copy-done), kind=kOutput, calls=%fused_computation.4 | convolution fusion | flops 5368709120 | bytes 27262976 | tf_op jit(solution)/shard_map/sth,td->shd/dot_general | solution.py:163
  207.2 4.4 %multiply_convert_fusion = bf16[2,128,5120]{2,1,0:T(8,128)(2,1)} fusion(f32[2,128,5120]{2,1,0:T(8,128)} %fusion), kind=kLoop, calls=%fused_computation.8 | loop fusion | flops 2621440 | bytes 7864320 | tf_op jit(solution)/shard_map/convert_element_type | solution.py:166
  211.6 5.9 %copy.142 = bf16[2,128,5120]{1,0,2:T(2,128)(2,1)S(1)} copy(bf16[2,128,5120]{2,1,0:T(8,128)(2,1)} %multiply_convert_fusion) | data formatting | bytes 5242880
  217.4 1.8 copy.155
  219.3 21.2 %shard_map.112 = (bf16[1,2048,128]{2,1,0:T(8,128)(2,1)}, bf16[1,2048,128]{2,1,0:T(8,128)(2,1)}, bf16[1,2048,128]{2,1,0:T(8,128)(2,1)}) custom-call(bf16[2,2048,128]{2,1,0:T(8,128)(2,1)} %bitcast.130, bf16[2,2048,128]{2,1,0:T(8,128)(2,1)} %bitcast.127, bf16[2,2048,128]{2,1,0:T(8,128)(2,1)} %bitcast.124, f32[2,2048,2048]{2,1,0:T(8,128)} %get-tuple-element.18.p_ref, ...), custom_call_target="tpu_custom_call" | custom-call | tf_op jit(solution)/shard_map/pallas_call | solution.py:91
  240.5 2.8 pad_maximum_fusion.1
  243.3 3.8 %all-to-all-start.3 = ((bf16[3,16,128,128]{3,2,0,1:T(8,128)(2,1)}), bf16[3,16,128,128]{3,2,0,1:T(8,128)(2,1)S(1)}, u32[]{:S(2)}, u32[]{:S(2)}) async-start(bf16[3,16,128,128]{3,2,0,1:T(8,128)(2,1)} %pad_maximum_fusion.1), calls=%async_computation.3 | async-start | bytes 3145728 | tf_op jit(solution)/shard_map/all_to_all | solution.py:170
  249.0 21.1 %shard_map.111 = (bf16[1,2048,128]{2,1,0:T(8,128)(2,1)}, bf16[1,2048,128]{2,1,0:T(8,128)(2,1)}, bf16[1,2048,128]{2,1,0:T(8,128)(2,1)}) custom-call(bf16[2,2048,128]{2,1,0:T(8,128)(2,1)} %bitcast.131, bf16[2,2048,128]{2,1,0:T(8,128)(2,1)} %bitcast.128, bf16[2,2048,128]{2,1,0:T(8,128)(2,1)} %bitcast.125, f32[2,2048,2048]{2,1,0:T(8,128)} %get-tuple-element.18.p_ref, ...), custom_call_target="tpu_custom_call" | custom-call | tf_op jit(solution)/shard_map/pallas_call | solution.py:91
  270.1 2.0 constant_dynamic-update-slice_fusion.2
  272.1 2.0 constant_dynamic-update-slice_fusion.1
  274.1 2.0 constant_dynamic-update-slice_fusion
  277.2 7.3 %all-to-all-start.2 = ((bf16[5,16,128,128]{3,2,0,1:T(8,128)(2,1)}), bf16[5,16,128,128]{3,2,0,1:T(8,128)(2,1)S(1)}, u32[]{:S(2)}, u32[]{:S(2)}) async-start(bf16[5,16,128,128]{3,2,0,1:T(8,128)(2,1)} %constant_dynamic-update-slice_fusion), calls=%async_computation.2 | async-start | bytes 5242880 | tf_op jit(solution)/shard_map/all_to_all | solution.py:170
  285.1 2.5 slice_bitcast_fusion
  287.6 31.4 %all-to-all-done.2 = bf16[5,16,128,128]{3,2,0,1:T(8,128)(2,1)S(1)} async-done(((bf16[5,16,128,128]{3,2,0,1:T(8,128)(2,1)}), bf16[5,16,128,128]{3,2,0,1:T(8,128)(2,1)S(1)}, u32[]{:S(2)}, u32[]{:S(2)}) %all-to-all-start.2) | async-done | bytes 2621472 | tf_op jit(solution)/shard_map/all_to_all | solution.py:170
  321.7 1.7 pad_maximum_fusion.3
  323.4 1.5 gather_fusion.1
  324.9 1.5 gather_fusion.2
  326.4 2.6 select_bitcast_fusion
  (73 shorter events, 31.3 us)
Async XLA Ops:
  7.2 179.2 %all-gather.2.cloned.1.call-start = ((), (), s32[]{:S(2)}) async-start(), calls=%async_computation.5 | async-start | bytes 22282240 | tf_op jit(solution)/shard_map/all_gather | solution.py:158
  10.7 6.1 %copy-start.9 = (bf16[1,128,2560]{2,1,0:T(8,128)(2,1)S(1)}, bf16[1,128,2560]{2,1,0:T(8,128)(2,1)}, u32[]{:S(2)}) copy-start(bf16[1,128,2560]{2,1,0:T(8,128)(2,1)} %param.9) | copy-start | bytes 1966084
  10.7 49.9 %all-to-all-start.1 = ((bf16[8,2,128,640]{3,2,1,0:T(8,128)(2,1)}), bf16[8,2,128,640]{3,2,1,0:T(8,128)(2,1)S(1)}, u32[]{:S(2)}, u32[]{:S(2)}) async-start(bf16[8,2,128,640]{3,2,1,0:T(8,128)(2,1)} %broadcast_in_dim.38), calls=%async_computation.1 | async-start | bytes 5242880 | tf_op jit(solution)/shard_map/all_to_all | solution.py:149
  16.8 2.6 copy-start.11
  30.6 1.2 copy-start.5
  30.6 1.5 copy-start.6
  34.2 37.5 %copy-start.10 = (s32[20,16,16]{0,2,1:T(8,128)S(1)}, s32[20,16,16]{0,2,1:T(8,128)}, u32[]{:S(2)}) copy-start(s32[20,16,16]{0,2,1:T(8,128)} %param.14) | copy-start | bytes 61444
  60.6 1.5 copy-start.3
  62.1 77.7 %all-to-all-start = ((bf16[16,3,2,128,128]{4,3,2,1,0:T(8,128)(2,1)}), bf16[16,3,2,128,128]{4,3,2,1,0:T(8,128)(2,1)S(1)}, u32[]{:S(2)}, u32[]{:S(2)}) async-start(bf16[16,3,2,128,128]{4,3,2,1,0:T(8,128)(2,1)} %pad_maximum_fusion), calls=%async_computation | async-start | bytes 6291456 | tf_op jit(solution)/shard_map/all_to_all | solution.py:143
  71.3 264.6 %reduce-scatter.4.cloned.1.call-start = ((), (), s32[]{:S(2)}) async-start(), calls=%async_computation.6 | async-start | bytes 2949120
  142.3 44.1 %copy-start.7 = (bf16[8,2,16,8,640]{4,3,0,2,1:T(8,128)(2,1)S(1)}, bf16[8,2,16,8,640]{4,3,0,2,1:T(8,128)(2,1)}, u32[]{:S(2)}) copy-start(bf16[8,2,16,8,640]{4,3,0,2,1:T(8,128)(2,1)} %copy.152) | copy-start | bytes 7864324
  186.4 13.2 %copy-start = (bf16[1,2048,5120]{2,1,0:T(8,128)(2,1)S(1)}, bf16[1,2048,5120]{2,1,0:T(8,128)(2,1)}, u32[]{:S(2)}) copy-start(bf16[1,2048,5120]{2,1,0:T(8,128)(2,1)} %all-gather.2.cloned.1.call-done) | copy-start | bytes 62914564
  186.4 13.3 %copy-start.1 = (bf16[2,2048,128]{2,1,0:T(8,128)(2,1)S(1)}, bf16[2,2048,128]{2,1,0:T(8,128)(2,1)}, u32[]{:S(2)}) copy-start(bf16[2,2048,128]{2,1,0:T(8,128)(2,1)} %get-tuple-element.17.o_ref) | copy-start | bytes 3145732
  240.5 6.6 %copy-start.2 = (bf16[2,2048,128]{2,1,0:T(8,128)(2,1)S(1)}, bf16[2,2048,128]{2,1,0:T(8,128)(2,1)}, u32[]{:S(2)}) copy-start(bf16[2,2048,128]{2,1,0:T(8,128)(2,1)} %get-tuple-element.17.o_ref) | copy-start | bytes 3145732
  243.3 32.8 %all-to-all-start.3 = ((bf16[3,16,128,128]{3,2,0,1:T(8,128)(2,1)}), bf16[3,16,128,128]{3,2,0,1:T(8,128)(2,1)S(1)}, u32[]{:S(2)}, u32[]{:S(2)}) async-start(bf16[3,16,128,128]{3,2,0,1:T(8,128)(2,1)} %pad_maximum_fusion.1), calls=%async_computation.3 | async-start | bytes 3145728 | tf_op jit(solution)/shard_map/all_to_all | solution.py:170
  276.1 1.2 copy-start.4
  277.2 41.7 %all-to-all-start.2 = ((bf16[5,16,128,128]{3,2,0,1:T(8,128)(2,1)}), bf16[5,16,128,128]{3,2,0,1:T(8,128)(2,1)S(1)}, u32[]{:S(2)}, u32[]{:S(2)}) async-start(bf16[5,16,128,128]{3,2,0,1:T(8,128)(2,1)} %constant_dynamic-update-slice_fusion), calls=%async_computation.2 | async-start | bytes 5242880 | tf_op jit(solution)/shard_map/all_to_all | solution.py:170
  329.0 2.6 copy-start.8
Sparse Core Ops, SparseCore 0:
  10.4 175.9 all-gather.1
  219.4 40.7 reduce-scatter.3

commit v12 on v11

--- a/solution.py
+++ b/solution.py
@@ -160,11 +160,12 @@
         "td,shd->sth", dy_rows, weight_full, preferred_element_type=jnp.float32
     ).astype(jnp.bfloat16)
     grad_attn = part
-    weight_total = jnp.einsum("sth,td->shd", slot_out, dy_rows, preferred_element_type=jnp.float32)
+    weight_total = jnp.einsum("td,sth->dsh", dy_rows, slot_out, preferred_element_type=jnp.float32)
     grad_attn, weight_total = lax.optimization_barrier((grad_attn, weight_total))
-    weight_grad = lax.psum_scatter(
-        (weight_total * grad_scale).astype(jnp.bfloat16), "dp", scatter_dimension=2, tiled=True
-    ).astype(jnp.float32)
+    weight_rows = lax.psum_scatter(
+        (weight_total * grad_scale).astype(jnp.bfloat16), "dp", scatter_dimension=0, tiled=True
+    )
+    weight_grad = jnp.transpose(weight_rows, (1, 2, 0)).astype(jnp.float32)
     def to_owners(tensors):
         one_stack = jnp.stack([t.reshape(seq_count, token_count, head_dim) for t in tensors])
         return lax.all_to_all(one_stack, "seq", split_axis=1, concat_axis=1, tiled=True)

time: 348 us -> 341 us (0.980)
  local copies, waits for them, and re-layouts: 59.9 us -> 54 us
    unnamed x39 -> x37, local copies, waits for them, and re-layouts: 28.8 us -> 22.9 us
  transfers between devices with their start and end apart: 6 -> 6, of which waited for: 4 -> 4; matrix products, arithmetic and copies ran while one was open for 17% -> 17% of each run, Pallas kernels for 22% -> 23%
where the time goes in v12:
time: 341 us; the launch traced here: 338 us
  waiting for transfers between devices  131 us (38%)
  Pallas kernels  76.5 us (22%)
  local copies, waits for them, and re-layouts  54 us (16%)
  starting transfers between devices  26.6 us (8%)
  matrix products  22.2 us (7%)
  between operations  14.3 us (4%)
  other arithmetic  14 us (4%)
    all_to_all x1, waiting for transfers between devices, on_device(): lax.all_to_all(stacked, 'seq', split_axis=0, concat_axis=3, tiled=True)[0]  64.3 us
    pallas_call x2, Pallas kernels, attn_backward(): pl.pallas_call(functools.partial(_bwd_kernel, nb=nb, scale=scale), grid=(...  42.3 us
    pallas_call x1, Pallas kernels, attn_forward(): pl.pallas_call(functools.partial(_fwd_kernel, scale=scale), grid=(slots,...  34.2 us
    all_to_all x2, waiting for transfers between devices, to_owners(): lax.all_to_all(one_stack, 'seq', split_axis=1, concat_axis=1, tiled=True)  31.4 us
    all_to_all x1, waiting for transfers between devices, on_device(): lax.all_to_all(weight_copies, 'dp', split_axis=0, concat_axis=0, tiled=True)  26.4 us
    unnamed x37, local copies, waits for them, and re-layouts  22.9 us
    dot_general x1, matrix products, on_device(): jnp.einsum('td,shd->sth', dy_rows, weight_full, preferred_element_type=jn...  13.2 us
    all_to_all x2, starting transfers between devices, to_owners(): lax.all_to_all(one_stack, 'seq', split_axis=1, concat_axis=1, tiled=True)  11.1 us
  transfers between devices with their start and end apart: 6, of which 4 were waited for; matrix products, arithmetic and copies ran while one was open for 17% of the time, Pallas kernels for 23%

profile of v12, /device:TPU:1, one launch (start us, length us, event | category | flops | bytes accessed | tf_op | source)
XLA Modules:
  0.0 338.2 jit_solution(8990367705307123933)
XLA Ops:
  7.9 2.8 broadcast_in_dim.38
  10.7 6.1 %all-to-all-start.1 = ((bf16[8,2,128,640]{3,2,1,0:T(8,128)(2,1)}), bf16[8,2,128,640]{3,2,1,0:T(8,128)(2,1)S(1)}, u32[]{:S(2)}, u32[]{:S(2)}) async-start(bf16[8,2,128,640]{3,2,1,0:T(8,128)(2,1)} %broadcast_in_dim.38), calls=%async_computation.1 | async-start | bytes 5242880 | tf_op jit(solution)/shard_map/all_to_all | solution.py:149
  17.9 1.5 copy.93
  21.4 2.2 copy.94
  23.5 1.6 copy.96
  27.0 2.2 copy.97
  32.2 2.0 pad_maximum_fusion
  34.2 26.4 %all-to-all-done.1 = bf16[8,2,128,640]{3,2,1,0:T(8,128)(2,1)S(1)} async-done(((bf16[8,2,128,640]{3,2,1,0:T(8,128)(2,1)}), bf16[8,2,128,640]{3,2,1,0:T(8,128)(2,1)S(1)}, u32[]{:S(2)}, u32[]{:S(2)}) %all-to-all-start.1) | async-done | bytes 2621472 | tf_op jit(solution)/shard_map/all_to_all | solution.py:149
  60.6 1.5 copy-done.3
  62.1 9.2 %all-to-all-start = ((bf16[16,3,2,128,128]{4,3,2,1,0:T(8,128)(2,1)}), bf16[16,3,2,128,128]{4,3,2,1,0:T(8,128)(2,1)S(1)}, u32[]{:S(2)}, u32[]{:S(2)}) async-start(bf16[16,3,2,128,128]{4,3,2,1,0:T(8,128)(2,1)} %pad_maximum_fusion), calls=%async_computation | async-start | bytes 6291456 | tf_op jit(solution)/shard_map/all_to_all | solution.py:143
  71.9 3.6 %copy.154 = bf16[8,2,16,8,640]{4,3,0,2,1:T(8,128)(2,1)} copy(bf16[8,2,16,8,640]{4,3,2,1,0:T(8,128)(2,1)} %bitcast.136) | data formatting | bytes 5242880 | tf_op jit(solution)/shard_map/reshape | solution.py:155
  75.6 64.3 %all-to-all-done = bf16[16,3,2,128,128]{4,3,2,1,0:T(8,128)(2,1)S(1)} async-done(((bf16[16,3,2,128,128]{4,3,2,1,0:T(8,128)(2,1)}), bf16[16,3,2,128,128]{4,3,2,1,0:T(8,128)(2,1)S(1)}, u32[]{:S(2)}, u32[]{:S(2)}) %all-to-all-start) | async-done | bytes 3145760 | tf_op jit(solution)/shard_map/all_to_all | solution.py:143
  144.2 34.2 %shard_map.110 = (bf16[2,2048,128]{2,1,0:T(8,128)(2,1)}, f32[2,2048,2048]{2,1,0:T(8,128)}) custom-call(bf16[2,2048,128]{2,1,0:T(8,128)(2,1)} %bitcast.132, bf16[2,2048,128]{2,1,0:T(8,128)(2,1)} %bitcast.129, bf16[2,2048,128]{2,1,0:T(8,128)(2,1)} %bitcast.126, f32[2,16,1,2048]{3,2,1,0:T(1,128)} %bitcast.156), custom_call_target="tpu_custom_call" | custom-call | tf_op jit(solution)/shard_map/pallas_call | solution.py:69
  178.4 8.0 %all-gather.2.cloned.1.call-done = bf16[1,2048,5120]{2,1,0:T(8,128)(2,1)} async-done(((bf16[1,128,5120]{2,1,0:T(8,128)(2,1)}), bf16[1,2048,5120]{2,1,0:T(8,128)(2,1)}) %all-gather.2.cloned.1.call-update) | async-done | bytes 20971536 | tf_op jit(solution)/shard_map/all_gather | solution.py:158
  186.4 13.2 %fusion.10.do_ref = bf16[2,2048,128]{2,1,0:T(8,128)(2,1)} fusion(bf16[2,128,5120]{2,1,0:T(8,128)(2,1)S(1)} %bitcast.145, bf16[1,2048,5120]{2,1,0:T(8,128)(2,1)} %all-gather.2.cloned.1.call-done), kind=kOutput, calls=%fused_computation.12 | convolution fusion | flops 5369233408 | bytes 24641536 | tf_op jit(solution)/shard_map/td,shd->sth/dot_general | solution.py:159
  199.8 7.5 %fusion.4 = f32[5120,2,128]{0,2,1:T(8,128)} fusion(bf16[2,2048,128]{2,1,0:T(8,128)(2,1)S(1)} %copy-done.1, bf16[1,2048,5120]{2,1,0:T(8,128)(2,1)S(1)} %copy-done), kind=kOutput, calls=%fused_computation.8 | convolution fusion | flops 5368709120 | bytes 27262976 | tf_op jit(solution)/shard_map/td,sth->dsh/dot_general | solution.py:163
  207.2 2.9 multiply_convert_fusion
  210.1 2.6 copy.144
  212.7 21.2 %shard_map.112 = (bf16[1,2048,128]{2,1,0:T(8,128)(2,1)}, bf16[1,2048,128]{2,1,0:T(8,128)(2,1)}, bf16[1,2048,128]{2,1,0:T(8,128)(2,1)}) custom-call(bf16[2,2048,128]{2,1,0:T(8,128)(2,1)} %bitcast.133, bf16[2,2048,128]{2,1,0:T(8,128)(2,1)} %bitcast.130, bf16[2,2048,128]{2,1,0:T(8,128)(2,1)} %bitcast.127, f32[2,2048,2048]{2,1,0:T(8,128)} %get-tuple-element.18.p_ref, ...), custom_call_target="tpu_custom_call" | custom-call | tf_op jit(solution)/shard_map/pallas_call | solution.py:91
  233.9 2.8 pad_maximum_fusion.1
  236.7 3.8 %all-to-all-start.3 = ((bf16[3,16,128,128]{3,2,0,1:T(8,128)(2,1)}), bf16[3,16,128,128]{3,2,0,1:T(8,128)(2,1)S(1)}, u32[]{:S(2)}, u32[]{:S(2)}) async-start(bf16[3,16,128,128]{3,2,0,1:T(8,128)(2,1)} %pad_maximum_fusion.1), calls=%async_computation.3 | async-start | bytes 3145728 | tf_op jit(solution)/shard_map/all_to_all | solution.py:171
  242.4 21.1 %shard_map.111 = (bf16[1,2048,128]{2,1,0:T(8,128)(2,1)}, bf16[1,2048,128]{2,1,0:T(8,128)(2,1)}, bf16[1,2048,128]{2,1,0:T(8,128)(2,1)}) custom-call(bf16[2,2048,128]{2,1,0:T(8,128)(2,1)} %bitcast.134, bf16[2,2048,128]{2,1,0:T(8,128)(2,1)} %bitcast.131, bf16[2,2048,128]{2,1,0:T(8,128)(2,1)} %bitcast.128, f32[2,2048,2048]{2,1,0:T(8,128)} %get-tuple-element.18.p_ref, ...), custom_call_target="tpu_custom_call" | custom-call | tf_op jit(solution)/shard_map/pallas_call | solution.py:91
  263.5 2.0 constant_dynamic-update-slice_fusion.2
  265.5 2.0 constant_dynamic-update-slice_fusion.1
  267.5 2.0 constant_dynamic-update-slice_fusion
  270.7 7.3 %all-to-all-start.2 = ((bf16[5,16,128,128]{3,2,0,1:T(8,128)(2,1)}), bf16[5,16,128,128]{3,2,0,1:T(8,128)(2,1)S(1)}, u32[]{:S(2)}, u32[]{:S(2)}) async-start(bf16[5,16,128,128]{3,2,0,1:T(8,128)(2,1)} %constant_dynamic-update-slice_fusion), calls=%async_computation.2 | async-start | bytes 5242880 | tf_op jit(solution)/shard_map/all_to_all | solution.py:171
  278.6 2.5 slice_bitcast_fusion
  281.1 31.4 %all-to-all-done.2 = bf16[5,16,128,128]{3,2,0,1:T(8,128)(2,1)S(1)} async-done(((bf16[5,16,128,128]{3,2,0,1:T(8,128)(2,1)}), bf16[5,16,128,128]{3,2,0,1:T(8,128)(2,1)S(1)}, u32[]{:S(2)}, u32[]{:S(2)}) %all-to-all-start.2) | async-done | bytes 2621472 | tf_op jit(solution)/shard_map/all_to_all | solution.py:171
  315.1 1.7 pad_maximum_fusion.3
  316.8 1.5 gather_fusion.1
  318.3 1.5 gather_fusion.2
  319.8 2.6 select_bitcast_fusion
  (71 shorter events, 29.0 us)
Async XLA Ops:
  7.2 179.2 %all-gather.2.cloned.1.call-start = ((), (), s32[]{:S(2)}) async-start(), calls=%async_computation.5 | async-start | bytes 22282240 | tf_op jit(solution)/shard_map/all_gather | solution.py:158
  10.7 6.1 %copy-start.9 = (bf16[1,128,2560]{2,1,0:T(8,128)(2,1)S(1)}, bf16[1,128,2560]{2,1,0:T(8,128)(2,1)}, u32[]{:S(2)}) copy-start(bf16[1,128,2560]{2,1,0:T(8,128)(2,1)} %param.9) | copy-start | bytes 1966084
  10.7 49.9 %all-to-all-start.1 = ((bf16[8,2,128,640]{3,2,1,0:T(8,128)(2,1)}), bf16[8,2,128,640]{3,2,1,0:T(8,128)(2,1)S(1)}, u32[]{:S(2)}, u32[]{:S(2)}) async-start(bf16[8,2,128,640]{3,2,1,0:T(8,128)(2,1)} %broadcast_in_dim.38), calls=%async_computation.1 | async-start | bytes 5242880 | tf_op jit(solution)/shard_map/all_to_all | solution.py:149
  16.8 2.6 copy-start.11
  30.6 1.2 copy-start.5
  30.6 1.5 copy-start.6
  34.2 37.5 %copy-start.10 = (s32[20,16,16]{0,2,1:T(8,128)S(1)}, s32[20,16,16]{0,2,1:T(8,128)}, u32[]{:S(2)}) copy-start(s32[20,16,16]{0,2,1:T(8,128)} %param.14) | copy-start | bytes 61444
  60.6 1.5 copy-start.3
  62.1 77.7 %all-to-all-start = ((bf16[16,3,2,128,128]{4,3,2,1,0:T(8,128)(2,1)}), bf16[16,3,2,128,128]{4,3,2,1,0:T(8,128)(2,1)S(1)}, u32[]{:S(2)}, u32[]{:S(2)}) async-start(bf16[16,3,2,128,128]{4,3,2,1,0:T(8,128)(2,1)} %pad_maximum_fusion), calls=%async_computation | async-start | bytes 6291456 | tf_op jit(solution)/shard_map/all_to_all | solution.py:143
  71.3 258.0 %reduce-scatter.4.cloned.1.call-start = ((), (), s32[]{:S(2)}) async-start(), calls=%async_computation.6 | async-start | bytes 2949120
  142.3 44.1 %copy-start.7 = (bf16[8,2,16,8,640]{4,3,0,2,1:T(8,128)(2,1)S(1)}, bf16[8,2,16,8,640]{4,3,0,2,1:T(8,128)(2,1)}, u32[]{:S(2)}) copy-start(bf16[8,2,16,8,640]{4,3,0,2,1:T(8,128)(2,1)} %copy.154) | copy-start | bytes 7864324
  186.4 13.2 %copy-start = (bf16[1,2048,5120]{2,1,0:T(8,128)(2,1)S(1)}, bf16[1,2048,5120]{2,1,0:T(8,128)(2,1)}, u32[]{:S(2)}) copy-start(bf16[1,2048,5120]{2,1,0:T(8,128)(2,1)} %all-gather.2.cloned.1.call-done) | copy-start | bytes 62914564
  186.4 13.3 %copy-start.1 = (bf16[2,2048,128]{2,1,0:T(8,128)(2,1)S(1)}, bf16[2,2048,128]{2,1,0:T(8,128)(2,1)}, u32[]{:S(2)}) copy-start(bf16[2,2048,128]{2,1,0:T(8,128)(2,1)} %get-tuple-element.17.o_ref) | copy-start | bytes 3145732
  233.9 6.6 %copy-start.2 = (bf16[2,2048,128]{2,1,0:T(8,128)(2,1)S(1)}, bf16[2,2048,128]{2,1,0:T(8,128)(2,1)}, u32[]{:S(2)}) copy-start(bf16[2,2048,128]{2,1,0:T(8,128)(2,1)} %get-tuple-element.17.o_ref) | copy-start | bytes 3145732
  236.7 32.8 %all-to-all-start.3 = ((bf16[3,16,128,128]{3,2,0,1:T(8,128)(2,1)}), bf16[3,16,128,128]{3,2,0,1:T(8,128)(2,1)S(1)}, u32[]{:S(2)}, u32[]{:S(2)}) async-start(bf16[3,16,128,128]{3,2,0,1:T(8,128)(2,1)} %pad_maximum_fusion.1), calls=%async_computation.3 | async-start | bytes 3145728 | tf_op jit(solution)/shard_map/all_to_all | solution.py:171
  269.5 1.2 copy-start.4
  270.7 41.7 %all-to-all-start.2 = ((bf16[5,16,128,128]{3,2,0,1:T(8,128)(2,1)}), bf16[5,16,128,128]{3,2,0,1:T(8,128)(2,1)S(1)}, u32[]{:S(2)}, u32[]{:S(2)}) async-start(bf16[5,16,128,128]{3,2,0,1:T(8,128)(2,1)} %constant_dynamic-update-slice_fusion), calls=%async_computation.2 | async-start | bytes 5242880 | tf_op jit(solution)/shard_map/all_to_all | solution.py:171
  322.5 2.6 copy-start.8
Sparse Core Ops, SparseCore 0:
  10.4 175.9 all-gather.1
  212.8 40.6 reduce-scatter.3

commit v13 on v12

--- a/solution.py
+++ b/solution.py
@@ -25,8 +25,7 @@
     o_ref[0] = out.astype(o_ref.dtype)
 
 
-def _bwd_kernel(q_ref, k_ref, v_ref, p_ref, o_ref, do_ref, dq_ref, dk_ref, dv_ref,
-                dk_scr, dv_scr, *, nb, scale):
+def _bwd_kernel(q_ref, k_ref, v_ref, p_ref, o_ref, do_ref, g_ref, dk_scr, dv_scr, *, nb, scale):
     qi = pl.program_id(0)
 
     @pl.when(qi == 0)
@@ -45,13 +44,15 @@
     dv_scr[...] += jnp.dot(low_t, do, preferred_element_type=jnp.float32)
     dp_t = lax.dot_general(v, do, NT, preferred_element_type=jnp.float32)
     ds_t = (prob_t * (dp_t - delta_row) * scale).astype(jnp.bfloat16)
-    dq_ref[0] = lax.dot_general(ds_t, k, TN, preferred_element_type=jnp.float32).astype(dq_ref.dtype)
+    row_first = pl.multiple_of(qi * TILE, TILE)
+    dq = lax.dot_general(ds_t, k, TN, preferred_element_type=jnp.float32)
+    g_ref[0, pl.ds(row_first, TILE), :] = dq.astype(g_ref.dtype)
     dk_scr[...] += jnp.dot(ds_t, q, preferred_element_type=jnp.float32)
 
     @pl.when(qi == nb - 1)
     def _():
-        dk_ref[0] = dk_scr[...].astype(dk_ref.dtype)
-        dv_ref[0] = dv_scr[...].astype(dv_ref.dtype)
+        g_ref[1] = dk_scr[...].astype(g_ref.dtype)
+        g_ref[2] = dv_scr[...].astype(g_ref.dtype)
 
 
 def mask_bias(slot_mask, length):
@@ -85,15 +86,13 @@
     row = pl.BlockSpec((1, TILE, hd), lambda i: (slot, i, 0))
     full = pl.BlockSpec((1, length, hd), lambda i: (slot, 0, 0))
     prow = pl.BlockSpec((1, length, TILE), lambda i: (slot, 0, i))
-    out_row = pl.BlockSpec((1, TILE, hd), lambda i: (0, i, 0))
-    out_full = pl.BlockSpec((1, length, hd), lambda i: (0, 0, 0))
-    shape = jax.ShapeDtypeStruct((1, length, hd), jnp.bfloat16)
+    stacked = pl.BlockSpec((3, length, hd), lambda i: (0, 0, 0))
     return pl.pallas_call(
         functools.partial(_bwd_kernel, nb=nb, scale=scale),
         grid=(nb,),
         in_specs=[row, full, full, prow, row, row],
-        out_specs=[out_row, out_full, out_full],
-        out_shape=(shape, shape, shape),
+        out_specs=stacked,
+        out_shape=jax.ShapeDtypeStruct((3, length, hd), jnp.bfloat16),
         scratch_shapes=[pltpu.VMEM((length, hd), jnp.float32), pltpu.VMEM((length, hd), jnp.float32)],
         compiler_params=pltpu.CompilerParams(dimension_semantics=("arbitrary",)),
     )(q, k, v, prob, o, do)
@@ -152,6 +151,8 @@
     def back_layout(stacked):
         return stacked.reshape(most_slots, seq_count, token_count, head_dim)
 
+    out_back = lax.all_to_all(back_layout(slot_out), "seq", split_axis=1, concat_axis=0, tiled=True)
+
     weight_full = jnp.transpose(weight_parts, (1, 2, 0, 3)).reshape(
         most_slots, head_dim, dp_count * out_weight.shape[2]
     )
@@ -166,29 +167,21 @@
         (weight_total * grad_scale).astype(jnp.bfloat16), "dp", scatter_dimension=0, tiled=True
     )
     weight_grad = jnp.transpose(weight_rows, (1, 2, 0)).astype(jnp.float32)
-    def to_owners(tensors):
-        one_stack = jnp.stack([t.reshape(seq_count, token_count, head_dim) for t in tensors])
+    def to_owners(one_stack):
         return lax.all_to_all(one_stack, "seq", split_axis=1, concat_axis=1, tiled=True)
 
     sent = []
     for slot_number in range(most_slots):
         slot_grads = attn_backward(
             slot_prob, slot_query, slot_key, slot_value, slot_out, grad_attn, score_scale, slot_number
-        )
-        if slot_number == 0:
-            sent.append(to_owners(tuple(slot_out) + tuple(slot_grads)))
-        else:
-            sent.append(to_owners(slot_grads))
-    base = most_slots
-
+        ).reshape(3, seq_count, token_count, head_dim)
+        sent.append(to_owners(slot_grads))
     def merged(pieces):
         return jnp.stack(pieces, axis=1).reshape(seq_count * most_slots, 1, token_count, head_dim)
 
-    all_back = [merged([sent[0][number] for number in range(most_slots)])]
+    all_back = [out_back]
     for which in range(3):
-        all_back.append(
-            merged([sent[0][base + which]] + [sent[number][which] for number in range(1, most_slots)])
-        )
+        all_back.append(merged([sent[number][which] for number in range(most_slots)]))
     attn_out = heads_to_tokens(all_back[0], head_slots, token_count, head_count, head_dim)
     query_grad = heads_to_tokens(all_back[1], head_slots, token_count, head_count, head_dim)
     key_grad = heads_to_tokens(all_back[2], head_slots, token_count, head_count, head_dim)

time: 341 us -> 337 us (0.988)
  waiting for transfers between devices: 131 us -> 125 us
    all_to_all x2, waiting for transfers between devices: 31.4 us -> 21.2 us  [to_owners(): lax.all_to_all(one_stack, 'seq', split_axis=1, concat_axis=1, tiled=True)]
    reshape x0 -> x3, local copies, waits for them, and re-layouts: none -> 6.62 us  [the longest x2 5.54 us: on_device(): slot_grads = attn_backward(slot_prob, slot_query, slot_key, slot_value, s...]
    all_to_all x0 -> x1, waiting for transfers between devices: none -> 4.46 us  [on_device(): lax.all_to_all(back_layout(slot_out), 'seq', split_axis=1, concat_axis=0,...]
    all_to_all x0 -> x1, starting transfers between devices: none -> 3.7 us  [on_device(): lax.all_to_all(back_layout(slot_out), 'seq', split_axis=1, concat_axis=0,...]
    unnamed x37 -> x33, local copies, waits for them, and re-layouts: 22.9 us -> 19.6 us
  transfers between devices with their start and end apart: 6 -> 7, of which waited for: 4 -> 6; matrix products, arithmetic and copies ran while one was open for 17% -> 16% of each run, Pallas kernels for 23% -> 23%
where the time goes in v13:
time: 337 us; the launch traced here: 335 us
  waiting for transfers between devices  125 us (37%)
  Pallas kernels  76.9 us (23%)
  local copies, waits for them, and re-layouts  55.9 us (17%)
  starting transfers between devices  27.9 us (8%)
  matrix products  22.2 us (7%)
  between operations  14.2 us (4%)
  other arithmetic  12.6 us (4%)
    all_to_all x1, waiting for transfers between devices, on_device(): lax.all_to_all(stacked, 'seq', split_axis=0, concat_axis=3, tiled=True)[0]  64.3 us
    pallas_call x2, Pallas kernels, attn_backward(): pl.pallas_call(functools.partial(_bwd_kernel, nb=nb, scale=scale), grid=(...  42.7 us
    pallas_call x1, Pallas kernels, attn_forward(): pl.pallas_call(functools.partial(_fwd_kernel, scale=scale), grid=(slots,...  34.3 us
    all_to_all x1, waiting for transfers between devices, on_device(): lax.all_to_all(weight_copies, 'dp', split_axis=0, concat_axis=0, tiled=True)  26.5 us
    all_to_all x2, waiting for transfers between devices, to_owners(): lax.all_to_all(one_stack, 'seq', split_axis=1, concat_axis=1, tiled=True)  21.2 us
    unnamed x33, local copies, waits for them, and re-layouts  19.6 us
    dot_general x1, matrix products, on_device(): jnp.einsum('td,shd->sth', dy_rows, weight_full, preferred_element_type=jn...  13.2 us
    all_to_all x1, starting transfers between devices, on_device(): lax.all_to_all(stacked, 'seq', split_axis=0, concat_axis=3, tiled=True)[0]  9.15 us
  transfers between devices with their start and end apart: 7, of which 6 were waited for; matrix products, arithmetic and copies ran while one was open for 16% of the time, Pallas kernels for 23%

profile of v13, /device:TPU:1, one launch (start us, length us, event | category | flops | bytes accessed | tf_op | source)
XLA Modules:
  0.0 334.9 jit_solution(1203918138198418457)
XLA Ops:
  7.9 2.8 broadcast_in_dim.38
  10.7 6.1 %all-to-all-start.2 = ((bf16[8,2,128,640]{3,2,1,0:T(8,128)(2,1)}), bf16[8,2,128,640]{3,2,1,0:T(8,128)(2,1)S(1)}, u32[]{:S(2)}, u32[]{:S(2)}) async-start(bf16[8,2,128,640]{3,2,1,0:T(8,128)(2,1)} %broadcast_in_dim.38), calls=%async_computation.2 | async-start | bytes 5242880 | tf_op jit(solution)/shard_map/all_to_all | solution.py:148
  21.4 2.2 copy.87
  23.5 1.6 copy.89
  27.0 2.2 copy.84
  32.2 2.0 pad_maximum_fusion
  34.1 26.5 %all-to-all-done.2 = bf16[8,2,128,640]{3,2,1,0:T(8,128)(2,1)S(1)} async-done(((bf16[8,2,128,640]{3,2,1,0:T(8,128)(2,1)}), bf16[8,2,128,640]{3,2,1,0:T(8,128)(2,1)S(1)}, u32[]{:S(2)}, u32[]{:S(2)}) %all-to-all-start.2) | async-done | bytes 2621472 | tf_op jit(solution)/shard_map/all_to_all | solution.py:148
  60.6 1.5 copy-done.2
  62.1 9.2 %all-to-all-start = ((bf16[16,3,2,128,128]{4,3,2,1,0:T(8,128)(2,1)}), bf16[16,3,2,128,128]{4,3,2,1,0:T(8,128)(2,1)S(1)}, u32[]{:S(2)}, u32[]{:S(2)}) async-start(bf16[16,3,2,128,128]{4,3,2,1,0:T(8,128)(2,1)} %pad_maximum_fusion), calls=%async_computation | async-start | bytes 6291456 | tf_op jit(solution)/shard_map/all_to_all | solution.py:142
  71.9 3.6 %copy.138 = bf16[8,2,16,8,640]{4,3,0,2,1:T(8,128)(2,1)} copy(bf16[8,2,16,8,640]{4,3,2,1,0:T(8,128)(2,1)} %bitcast.112) | data formatting | bytes 5242880 | tf_op jit(solution)/shard_map/reshape | solution.py:156
  75.6 64.3 %all-to-all-done = bf16[16,3,2,128,128]{4,3,2,1,0:T(8,128)(2,1)S(1)} async-done(((bf16[16,3,2,128,128]{4,3,2,1,0:T(8,128)(2,1)}), bf16[16,3,2,128,128]{4,3,2,1,0:T(8,128)(2,1)S(1)}, u32[]{:S(2)}, u32[]{:S(2)}) %all-to-all-start) | async-done | bytes 3145760 | tf_op jit(solution)/shard_map/all_to_all | solution.py:142
  144.2 34.3 %shard_map.110 = (bf16[2,2048,128]{2,1,0:T(8,128)(2,1)}, f32[2,2048,2048]{2,1,0:T(8,128)}) custom-call(bf16[2,2048,128]{2,1,0:T(8,128)(2,1)} %bitcast.102, bf16[2,2048,128]{2,1,0:T(8,128)(2,1)} %bitcast.105, bf16[2,2048,128]{2,1,0:T(8,128)(2,1)} %bitcast.108, f32[2,16,1,2048]{3,2,1,0:T(1,128)} %bitcast.132), custom_call_target="tpu_custom_call" | custom-call | tf_op jit(solution)/shard_map/pallas_call | solution.py:70
  178.5 7.9 %all-gather.2.cloned.1.call-done = bf16[1,2048,5120]{2,1,0:T(8,128)(2,1)} async-done(((bf16[1,128,5120]{2,1,0:T(8,128)(2,1)}), bf16[1,2048,5120]{2,1,0:T(8,128)(2,1)}) %all-gather.2.cloned.1.call-update) | async-done | bytes 20971536 | tf_op jit(solution)/shard_map/all_gather | solution.py:159
  186.4 13.2 %fusion.10.do_ref = bf16[2,2048,128]{2,1,0:T(8,128)(2,1)} fusion(bf16[2,128,5120]{2,1,0:T(8,128)(2,1)} %bitcast.123, bf16[1,2048,5120]{2,1,0:T(8,128)(2,1)} %all-gather.2.cloned.1.call-done), kind=kOutput, calls=%fused_computation.12 | convolution fusion | flops 5369233408 | bytes 24641536 | tf_op jit(solution)/shard_map/td,shd->sth/dot_general | solution.py:160
  200.7 7.5 %fusion.4 = f32[5120,2,128]{0,2,1:T(8,128)} fusion(bf16[2,2048,128]{2,1,0:T(8,128)(2,1)S(1)} %copy-done.1, bf16[1,2048,5120]{2,1,0:T(8,128)(2,1)S(1)} %copy-done), kind=kOutput, calls=%fused_computation.8 | convolution fusion | flops 5368709120 | bytes 27262976 | tf_op jit(solution)/shard_map/td,sth->dsh/dot_general | solution.py:164
  208.2 4.4 %multiply_convert_fusion = bf16[5120,2,128]{0,2,1:T(8,128)(2,1)} fusion(f32[5120,2,128]{0,2,1:T(8,128)} %fusion.4), kind=kLoop, calls=%fused_computation.9 | loop fusion | flops 2621440 | bytes 7864320 | tf_op jit(solution)/shard_map/convert_element_type | solution.py:167
  212.6 4.4 %copy.130 = bf16[5120,256]{1,0:T(8,128)(2,1)} copy(bf16[5120,256]{0,1:T(8,128)(2,1)} %bitcast.113) | data formatting | bytes 5242880
  218.1 3.7 %all-to-all-start.1 = ((bf16[2,16,128,128]{3,2,0,1:T(8,128)(2,1)}), bf16[2,16,128,128]{3,2,0,1:T(8,128)(2,1)S(1)}, u32[]{:S(2)}, u32[]{:S(2)}) async-start(bf16[2,16,128,128]{3,2,0,1:T(8,128)(2,1)} %copy.100), calls=%async_computation.1 | async-start | bytes 2097152 | tf_op jit(solution)/shard_map/all_to_all | solution.py:154
  221.8 21.4 %shard_map.112 = bf16[3,2048,128]{2,1,0:T(8,128)(2,1)} custom-call(bf16[2,2048,128]{2,1,0:T(8,128)(2,1)} %bitcast.103, bf16[2,2048,128]{2,1,0:T(8,128)(2,1)} %bitcast.106, bf16[2,2048,128]{2,1,0:T(8,128)(2,1)} %bitcast.109, f32[2,2048,2048]{2,1,0:T(8,128)} %get-tuple-element.13.p_ref, bf16[2,2048,128]{2,1,0:T(8,128)(2,1)} %get-tuple-element.11.o_ref, ...), custom_call_target="tpu_custom_call" | custom-call | tf_op jit(solution)/shard_map/pallas_call | solution.py:90
  243.2 2.8 copy.107
  246.0 4.5 %all-to-all-done.1 = bf16[2,16,128,128]{3,2,0,1:T(8,128)(2,1)S(1)} async-done(((bf16[2,16,128,128]{3,2,0,1:T(8,128)(2,1)}), bf16[2,16,128,128]{3,2,0,1:T(8,128)(2,1)S(1)}, u32[]{:S(2)}, u32[]{:S(2)}) %all-to-all-start.1) | async-done | bytes 1048608 | tf_op jit(solution)/shard_map/all_to_all | solution.py:154
  251.4 4.3 %all-to-all-start.4 = ((bf16[3,16,128,128]{3,2,0,1:T(8,128)(2,1)}), bf16[3,16,128,128]{3,2,0,1:T(8,128)(2,1)S(1)}, u32[]{:S(2)}, u32[]{:S(2)}) async-start(bf16[3,16,128,128]{3,2,0,1:T(8,128)(2,1)} %copy.107), calls=%async_computation.4 | async-start | bytes 3145728 | tf_op jit(solution)/shard_map/all_to_all | solution.py:171
  255.8 21.2 %shard_map.111 = bf16[3,2048,128]{2,1,0:T(8,128)(2,1)} custom-call(bf16[2,2048,128]{2,1,0:T(8,128)(2,1)} %bitcast.104, bf16[2,2048,128]{2,1,0:T(8,128)(2,1)} %bitcast.107, bf16[2,2048,128]{2,1,0:T(8,128)(2,1)} %bitcast.110, f32[2,2048,2048]{2,1,0:T(8,128)} %get-tuple-element.13.p_ref, bf16[2,2048,128]{2,1,0:T(8,128)(2,1)} %get-tuple-element.11.o_ref, ...), custom_call_target="tpu_custom_call" | custom-call | tf_op jit(solution)/shard_map/pallas_call | solution.py:90
  277.0 2.8 copy.105
  279.7 2.9 all-to-all-done.4
  282.7 4.4 %all-to-all-start.3 = ((bf16[3,16,128,128]{3,2,0,1:T(8,128)(2,1)}), bf16[3,16,128,128]{3,2,0,1:T(8,128)(2,1)S(1)}, u32[]{:S(2)}, u32[]{:S(2)}) async-start(bf16[3,16,128,128]{3,2,0,1:T(8,128)(2,1)} %copy.105), calls=%async_computation.3 | async-start | bytes 3145728 | tf_op jit(solution)/shard_map/all_to_all | solution.py:171
  287.7 2.7 gather_fusion
  291.6 18.3 %all-to-all-done.3 = bf16[3,16,128,128]{3,2,0,1:T(8,128)(2,1)S(1)} async-done(((bf16[3,16,128,128]{3,2,0,1:T(8,128)(2,1)}), bf16[3,16,128,128]{3,2,0,1:T(8,128)(2,1)S(1)}, u32[]{:S(2)}, u32[]{:S(2)}) %all-to-all-start.3) | async-done | bytes 1572896 | tf_op jit(solution)/shard_map/all_to_all | solution.py:171
  311.7 1.8 pad_maximum_fusion.1
  313.5 1.5 gather_fusion.1
  315.0 1.5 gather_fusion.2
  316.5 2.6 select_bitcast_fusion
  (69 shorter events, 30.7 us)
Async XLA Ops:
  7.2 179.2 %all-gather.2.cloned.1.call-start = ((), (), s32[]{:S(2)}) async-start(), calls=%async_computation.6 | async-start | bytes 22282240 | tf_op jit(solution)/shard_map/all_gather | solution.py:159
  10.7 6.1 %copy-start.9 = (bf16[1,128,2560]{2,1,0:T(8,128)(2,1)S(1)}, bf16[1,128,2560]{2,1,0:T(8,128)(2,1)}, u32[]{:S(2)}) copy-start(bf16[1,128,2560]{2,1,0:T(8,128)(2,1)} %param.11) | copy-start | bytes 1966084
  10.7 49.9 %all-to-all-start.2 = ((bf16[8,2,128,640]{3,2,1,0:T(8,128)(2,1)}), bf16[8,2,128,640]{3,2,1,0:T(8,128)(2,1)S(1)}, u32[]{:S(2)}, u32[]{:S(2)}) async-start(bf16[8,2,128,640]{3,2,1,0:T(8,128)(2,1)} %broadcast_in_dim.38), calls=%async_computation.2 | async-start | bytes 5242880 | tf_op jit(solution)/shard_map/all_to_all | solution.py:148
  16.8 2.6 copy-start.11
  30.6 1.2 copy-start.3
  30.6 1.5 copy-start.4
  34.1 37.5 %copy-start.10 = (s32[20,16,16]{0,2,1:T(8,128)S(1)}, s32[20,16,16]{0,2,1:T(8,128)}, u32[]{:S(2)}) copy-start(s32[20,16,16]{0,2,1:T(8,128)} %param.14) | copy-start | bytes 61444
  60.6 1.5 copy-start.2
  62.1 77.7 %all-to-all-start = ((bf16[16,3,2,128,128]{4,3,2,1,0:T(8,128)(2,1)}), bf16[16,3,2,128,128]{4,3,2,1,0:T(8,128)(2,1)S(1)}, u32[]{:S(2)}, u32[]{:S(2)}) async-start(bf16[16,3,2,128,128]{4,3,2,1,0:T(8,128)(2,1)} %pad_maximum_fusion), calls=%async_computation | async-start | bytes 6291456 | tf_op jit(solution)/shard_map/all_to_all | solution.py:142
  71.3 254.7 %reduce-scatter.4.cloned.1.call-start = ((), (), s32[]{:S(2)}) async-start(), calls=%async_computation.7 | async-start | bytes 2949120
  186.4 14.1 %copy-start = (bf16[1,2048,5120]{2,1,0:T(8,128)(2,1)S(1)}, bf16[1,2048,5120]{2,1,0:T(8,128)(2,1)}, u32[]{:S(2)}) copy-start(bf16[1,2048,5120]{2,1,0:T(8,128)(2,1)} %all-gather.2.cloned.1.call-done) | copy-start | bytes 62914564
  186.4 14.3 %copy-start.1 = (bf16[2,2048,128]{2,1,0:T(8,128)(2,1)S(1)}, bf16[2,2048,128]{2,1,0:T(8,128)(2,1)}, u32[]{:S(2)}) copy-start(bf16[2,2048,128]{2,1,0:T(8,128)(2,1)} %get-tuple-element.11.o_ref) | copy-start | bytes 3145732
  218.1 32.4 %all-to-all-start.1 = ((bf16[2,16,128,128]{3,2,0,1:T(8,128)(2,1)}), bf16[2,16,128,128]{3,2,0,1:T(8,128)(2,1)S(1)}, u32[]{:S(2)}, u32[]{:S(2)}) async-start(bf16[2,16,128,128]{3,2,0,1:T(8,128)(2,1)} %copy.100), calls=%async_computation.1 | async-start | bytes 2097152 | tf_op jit(solution)/shard_map/all_to_all | solution.py:154
  250.4 1.0 copy-start.5
  251.4 31.2 %all-to-all-start.4 = ((bf16[3,16,128,128]{3,2,0,1:T(8,128)(2,1)}), bf16[3,16,128,128]{3,2,0,1:T(8,128)(2,1)S(1)}, u32[]{:S(2)}, u32[]{:S(2)}) async-start(bf16[3,16,128,128]{3,2,0,1:T(8,128)(2,1)} %copy.107), calls=%async_computation.4 | async-start | bytes 3145728 | tf_op jit(solution)/shard_map/all_to_all | solution.py:171
  282.7 27.1 %all-to-all-start.3 = ((bf16[3,16,128,128]{3,2,0,1:T(8,128)(2,1)}), bf16[3,16,128,128]{3,2,0,1:T(8,128)(2,1)S(1)}, u32[]{:S(2)}, u32[]{:S(2)}) async-start(bf16[3,16,128,128]{3,2,0,1:T(8,128)(2,1)} %copy.105), calls=%async_computation.3 | async-start | bytes 3145728 | tf_op jit(solution)/shard_map/all_to_all | solution.py:171
  291.6 19.3 %copy-start.8 = (bf16[16,1,128,128]{3,2,1,0:T(8,128)(2,1)S(1)}, bf16[16,1,128,128]{3,2,1,0:T(8,128)(2,1)}, u32[]{:S(2)}) copy-start(bf16[16,1,128,128]{3,2,1,0:T(8,128)(2,1)} %get-tuple-element.37) | copy-start | bytes 1572868
  311.7 4.8 %copy-start.6 = (bf16[20,128,128]{2,1,0:T(8,128)(2,1)S(1)}, bf16[20,128,128]{2,1,0:T(8,128)(2,1)}, u32[]{:S(2)}) copy-start(bf16[20,128,128]{2,1,0:T(8,128)(2,1)} %gather_fusion) | copy-start | bytes 1966084
  319.1 2.6 copy-start.7
Sparse Core Ops, SparseCore 0:
  10.4 175.9 all-gather.1
  217.1 47.7 reduce-scatter.3

commit v14 on v13

--- a/solution.py
+++ b/solution.py
@@ -44,15 +44,14 @@
     dv_scr[...] += jnp.dot(low_t, do, preferred_element_type=jnp.float32)
     dp_t = lax.dot_general(v, do, NT, preferred_element_type=jnp.float32)
     ds_t = (prob_t * (dp_t - delta_row) * scale).astype(jnp.bfloat16)
-    row_first = pl.multiple_of(qi * TILE, TILE)
     dq = lax.dot_general(ds_t, k, TN, preferred_element_type=jnp.float32)
-    g_ref[0, pl.ds(row_first, TILE), :] = dq.astype(g_ref.dtype)
+    g_ref[qi, 0] = dq.astype(g_ref.dtype)
     dk_scr[...] += jnp.dot(ds_t, q, preferred_element_type=jnp.float32)
 
     @pl.when(qi == nb - 1)
     def _():
-        g_ref[1] = dk_scr[...].astype(g_ref.dtype)
-        g_ref[2] = dv_scr[...].astype(g_ref.dtype)
+        g_ref[:, 1] = dk_scr[...].reshape(nb, TILE, dk_scr.shape[1]).astype(g_ref.dtype)
+        g_ref[:, 2] = dv_scr[...].reshape(nb, TILE, dv_scr.shape[1]).astype(g_ref.dtype)
 
 
 def mask_bias(slot_mask, length):
@@ -86,13 +85,13 @@
     row = pl.BlockSpec((1, TILE, hd), lambda i: (slot, i, 0))
     full = pl.BlockSpec((1, length, hd), lambda i: (slot, 0, 0))
     prow = pl.BlockSpec((1, length, TILE), lambda i: (slot, 0, i))
-    stacked = pl.BlockSpec((3, length, hd), lambda i: (0, 0, 0))
+    stacked = pl.BlockSpec((nb, 3, TILE, hd), lambda i: (0, 0, 0, 0))
     return pl.pallas_call(
         functools.partial(_bwd_kernel, nb=nb, scale=scale),
         grid=(nb,),
         in_specs=[row, full, full, prow, row, row],
         out_specs=stacked,
-        out_shape=jax.ShapeDtypeStruct((3, length, hd), jnp.bfloat16),
+        out_shape=jax.ShapeDtypeStruct((nb, 3, TILE, hd), jnp.bfloat16),
         scratch_shapes=[pltpu.VMEM((length, hd), jnp.float32), pltpu.VMEM((length, hd), jnp.float32)],
         compiler_params=pltpu.CompilerParams(dimension_semantics=("arbitrary",)),
     )(q, k, v, prob, o, do)
@@ -174,7 +173,7 @@
     for slot_number in range(most_slots):
         slot_grads = attn_backward(
             slot_prob, slot_query, slot_key, slot_value, slot_out, grad_attn, score_scale, slot_number
-        ).reshape(3, seq_count, token_count, head_dim)
+        ).transpose(1, 0, 2, 3)
         sent.append(to_owners(slot_grads))
     def merged(pieces):
         return jnp.stack(pieces, axis=1).reshape(seq_count * most_slots, 1, token_count, head_dim)

time: 337 us -> 337 us (level)
  waiting for transfers between devices: 125 us -> 130 us
  local copies, waits for them, and re-layouts: 55.9 us -> 51.3 us
    reshape x2 -> x0, local copies, waits for them, and re-layouts: 5.54 us -> none  [on_device(): slot_grads = attn_backward(slot_prob, slot_query, slot_key, slot_value, s...]
    unnamed x33 -> x37, local copies, waits for them, and re-layouts: 19.6 us -> 20.1 us
  transfers between devices with their start and end apart: 7 -> 7, of which waited for: 6 -> 6; matrix products, arithmetic and copies ran while one was open for 16% -> 15% of each run, Pallas kernels for 23% -> 23%
where the time goes in v14:
time: 337 us; the launch traced here: 335 us
  waiting for transfers between devices  130 us (39%)
  Pallas kernels  76.9 us (23%)
  local copies, waits for them, and re-layouts  51.3 us (15%)
  starting transfers between devices  28 us (8%)
  matrix products  22.2 us (7%)
  between operations  14.3 us (4%)
  other arithmetic  11.9 us (4%)
    all_to_all x1, waiting for transfers between devices, on_device(): lax.all_to_all(stacked, 'seq', split_axis=0, concat_axis=3, tiled=True)[0]  64.3 us
    pallas_call x2, Pallas kernels, attn_backward(): pl.pallas_call(functools.partial(_bwd_kernel, nb=nb, scale=scale), grid=(...  42.7 us
    pallas_call x1, Pallas kernels, attn_forward(): pl.pallas_call(functools.partial(_fwd_kernel, scale=scale), grid=(slots,...  34.2 us
    all_to_all x1, waiting for transfers between devices, on_device(): lax.all_to_all(weight_copies, 'dp', split_axis=0, concat_axis=0, tiled=True)  26.5 us
    all_to_all x2, waiting for transfers between devices, to_owners(): lax.all_to_all(one_stack, 'seq', split_axis=1, concat_axis=1, tiled=True)  23.9 us
    unnamed x37, local copies, waits for them, and re-layouts  20.1 us
    dot_general x1, matrix products, on_device(): jnp.einsum('td,shd->sth', dy_rows, weight_full, preferred_element_type=jn...  13.2 us
    all_to_all x1, starting transfers between devices, on_device(): lax.all_to_all(stacked, 'seq', split_axis=0, concat_axis=3, tiled=True)[0]  9.15 us
  transfers between devices with their start and end apart: 7, of which 6 were waited for; matrix products, arithmetic and copies ran while one was open for 15% of the time, Pallas kernels for 23%

profile of v14, /device:TPU:1, one launch (start us, length us, event | category | flops | bytes accessed | tf_op | source)
XLA Modules:
  0.0 335.0 jit_solution(16377931727903732623)
XLA Ops:
  7.9 2.8 broadcast_in_dim.38
  10.7 6.1 %all-to-all-start.2 = ((bf16[8,2,128,640]{3,2,1,0:T(8,128)(2,1)}), bf16[8,2,128,640]{3,2,1,0:T(8,128)(2,1)S(1)}, u32[]{:S(2)}, u32[]{:S(2)}) async-start(bf16[8,2,128,640]{3,2,1,0:T(8,128)(2,1)} %broadcast_in_dim.38), calls=%async_computation.2 | async-start | bytes 5242880 | tf_op jit(solution)/shard_map/all_to_all | solution.py:147
  17.9 1.5 copy.96
  21.4 2.2 copy.91
  23.5 1.6 copy.93
  27.0 2.2 copy.88
  29.1 1.5 copy.90
  32.2 2.0 pad_maximum_fusion
  34.1 26.5 %all-to-all-done.2 = bf16[8,2,128,640]{3,2,1,0:T(8,128)(2,1)S(1)} async-done(((bf16[8,2,128,640]{3,2,1,0:T(8,128)(2,1)}), bf16[8,2,128,640]{3,2,1,0:T(8,128)(2,1)S(1)}, u32[]{:S(2)}, u32[]{:S(2)}) %all-to-all-start.2) | async-done | bytes 2621472 | tf_op jit(solution)/shard_map/all_to_all | solution.py:147
  60.6 1.5 copy-done.2
  62.1 9.2 %all-to-all-start = ((bf16[16,3,2,128,128]{4,3,2,1,0:T(8,128)(2,1)}), bf16[16,3,2,128,128]{4,3,2,1,0:T(8,128)(2,1)S(1)}, u32[]{:S(2)}, u32[]{:S(2)}) async-start(bf16[16,3,2,128,128]{4,3,2,1,0:T(8,128)(2,1)} %pad_maximum_fusion), calls=%async_computation | async-start | bytes 6291456 | tf_op jit(solution)/shard_map/all_to_all | solution.py:141
  71.9 3.6 %copy.137 = bf16[8,2,16,8,640]{4,3,0,2,1:T(8,128)(2,1)} copy(bf16[8,2,16,8,640]{4,3,2,1,0:T(8,128)(2,1)} %bitcast.106) | data formatting | bytes 5242880 | tf_op jit(solution)/shard_map/reshape | solution.py:155
  75.6 64.3 %all-to-all-done = bf16[16,3,2,128,128]{4,3,2,1,0:T(8,128)(2,1)S(1)} async-done(((bf16[16,3,2,128,128]{4,3,2,1,0:T(8,128)(2,1)}), bf16[16,3,2,128,128]{4,3,2,1,0:T(8,128)(2,1)S(1)}, u32[]{:S(2)}, u32[]{:S(2)}) %all-to-all-start) | async-done | bytes 3145760 | tf_op jit(solution)/shard_map/all_to_all | solution.py:141
  144.2 34.2 %shard_map.110 = (bf16[2,2048,128]{2,1,0:T(8,128)(2,1)}, f32[2,2048,2048]{2,1,0:T(8,128)}) custom-call(bf16[2,2048,128]{2,1,0:T(8,128)(2,1)} %bitcast.96, bf16[2,2048,128]{2,1,0:T(8,128)(2,1)} %bitcast.99, bf16[2,2048,128]{2,1,0:T(8,128)(2,1)} %bitcast.102, f32[2,16,1,2048]{3,2,1,0:T(1,128)} %bitcast.126), custom_call_target="tpu_custom_call" | custom-call | tf_op jit(solution)/shard_map/pallas_call | solution.py:69
  178.4 8.0 %all-gather.2.cloned.1.call-done = bf16[1,2048,5120]{2,1,0:T(8,128)(2,1)} async-done(((bf16[1,128,5120]{2,1,0:T(8,128)(2,1)}), bf16[1,2048,5120]{2,1,0:T(8,128)(2,1)}) %all-gather.2.cloned.1.call-update) | async-done | bytes 20971536 | tf_op jit(solution)/shard_map/all_gather | solution.py:158
  186.4 13.2 %fusion.10.do_ref = bf16[2,2048,128]{2,1,0:T(8,128)(2,1)} fusion(bf16[2,128,5120]{2,1,0:T(8,128)(2,1)} %bitcast.117, bf16[1,2048,5120]{2,1,0:T(8,128)(2,1)} %all-gather.2.cloned.1.call-done), kind=kOutput, calls=%fused_computation.12 | convolution fusion | flops 5369233408 | bytes 24641536 | tf_op jit(solution)/shard_map/td,shd->sth/dot_general | solution.py:159
  200.7 7.5 %fusion.4 = f32[5120,2,128]{0,2,1:T(8,128)} fusion(bf16[2,2048,128]{2,1,0:T(8,128)(2,1)S(1)} %copy-done.1, bf16[1,2048,5120]{2,1,0:T(8,128)(2,1)S(1)} %copy-done), kind=kOutput, calls=%fused_computation.8 | convolution fusion | flops 5368709120 | bytes 27262976 | tf_op jit(solution)/shard_map/td,sth->dsh/dot_general | solution.py:163
  208.2 4.4 %multiply_convert_fusion = bf16[5120,2,128]{0,2,1:T(8,128)(2,1)} fusion(f32[5120,2,128]{0,2,1:T(8,128)} %fusion.4), kind=kLoop, calls=%fused_computation.9 | loop fusion | flops 2621440 | bytes 7864320 | tf_op jit(solution)/shard_map/convert_element_type | solution.py:166
  212.5 4.4 %copy.132 = bf16[5120,256]{1,0:T(8,128)(2,1)} copy(bf16[5120,256]{0,1:T(8,128)(2,1)} %bitcast.107) | data formatting | bytes 5242880
  218.0 3.7 %all-to-all-start.1 = ((bf16[2,16,128,128]{3,2,0,1:T(8,128)(2,1)}), bf16[2,16,128,128]{3,2,0,1:T(8,128)(2,1)S(1)}, u32[]{:S(2)}, u32[]{:S(2)}) async-start(bf16[2,16,128,128]{3,2,0,1:T(8,128)(2,1)} %copy.104), calls=%async_computation.1 | async-start | bytes 2097152 | tf_op jit(solution)/shard_map/all_to_all | solution.py:153
  221.7 21.5 %shard_map.112 = bf16[16,3,128,128]{3,2,1,0:T(8,128)(2,1)} custom-call(bf16[2,2048,128]{2,1,0:T(8,128)(2,1)} %bitcast.97, bf16[2,2048,128]{2,1,0:T(8,128)(2,1)} %bitcast.100, bf16[2,2048,128]{2,1,0:T(8,128)(2,1)} %bitcast.103, f32[2,2048,2048]{2,1,0:T(8,128)} %get-tuple-element.13.p_ref, bf16[2,2048,128]{2,1,0:T(8,128)(2,1)} %get-tuple-element.11.o_ref, ...), custom_call_target="tpu_custom_call" | custom-call | tf_op jit(solution)/shard_map/pallas_call | solution.py:89
  243.1 7.1 %all-to-all-done.1 = bf16[2,16,128,128]{3,2,0,1:T(8,128)(2,1)S(1)} async-done(((bf16[2,16,128,128]{3,2,0,1:T(8,128)(2,1)}), bf16[2,16,128,128]{3,2,0,1:T(8,128)(2,1)S(1)}, u32[]{:S(2)}, u32[]{:S(2)}) %all-to-all-start.1) | async-done | bytes 1048608 | tf_op jit(solution)/shard_map/all_to_all | solution.py:153
  251.3 4.4 %all-to-all-start.4 = ((bf16[3,16,128,128]{3,2,0,1:T(8,128)(2,1)}), bf16[3,16,128,128]{3,2,0,1:T(8,128)(2,1)S(1)}, u32[]{:S(2)}, u32[]{:S(2)}) async-start(bf16[3,16,128,128]{3,2,0,1:T(8,128)(2,1)} %bitcast.109), calls=%async_computation.4 | async-start | bytes 3145728 | tf_op jit(solution)/shard_map/all_to_all | solution.py:170
  255.7 21.2 %shard_map.111 = bf16[16,3,128,128]{3,2,1,0:T(8,128)(2,1)} custom-call(bf16[2,2048,128]{2,1,0:T(8,128)(2,1)} %bitcast.98, bf16[2,2048,128]{2,1,0:T(8,128)(2,1)} %bitcast.101, bf16[2,2048,128]{2,1,0:T(8,128)(2,1)} %bitcast.104, f32[2,2048,2048]{2,1,0:T(8,128)} %get-tuple-element.13.p_ref, bf16[2,2048,128]{2,1,0:T(8,128)(2,1)} %get-tuple-element.11.o_ref, ...), custom_call_target="tpu_custom_call" | custom-call | tf_op jit(solution)/shard_map/pallas_call | solution.py:89
  276.9 5.7 %all-to-all-done.4 = bf16[3,16,128,128]{3,2,0,1:T(8,128)(2,1)S(1)} async-done(((bf16[3,16,128,128]{3,2,0,1:T(8,128)(2,1)}), bf16[3,16,128,128]{3,2,0,1:T(8,128)(2,1)S(1)}, u32[]{:S(2)}, u32[]{:S(2)}) %all-to-all-start.4) | async-done | bytes 1572896 | tf_op jit(solution)/shard_map/all_to_all | solution.py:170
  282.6 4.5 %all-to-all-start.3 = ((bf16[3,16,128,128]{3,2,0,1:T(8,128)(2,1)}), bf16[3,16,128,128]{3,2,0,1:T(8,128)(2,1)S(1)}, u32[]{:S(2)}, u32[]{:S(2)}) async-start(bf16[3,16,128,128]{3,2,0,1:T(8,128)(2,1)} %bitcast.108), calls=%async_computation.3 | async-start | bytes 3145728 | tf_op jit(solution)/shard_map/all_to_all | solution.py:170
  287.6 2.7 gather_fusion
  291.5 18.3 %all-to-all-done.3 = bf16[3,16,128,128]{3,2,0,1:T(8,128)(2,1)S(1)} async-done(((bf16[3,16,128,128]{3,2,0,1:T(8,128)(2,1)}), bf16[3,16,128,128]{3,2,0,1:T(8,128)(2,1)S(1)}, u32[]{:S(2)}, u32[]{:S(2)}) %all-to-all-start.3) | async-done | bytes 1572896 | tf_op jit(solution)/shard_map/all_to_all | solution.py:170
  313.5 1.5 gather_fusion.1
  315.8 2.4 select_bitcast_fusion
  318.3 1.4 copy.105
  320.8 1.4 copy.111
  (74 shorter events, 28.6 us)
Async XLA Ops:
  7.2 179.2 %all-gather.2.cloned.1.call-start = ((), (), s32[]{:S(2)}) async-start(), calls=%async_computation.6 | async-start | bytes 22282240 | tf_op jit(solution)/shard_map/all_gather | solution.py:158
  10.7 6.1 %copy-start.11 = (bf16[1,128,2560]{2,1,0:T(8,128)(2,1)S(1)}, bf16[1,128,2560]{2,1,0:T(8,128)(2,1)}, u32[]{:S(2)}) copy-start(bf16[1,128,2560]{2,1,0:T(8,128)(2,1)} %param.11) | copy-start | bytes 1966084
  10.7 8.7 %copy-start.13 = (s32[20]{0:T(128)S(1)}, s32[20]{0:T(128)}, u32[]{:S(2)}) copy-start(s32[20]{0:T(128)} %param.15) | copy-start | bytes 244
  10.7 49.9 %all-to-all-start.2 = ((bf16[8,2,128,640]{3,2,1,0:T(8,128)(2,1)}), bf16[8,2,128,640]{3,2,1,0:T(8,128)(2,1)S(1)}, u32[]{:S(2)}, u32[]{:S(2)}) async-start(bf16[8,2,128,640]{3,2,1,0:T(8,128)(2,1)} %broadcast_in_dim.38), calls=%async_computation.2 | async-start | bytes 5242880 | tf_op jit(solution)/shard_map/all_to_all | solution.py:147
  30.6 1.2 copy-start.3
  30.6 1.5 copy-start.4
  34.1 37.5 %copy-start.12 = (s32[20,16,16]{0,2,1:T(8,128)S(1)}, s32[20,16,16]{0,2,1:T(8,128)}, u32[]{:S(2)}) copy-start(s32[20,16,16]{0,2,1:T(8,128)} %param.14) | copy-start | bytes 61444
  60.6 1.5 copy-start.2
  62.1 77.7 %all-to-all-start = ((bf16[16,3,2,128,128]{4,3,2,1,0:T(8,128)(2,1)}), bf16[16,3,2,128,128]{4,3,2,1,0:T(8,128)(2,1)S(1)}, u32[]{:S(2)}, u32[]{:S(2)}) async-start(bf16[16,3,2,128,128]{4,3,2,1,0:T(8,128)(2,1)} %pad_maximum_fusion), calls=%async_computation | async-start | bytes 6291456 | tf_op jit(solution)/shard_map/all_to_all | solution.py:141
  71.3 254.9 %reduce-scatter.4.cloned.1.call-start = ((), (), s32[]{:S(2)}) async-start(), calls=%async_computation.7 | async-start | bytes 2949120
  186.4 14.1 %copy-start = (bf16[1,2048,5120]{2,1,0:T(8,128)(2,1)S(1)}, bf16[1,2048,5120]{2,1,0:T(8,128)(2,1)}, u32[]{:S(2)}) copy-start(bf16[1,2048,5120]{2,1,0:T(8,128)(2,1)} %all-gather.2.cloned.1.call-done) | copy-start | bytes 62914564
  186.4 14.3 %copy-start.1 = (bf16[2,2048,128]{2,1,0:T(8,128)(2,1)S(1)}, bf16[2,2048,128]{2,1,0:T(8,128)(2,1)}, u32[]{:S(2)}) copy-start(bf16[2,2048,128]{2,1,0:T(8,128)(2,1)} %get-tuple-element.11.o_ref) | copy-start | bytes 3145732
  218.0 32.3 %all-to-all-start.1 = ((bf16[2,16,128,128]{3,2,0,1:T(8,128)(2,1)}), bf16[2,16,128,128]{3,2,0,1:T(8,128)(2,1)S(1)}, u32[]{:S(2)}, u32[]{:S(2)}) async-start(bf16[2,16,128,128]{3,2,0,1:T(8,128)(2,1)} %copy.104), calls=%async_computation.1 | async-start | bytes 2097152 | tf_op jit(solution)/shard_map/all_to_all | solution.py:153
  250.3 1.0 copy-start.5
  251.3 31.3 %all-to-all-start.4 = ((bf16[3,16,128,128]{3,2,0,1:T(8,128)(2,1)}), bf16[3,16,128,128]{3,2,0,1:T(8,128)(2,1)S(1)}, u32[]{:S(2)}, u32[]{:S(2)}) async-start(bf16[3,16,128,128]{3,2,0,1:T(8,128)(2,1)} %bitcast.109), calls=%async_computation.4 | async-start | bytes 3145728 | tf_op jit(solution)/shard_map/all_to_all | solution.py:170
  282.6 27.2 %all-to-all-start.3 = ((bf16[3,16,128,128]{3,2,0,1:T(8,128)(2,1)}), bf16[3,16,128,128]{3,2,0,1:T(8,128)(2,1)S(1)}, u32[]{:S(2)}, u32[]{:S(2)}) async-start(bf16[3,16,128,128]{3,2,0,1:T(8,128)(2,1)} %bitcast.108), calls=%async_computation.3 | async-start | bytes 3145728 | tf_op jit(solution)/shard_map/all_to_all | solution.py:170
  291.5 19.4 %copy-start.7 = (bf16[16,1,128,128]{3,2,0,1:T(8,128)(2,1)S(1)}, bf16[16,1,128,128]{3,2,0,1:T(8,128)(2,1)}, u32[]{:S(2)}) copy-start(bf16[16,1,128,128]{3,2,0,1:T(8,128)(2,1)} %get-tuple-element.37) | copy-start | bytes 1572868
  310.9 1.0 copy-start.8
  310.9 1.2 copy-start.9
  310.9 1.4 copy-start.10
  313.5 2.4 copy-start.6
Sparse Core Ops, SparseCore 0:
  10.4 175.9 all-gather.1
  217.0 47.9 reduce-scatter.3
